TPU v7x, 512 devices: a whole 4x4x16 slice. The times are simulated.
512 devices in a mesh: graph: 32 (over z, core), irreps: 16 (over y, x).
Axes of the slice: x: 4, y: 4, z: 16, core: 2. Of those that a mesh axis runs over, the one named last changes fastest.
Arguments:
- node_feats: bfloat16 [49, 128, 2048], P(None, 'irreps', 'graph'), may hold values from -8 to 8
- norm_gain: float32 [7, 128], P(None, 'irreps'), may hold values from 0.1 to 1.9
- species: int32 [2048], P('graph'), may hold values from 0 to 89
- send_list: int32 [8192], P('graph'), may hold values from 0 to 63
- edge_source: int32 [32768], P('graph'), may hold values from 0 to 319, as said below
- edge_target: int32 [32768], P('graph'), may hold values from 0 to 63
- edge_count: int32 [32], P('graph'), may hold values from 512 to 1024, as said below
- edge_length: float32 [32768], P('graph'), may hold values from 0.8 to 6
- wigner: bfloat16 [235, 32768], P(None, 'graph'), may hold values from -2.5 to 2.5
- radial_in: bfloat16 [512, 128], replicated, may hold values from -0.25 to 0.25
- species_table: bfloat16 [90, 128], replicated, may hold values from -6 to 6
- radial_out: bfloat16 [128, 896], replicated, may hold values from -0.5 to 0.5
- order_zero: bfloat16 [896, 896], replicated, may hold values from -0.1875 to 0.1875
- order_one: bfloat16 [2, 768, 768], replicated, may hold values from -0.15625 to 0.15625
- order_two: bfloat16 [2, 640, 640], replicated, may hold values from -0.15625 to 0.15625
- project_weight: bfloat16 [7, 128, 128], P(None, None, 'irreps'), may hold values from -0.5 to 0.5
Outputs:
- new_feats: bfloat16 [49, 128, 2048], P(None, 'irreps', 'graph')
Inputs may be any that keep to these rules, and one draw needn't show every extreme that they name: `edge_source`: an index into the table of its edge's domain. A domain reads no slot of its own send block; from each other domain it reads only the first few slots (between 1 and 8 of them), and it reads slot 7 of some domain. `edge_count`: edge slots at or past a domain's count are padding; some domain has all 1024 live.
All inputs are finite; a program needn't handle non-finite values.
Results may differ from a plain program's by a relative error of at most 0.006.
Values may be sent and summed in bfloat16 or wider, within the bound.
No kernel may reach another device: no remote copies, remote signals or barrier semaphores. Data moves between devices by JAX's collectives and lax.ppermute only.
A program may use at most 128 MiB of HBM per device.

v0:
```python
import jax
import jax.numpy as jnp
import numpy as np
from jax import lax
from jax.sharding import PartitionSpec as P

CHANNELS = 128
MAX_DEGREE = 6
MAX_ORDER = 2
ROTATED = 29


EPSILON = 1e-06
CUTOFF = 6.0


def order_index(degree, harmonic):
    if harmonic == 0:
        return degree
    first_row = MAX_DEGREE + 1
    for level in range(1, abs(harmonic)):
        first_row = first_row + 2 * (MAX_DEGREE + 1 - level)
    if harmonic < 0:
        first_row = first_row + MAX_DEGREE + 1 - abs(harmonic)
    return first_row + degree - abs(harmonic)


def wigner_start(degree):
    running = 0
    for level in range(degree):
        running = running + (2 * min(level, MAX_ORDER) + 1) * (2 * level + 1)
    return running


def left_dot(weight, values):
    return lax.dot_general(
        weight, values, (((0,), (0,)), ((), ())), preferred_element_type=jnp.float32
    )


def degree_sums(squares):
    return jnp.stack(
        [
            jnp.sum(squares[degree * degree : (degree + 1) ** 2], axis=0)
            for degree in range(MAX_DEGREE + 1)
        ]
    )


def normalize(node_feats, norm_gain, totals):
    levels = MAX_DEGREE + 1
    degree_of = np.repeat(np.arange(levels), 2 * np.arange(levels) + 1)
    entry_counts = (2 * np.arange(levels) + 1) * CHANNELS
    inverse = 1.0 / jnp.sqrt(totals / jnp.asarray(entry_counts, jnp.float32)[:, None] + EPSILON)
    gain_rows = norm_gain[degree_of]
    scale_rows = inverse[degree_of]
    return (node_feats.astype(jnp.float32) * gain_rows[:, :, None] * scale_rows[:, None, :]).astype(
        jnp.bfloat16
    )


def normalize_rows(values, gain_full, totals):
    levels = MAX_DEGREE + 1
    degree_of = np.repeat(np.arange(levels), 2 * np.arange(levels) + 1)
    entry_counts = (2 * np.arange(levels) + 1) * CHANNELS
    inverse = 1.0 / jnp.sqrt(totals / jnp.asarray(entry_counts, jnp.float32)[:, None] + EPSILON)
    gain_rows = gain_full[degree_of]
    scale_rows = inverse[degree_of]
    return (values * gain_rows[:, :, None] * scale_rows[:, None, :]).astype(jnp.bfloat16)


def rotate(source, wig_rows):
    pieces = [None] * ROTATED
    for degree in range(MAX_DEGREE + 1):
        reach_order = min(degree, MAX_ORDER)
        span_cols = 2 * degree + 1
        first_row = wigner_start(degree)
        for position in range(2 * reach_order + 1):
            total = None
            for column in range(span_cols):
                term = wig_rows[first_row + position * span_cols + column][None, :] * source[degree * degree + column]
                total = term if total is None else total + term
            pieces[order_index(degree, position - reach_order)] = total
    return jnp.stack(pieces).astype(jnp.bfloat16)


def unrotate(gated, wig_rows):
    pieces = []
    for degree in range(MAX_DEGREE + 1):
        reach_order = min(degree, MAX_ORDER)
        span_cols = 2 * degree + 1
        first_row = wigner_start(degree)
        for column in range(span_cols):
            total = None
            for position in range(2 * reach_order + 1):
                term = wig_rows[first_row + position * span_cols + column][None, :] * gated[
                    order_index(degree, position - reach_order)
                ]
                total = term if total is None else total + term
            pieces.append(total)
    return jnp.stack(pieces)


def radial_weights(lengths, kind_ids, radial_in, species_table, radial_out):
    basis_count = radial_in.shape[0]
    spacing = CUTOFF / (basis_count - 1)
    centers = jnp.arange(basis_count, dtype=jnp.float32) * spacing
    basis_rows = jnp.exp(
        -0.5 * jnp.square((lengths[None, :] - centers[:, None]) / (2.0 * spacing))
    ).astype(jnp.bfloat16)
    onehot = (
        kind_ids[None, :] == jnp.arange(species_table.shape[0], dtype=jnp.int32)[:, None]
    ).astype(jnp.bfloat16)
    hidden = jax.nn.silu(left_dot(radial_in, basis_rows) + left_dot(species_table, onehot)).astype(
        jnp.bfloat16
    )
    return left_dot(radial_out, hidden)


def convolve(rotated, radial, order_zero, order_one, order_two):
    levels = MAX_DEGREE + 1
    channel_count = rotated.shape[1]
    num_edges = rotated.shape[2]
    lowest = (
        rotated[:levels].astype(jnp.float32).reshape(levels * channel_count, num_edges) * radial
    ).astype(jnp.bfloat16)
    outputs = [left_dot(order_zero, lowest).reshape(levels, channel_count, num_edges)]
    first_row = levels
    for harmonic, weight in ((1, order_one), (2, order_two)):
        span_rows = levels - harmonic
        plus_rows = rotated[first_row : first_row + span_rows].reshape(
            span_rows * channel_count, num_edges
        )
        minus_rows = rotated[first_row + span_rows : first_row + 2 * span_rows].reshape(
            span_rows * channel_count, num_edges
        )
        joined = jnp.concatenate([plus_rows, minus_rows], axis=1)
        real_part = left_dot(weight[0], joined)
        cross_part = left_dot(weight[1], joined)
        outputs.append(
            (real_part[:, :num_edges] - cross_part[:, num_edges:]).reshape(
                span_rows, channel_count, num_edges
            )
        )
        outputs.append(
            (cross_part[:, :num_edges] + real_part[:, num_edges:]).reshape(
                span_rows, channel_count, num_edges
            )
        )
        first_row = first_row + 2 * span_rows
    mixed = jnp.concatenate(outputs, axis=0)
    scalar = mixed[0]
    return jnp.concatenate(
        [jax.nn.silu(scalar)[None], mixed[1:] * jax.nn.sigmoid(scalar)[None]], axis=0
    ).astype(jnp.bfloat16)


def split_dot(values, weight):
    upper_part = values.astype(jnp.bfloat16)
    lower_part = (values - upper_part.astype(jnp.float32)).astype(jnp.bfloat16)
    return jnp.dot(upper_part, weight, preferred_element_type=jnp.float32) + jnp.dot(
        lower_part, weight, preferred_element_type=jnp.float32
    )


def body(
    node_feats,
    norm_gain,
    species,
    send_list,
    edge_source,
    edge_target,
    edge_count,
    edge_length,
    wigner,
    radial_in,
    species_table,
    radial_out,
    order_zero,
    order_one,
    order_two,
    project_weight,
):
    levels = MAX_DEGREE + 1
    owners = lax.axis_size("irreps")
    quarter = lax.axis_index("irreps")
    coeffs, span_chan, atom_count = node_feats.shape
    per_owner = edge_source.shape[0] // owners
    first_edge = quarter * per_owner

    outgoing = node_feats[:, :, send_list]
    arrived = lax.all_to_all(outgoing, "graph", split_axis=2, concat_axis=2, tiled=True)

    packed = jnp.concatenate(
        [norm_gain, project_weight.astype(jnp.float32).reshape(levels, -1)], axis=1
    )
    spread = lax.all_to_all(
        jnp.broadcast_to(packed[None], (owners,) + packed.shape), "irreps", 0, 0, tiled=True
    )
    gain_full = jnp.transpose(spread[:, :, :span_chan], (1, 0, 2)).reshape(levels, owners * span_chan)
    weight_full = jnp.transpose(
        spread[:, :, span_chan:].reshape(owners, levels, CHANNELS, span_chan), (1, 2, 0, 3)
    ).reshape(levels, CHANNELS, owners * span_chan)

    lookup = jnp.concatenate([node_feats, arrived], axis=2)
    source = lax.all_to_all(
        lookup[:, :, edge_source], "irreps", split_axis=2, concat_axis=1, tiled=True
    )
    source = source.astype(jnp.float32)
    squares = jnp.sum(jnp.square(source), axis=1)
    totals = degree_sums(squares)
    normed = normalize_rows(source, gain_full, totals)

    wig_mine = lax.dynamic_slice_in_dim(wigner, first_edge, per_owner, 1).astype(jnp.float32)
    rotated = rotate(normed.astype(jnp.float32), wig_mine)
    targets_mine = lax.dynamic_slice_in_dim(edge_target, first_edge, per_owner)
    lengths_mine = lax.dynamic_slice_in_dim(edge_length, first_edge, per_owner)
    radial = radial_weights(
        lengths_mine, species[targets_mine], radial_in, species_table, radial_out
    )
    gated = convolve(rotated, radial, order_zero, order_one, order_two)
    messages = unrotate(gated.astype(jnp.float32), wig_mine)
    edge_weight = jnp.where(
        first_edge + jnp.arange(per_owner, dtype=jnp.int32) < edge_count[0], 0.25, 0.0
    ).astype(jnp.float32)
    onehot = jnp.where(
        targets_mine[:, None] == jnp.arange(atom_count, dtype=jnp.int32)[None, :],
        edge_weight[:, None],
        0.0,
    ).astype(jnp.bfloat16)
    summed = split_dot(messages.reshape(-1, per_owner), onehot).reshape(coeffs, CHANNELS, atom_count)
    upper_part = summed.astype(jnp.bfloat16)
    lower_part = (summed - upper_part.astype(jnp.float32)).astype(jnp.bfloat16)
    updates = []
    for degree in range(levels):
        rows = slice(degree * degree, (degree + 1) ** 2)
        weight = weight_full[degree].astype(jnp.bfloat16)
        updates.append(
            jnp.einsum("io,jia->oja", weight, upper_part[rows], preferred_element_type=jnp.float32)
            + jnp.einsum("io,jia->oja", weight, lower_part[rows], preferred_element_type=jnp.float32)
        )
    projected = jnp.concatenate(updates, axis=1)
    returned = lax.all_to_all(
        projected.reshape(owners, span_chan, coeffs, atom_count), "irreps", 0, 0, tiled=True
    )
    total = jnp.transpose(jnp.sum(returned, axis=0), (1, 0, 2))
    return (node_feats.astype(jnp.float32) + total).astype(jnp.bfloat16)


def solution(mesh):
    return jax.shard_map(
        body,
        mesh=mesh,
        in_specs=(
            P(None, "irreps", "graph"),
            P(None, "irreps"),
            P("graph"),
            P("graph"),
            P("graph"),
            P("graph"),
            P("graph"),
            P("graph"),
            P(None, "graph"),
            P(),
            P(),
            P(),
            P(),
            P(),
            P(),
            P(None, None, "irreps"),
        ),
        out_specs=P(None, "irreps", "graph"),
        check_vma=False,
    )
```

profile of v0, /device:TPU:2, one launch (start us, length us, event | category | flops | bytes accessed | tf_op | source)
XLA Modules:
  0.0 238.1 jit_solution(476793149073174638)
XLA Ops:
  0.0 1.2 copy.225
  2.5 0.8 gather_fusion
  3.4 2.0 reshape.3035
  5.5 15.5 %all-to-all-start.1 = ((bf16[32,2,1568]{2,1,0:T(2,128)(2,1)}), bf16[32,2,1568]{2,1,0:T(2,128)(2,1)S(1)}, u32[]{:S(2)}, u32[]{:S(2)}) async-start(bf16[32,2,1568]{2,1,0:T(2,128)(2,1)} %reshape.3035), calls=%async_computation.1 | async-start | bytes 425984 | tf_op jit(solution)/shard_map/all_to_all | solution.py:192
  21.0 0.9 dynamic-slice_convert_fusion
  30.8 1.3 compare_select_fusion.2
  34.0 7.6 %all-to-all-done.1 = bf16[32,2,1568]{2,1,0:T(2,128)(2,1)S(1)} async-done(((bf16[32,2,1568]{2,1,0:T(2,128)(2,1)}), bf16[32,2,1568]{2,1,0:T(2,128)(2,1)S(1)}, u32[]{:S(2)}, u32[]{:S(2)}) %all-to-all-start.1) | async-done | bytes 200736 | tf_op jit(solution)/shard_map/all_to_all | solution.py:192
  41.6 0.9 broadcast_in_dim.56
  42.6 7.5 %all-to-all-start = ((f32[16,7,1032]{2,1,0:T(8,128)}), f32[16,7,1032]{2,1,0:T(8,128)}, u32[]{:S(2)}, u32[]{:S(2)}) async-start(f32[16,7,1032]{2,1,0:T(8,128)} %broadcast_in_dim.56), calls=%async_computation | async-start | bytes 1179648 | tf_op jit(solution)/shard_map/all_to_all | solution.py:197
  50.0 1.6 reshape.3036
  51.8 7.7 %gather_fusion.1 = bf16[1024,49,8]{1,2,0:T(8,128)(2,1)} fusion(bf16[49,8,320]{0,1,2:T(8,128)(2,1)S(1)} %pad_maximum_fusion, s32[1024]{0:T(1024)S(1)} %get-tuple-element.263), kind=kCustom, calls=%fused_computation.1 | custom fusion | bytes 1609728 | tf_op jit(solution)/shard_map/gather | solution.py:207
  59.5 3.1 %bitcast_bitcast_fusion = bf16[1024,8,49]{2,1,0:T(8,128)(2,1)} fusion(bf16[1024,49,8]{1,2,0:T(8,128)(2,1)} %gather_fusion.1), kind=kLoop, calls=%fused_computation.490 | loop fusion | bytes 1605632
  62.6 5.8 %reshape.3037 = bf16[16,2,12544]{2,1,0:T(2,128)(2,1)} reshape(bf16[1024,8,49]{2,1,0:T(8,128)(2,1)} %bitcast_bitcast_fusion) | data formatting | bytes 1605632
  68.4 7.4 %all-to-all-start.2 = ((bf16[16,2,12544]{2,1,0:T(2,128)(2,1)}), bf16[16,2,12544]{2,1,0:T(2,128)(2,1)S(1)}, u32[]{:S(2)}, u32[]{:S(2)}) async-start(bf16[16,2,12544]{2,1,0:T(2,128)(2,1)} %reshape.3037), calls=%async_computation.2 | async-start | bytes 1605632 | tf_op jit(solution)/shard_map/all_to_all | solution.py:206
  77.4 1.2 slice.2090
  78.7 1.6 copy.222
  80.4 2.4 %fusion.73 = (bf16[1,128,16,8]{2,3,1,0:T(8,128)(2,1)S(1)}, bf16[1,128,16,8]{2,3,1,0:T(8,128)(2,1)S(1)}, bf16[1,128,16,8]{2,3,1,0:T(8,128)(2,1)S(1)}, bf16[1,128,...) fusion(bf16[7,128,16,8]{2,3,1,0:T(8,128)(2,1)} %bitcast.748), kind=kLoop, calls=%fused_computation.487 | loop fusion | bytes 458752 | tf_op jit(solution)/shard_map/slice | solution.py:237
  82.8 1.8 copy.223
  84.6 0.8 slice_bitcast_fusion
  85.5 1.8 copy.244
  87.3 1.8 copy.248
  89.0 0.8 copy.252
  89.8 0.8 copy.256
  92.8 7.4 %reshape.3038 = bf16[1024,8,49]{2,1,0:T(8,128)(2,1)} reshape(bf16[16,2,12544]{2,1,0:T(2,128)(2,1)S(1)} %all-to-all-done.2) | data formatting | bytes 1605632
  100.2 3.1 %multiply_reduce_fusion = f32[49,1024]{0,1:T(8,128)S(1)} fusion(bf16[1024,8,49]{2,1,0:T(8,128)(2,1)} %reshape.3038), kind=kLoop, calls=%fused_computation.6 | loop fusion | flops 1154048 | bytes 1003520 | tf_op jit(solution)/shard_map/reduce_sum | solution.py:210
  104.4 4.9 %copy.226 = f32[49,8,16,64]{3,1,2,0:T(8,128)} copy(bf16[49,8,16,64]{0,1,3,2:T(8,128)(2,1)} %bitcast.745) | data formatting | bytes 2408448 | tf_op jit(solution)/shard_map/convert_element_type | solution.py:209
  109.4 3.4 %copy.228 = f32[49,128,64]{1,2,0:T(8,128)} copy(f32[49,128,64]{2,1,0:T(8,128)} %bitcast.746) | data formatting | bytes 3211264 | tf_op jit(solution)/shard_map/convert_element_type | solution.py:209
  113.7 1.9 fusion.17
  117.5 0.8 constant_dynamic-update-slice_fusion.10
  118.4 0.9 constant_dynamic-update-slice_fusion.9
  119.7 0.9 constant_dynamic-update-slice_fusion.7
  120.7 1.6 constant_dynamic-update-slice_fusion.29
  122.3 1.4 constant_dynamic-update-slice_fusion.25
  123.7 1.4 constant_dynamic-update-slice_fusion.18
  125.3 0.8 constant_dynamic-update-slice_fusion.16
  127.3 0.9 constant_dynamic-update-slice_fusion.13
  128.4 1.1 convolution_bitcast_fusion.1
  129.7 1.1 convolution_bitcast_fusion
  131.0 0.9 constant_dynamic-update-slice_fusion.23
  132.9 0.9 constant_dynamic-update-slice_fusion.21
  134.4 0.9 constant_dynamic-update-slice_fusion.26
  136.0 1.1 convolution_bitcast_fusion.2
  139.6 1.4 constant_dynamic-update-slice_fusion
  141.0 1.5 fusion.9
  142.6 1.3 fusion.22
  155.2 0.8 constant_dynamic-update-slice_fusion.69
  159.3 0.8 constant_dynamic-update-slice_fusion.64
  162.6 0.8 constant_dynamic-update-slice_fusion.60
  172.0 0.8 constant_dynamic-update-slice_fusion.47
  172.9 0.8 constant_dynamic-update-slice_fusion.46
  183.9 0.8 copy.247
  187.0 0.8 add.2075
  187.8 1.2 copy.263
  189.9 1.6 bitcast_dynamic-update-slice_fusion.8
  192.3 0.8 bitcast_dynamic-update-slice_fusion.3
  193.1 0.9 bitcast_dynamic-update-slice_fusion.2
  194.0 0.9 bitcast_dynamic-update-slice_fusion.1
  194.9 1.0 bitcast_dynamic-update-slice_fusion
  195.8 2.1 copy.322
  198.0 3.0 %reshape.3039 = f32[16,1,25088]{2,1,0:T(1,128)} reshape(f32[16,49,8,64]{3,2,1,0:T(8,128)S(1)} %bitcast.747) | data formatting | bytes 3211264
  200.9 27.3 %all_to_all.24 = f32[16,1,25088]{2,1,0:T(1,128)S(1)} all-to-all(f32[16,1,25088]{2,1,0:T(1,128)} %reshape.3039), channel_id=1, replica_groups=mesh['graph'=32,'irreps'=16] {'irreps'}, dimensions={0} | all-to-all | bytes 3211264 | tf_op jit(solution)/shard_map/all_to_all | solution.py:243
  228.7 4.5 %reduce.4 = f32[16,25088]{1,0:T(8,128)S(1)} reduce(f32[16,1,25088]{2,1,0:T(1,128)S(1)} %all_to_all.24, f32[]{:T(128)} %broadcast.1939), dimensions={1}, to_apply=%all_to_all.19.reduce_sub_computation | reduce | bytes 3211268 | tf_op jit(solution)/shard_map/all_to_all | solution.py:243
  233.2 2.0 reshape.3040
  235.3 2.2 bitcast_reduce_fusion
  (725 shorter events, 63.4 us)
Async XLA Ops:
  0.0 141.0 %copy-start = (bf16[896,896]{1,0:T(8,128)(2,1)S(1)}, bf16[896,896]{1,0:T(8,128)(2,1)}, u32[]{:S(2)}) copy-start(bf16[896,896]{1,0:T(8,128)(2,1)} %param.32) | copy-start | bytes 4816900
  0.0 29.8 %copy-start.16 = (bf16[7,128,8]{1,2,0:T(8,128)(2,1)S(1)}, bf16[7,128,8]{1,2,0:T(8,128)(2,1)}, u32[]{:S(2)}) copy-start(bf16[7,128,8]{1,2,0:T(8,128)(2,1)} %param.35) | copy-start | bytes 43012
  3.4 29.5 %copy-start.274 = (s32[1024]{0:T(1024)S(1)}, s32[1024]{0:T(1024)}, u32[]{:S(2)}) copy-start(s32[1024]{0:T(1024)} %param.24) | copy-start | bytes 12292
  3.4 30.2 %copy-start.275 = (f32[7,8]{1,0:T(8,128)S(1)}, f32[7,8]{1,0:T(8,128)}, u32[]{:S(2)}) copy-start(f32[7,8]{1,0:T(8,128)} %param.21) | copy-start | bytes 676
  3.4 30.3 %copy-start.278 = (bf16[512,128]{1,0:T(8,128)(2,1)S(1)}, bf16[512,128]{1,0:T(8,128)(2,1)}, u32[]{:S(2)}) copy-start(bf16[512,128]{1,0:T(8,128)(2,1)} %param.29) | copy-start | bytes 393220
  5.5 36.2 %all-to-all-start.1 = ((bf16[32,2,1568]{2,1,0:T(2,128)(2,1)}), bf16[32,2,1568]{2,1,0:T(2,128)(2,1)S(1)}, u32[]{:S(2)}, u32[]{:S(2)}) async-start(bf16[32,2,1568]{2,1,0:T(2,128)(2,1)} %reshape.3035), calls=%async_computation.1 | async-start | bytes 425984 | tf_op jit(solution)/shard_map/all_to_all | solution.py:192
  25.2 108.9 %copy-start.23 = (f32[64]{0:T(128)}, f32[64]{0:T(128)S(1)}, u32[]{:S(2)}) copy-start(f32[64]{0:T(128)S(1)} %get-tuple-element.48) | copy-start | bytes 772
  25.2 108.9 %copy-start.25 = (f32[64]{0:T(128)}, f32[64]{0:T(128)S(1)}, u32[]{:S(2)}) copy-start(f32[64]{0:T(128)S(1)} %get-tuple-element.49) | copy-start | bytes 772
  42.6 25.9 %all-to-all-start = ((f32[16,7,1032]{2,1,0:T(8,128)}), f32[16,7,1032]{2,1,0:T(8,128)}, u32[]{:S(2)}, u32[]{:S(2)}) async-start(f32[16,7,1032]{2,1,0:T(8,128)} %broadcast_in_dim.56), calls=%async_computation | async-start | bytes 1179648 | tf_op jit(solution)/shard_map/all_to_all | solution.py:197
  62.6 13.8 %copy-start.2 = (s32[64]{0:T(128)S(1)}, s32[64]{0:T(128)}, u32[]{:S(2)}) copy-start(s32[64]{0:T(128)} %param.22) | copy-start | bytes 772
  68.4 24.4 %all-to-all-start.2 = ((bf16[16,2,12544]{2,1,0:T(2,128)(2,1)}), bf16[16,2,12544]{2,1,0:T(2,128)(2,1)S(1)}, u32[]{:S(2)}, u32[]{:S(2)}) async-start(bf16[16,2,12544]{2,1,0:T(2,128)(2,1)} %reshape.3037), calls=%async_computation.2 | async-start | bytes 1605632 | tf_op jit(solution)/shard_map/all_to_all | solution.py:206
  144.5 10.6 %copy-start.58 = (f32[64]{0:T(128)S(1)}, f32[64]{0:T(128)}, u32[]{:S(2)}) copy-start(f32[64]{0:T(128)} %get-tuple-element.107) | copy-start | bytes 772
  144.6 11.4 %copy-start.48 = (f32[64]{0:T(128)S(1)}, f32[64]{0:T(128)}, u32[]{:S(2)}) copy-start(f32[64]{0:T(128)} %get-tuple-element.106) | copy-start | bytes 772
  144.6 12.2 %copy-start.40 = (f32[64]{0:T(128)S(1)}, f32[64]{0:T(128)}, u32[]{:S(2)}) copy-start(f32[64]{0:T(128)} %get-tuple-element.104) | copy-start | bytes 772
  144.6 13.0 %copy-start.34 = (f32[64]{0:T(128)S(1)}, f32[64]{0:T(128)}, u32[]{:S(2)}) copy-start(f32[64]{0:T(128)} %get-tuple-element.105) | copy-start | bytes 772
  147.0 13.1 %copy-start.88 = (f32[64]{0:T(128)S(1)}, f32[64]{0:T(128)}, u32[]{:S(2)}) copy-start(f32[64]{0:T(128)} %get-tuple-element.56) | copy-start | bytes 772
  147.8 13.1 %copy-start.78 = (f32[64]{0:T(128)S(1)}, f32[64]{0:T(128)}, u32[]{:S(2)}) copy-start(f32[64]{0:T(128)} %get-tuple-element.55) | copy-start | bytes 772
  148.6 13.1 %copy-start.66 = (f32[64]{0:T(128)S(1)}, f32[64]{0:T(128)}, u32[]{:S(2)}) copy-start(f32[64]{0:T(128)} %get-tuple-element.54) | copy-start | bytes 772
  149.4 13.1 %copy-start.56 = (f32[64]{0:T(128)S(1)}, f32[64]{0:T(128)}, u32[]{:S(2)}) copy-start(f32[64]{0:T(128)} %get-tuple-element.53) | copy-start | bytes 772
  150.3 13.1 %copy-start.46 = (f32[64]{0:T(128)S(1)}, f32[64]{0:T(128)}, u32[]{:S(2)}) copy-start(f32[64]{0:T(128)} %get-tuple-element.52) | copy-start | bytes 772
  151.1 13.1 %copy-start.38 = (f32[64]{0:T(128)S(1)}, f32[64]{0:T(128)}, u32[]{:S(2)}) copy-start(f32[64]{0:T(128)} %get-tuple-element.47) | copy-start | bytes 772
  151.1 13.1 %copy-start.90 = (f32[64]{0:T(128)S(1)}, f32[64]{0:T(128)}, u32[]{:S(2)}) copy-start(f32[64]{0:T(128)} %get-tuple-element.230) | copy-start | bytes 772
  151.9 13.1 %copy-start.32 = (f32[64]{0:T(128)S(1)}, f32[64]{0:T(128)}, u32[]{:S(2)}) copy-start(f32[64]{0:T(128)} %get-tuple-element.51) | copy-start | bytes 772
  151.9 13.1 %copy-start.80 = (f32[64]{0:T(128)S(1)}, f32[64]{0:T(128)}, u32[]{:S(2)}) copy-start(f32[64]{0:T(128)} %get-tuple-element.237) | copy-start | bytes 772
  152.6 10.8 %copy-start.101 = (f32[64]{0:T(128)S(1)}, f32[64]{0:T(128)}, u32[]{:S(2)}) copy-start(f32[64]{0:T(128)} %get-tuple-element.238) | copy-start | bytes 772
  152.6 13.1 %copy-start.28 = (f32[64]{0:T(128)S(1)}, f32[64]{0:T(128)}, u32[]{:S(2)}) copy-start(f32[64]{0:T(128)} %get-tuple-element.50) | copy-start | bytes 772
  152.6 13.1 %copy-start.70 = (f32[64]{0:T(128)S(1)}, f32[64]{0:T(128)}, u32[]{:S(2)}) copy-start(f32[64]{0:T(128)} %get-tuple-element.236) | copy-start | bytes 772
  153.5 13.0 %copy-start.26 = (f32[64]{0:T(128)S(1)}, f32[64]{0:T(128)}, u32[]{:S(2)}) copy-start(f32[64]{0:T(128)} %copy-done.25) | copy-start | bytes 772
  153.5 13.0 %copy-start.60 = (f32[64]{0:T(128)S(1)}, f32[64]{0:T(128)}, u32[]{:S(2)}) copy-start(f32[64]{0:T(128)} %get-tuple-element.235) | copy-start | bytes 772
  154.3 12.2 %copy-start.114 = (f32[64]{0:T(128)S(1)}, f32[64]{0:T(128)}, u32[]{:S(2)}) copy-start(f32[64]{0:T(128)} %get-tuple-element.186) | copy-start | bytes 772
  154.3 13.0 %copy-start.24 = (f32[64]{0:T(128)S(1)}, f32[64]{0:T(128)}, u32[]{:S(2)}) copy-start(f32[64]{0:T(128)} %copy-done.23) | copy-start | bytes 772
  154.3 13.0 %copy-start.50 = (f32[64]{0:T(128)S(1)}, f32[64]{0:T(128)}, u32[]{:S(2)}) copy-start(f32[64]{0:T(128)} %get-tuple-element.234) | copy-start | bytes 772
  154.3 13.0 %copy-start.103 = (f32[64]{0:T(128)S(1)}, f32[64]{0:T(128)}, u32[]{:S(2)}) copy-start(f32[64]{0:T(128)} %get-tuple-element.185) | copy-start | bytes 772
  155.1 10.6 %copy-start.124 = (f32[64]{0:T(128)S(1)}, f32[64]{0:T(128)}, u32[]{:S(2)}) copy-start(f32[64]{0:T(128)} %get-tuple-element.187) | copy-start | bytes 772
  155.1 13.0 %copy-start.42 = (f32[64]{0:T(128)S(1)}, f32[64]{0:T(128)}, u32[]{:S(2)}) copy-start(f32[64]{0:T(128)} %get-tuple-element.233) | copy-start | bytes 772
  155.1 13.0 %copy-start.94 = (f32[64]{0:T(128)S(1)}, f32[64]{0:T(128)}, u32[]{:S(2)}) copy-start(f32[64]{0:T(128)} %get-tuple-element.184) | copy-start | bytes 772
  156.0 13.0 %copy-start.36 = (f32[64]{0:T(128)S(1)}, f32[64]{0:T(128)}, u32[]{:S(2)}) copy-start(f32[64]{0:T(128)} %get-tuple-element.232) | copy-start | bytes 772
  156.0 13.0 %copy-start.84 = (f32[64]{0:T(128)S(1)}, f32[64]{0:T(128)}, u32[]{:S(2)}) copy-start(f32[64]{0:T(128)} %get-tuple-element.183) | copy-start | bytes 772
  156.8 13.1 %copy-start.30 = (f32[64]{0:T(128)S(1)}, f32[64]{0:T(128)}, u32[]{:S(2)}) copy-start(f32[64]{0:T(128)} %get-tuple-element.231) | copy-start | bytes 772
  156.8 13.1 %copy-start.74 = (f32[64]{0:T(128)S(1)}, f32[64]{0:T(128)}, u32[]{:S(2)}) copy-start(f32[64]{0:T(128)} %get-tuple-element.182) | copy-start | bytes 772
  156.8 13.1 %copy-start.128 = (f32[64]{0:T(128)S(1)}, f32[64]{0:T(128)}, u32[]{:S(2)}) copy-start(f32[64]{0:T(128)} %get-tuple-element.134) | copy-start | bytes 772
  157.7 11.4 %copy-start.138 = (f32[64]{0:T(128)S(1)}, f32[64]{0:T(128)}, u32[]{:S(2)}) copy-start(f32[64]{0:T(128)} %get-tuple-element.136) | copy-start | bytes 772
  157.7 13.1 %copy-start.22 = (f32[64]{0:T(128)S(1)}, f32[64]{0:T(128)}, u32[]{:S(2)}) copy-start(f32[64]{0:T(128)} %get-tuple-element.229) | copy-start | bytes 772
  157.7 13.1 %copy-start.64 = (f32[64]{0:T(128)S(1)}, f32[64]{0:T(128)}, u32[]{:S(2)}) copy-start(f32[64]{0:T(128)} %get-tuple-element.181) | copy-start | bytes 772
  157.7 13.1 %copy-start.118 = (f32[64]{0:T(128)S(1)}, f32[64]{0:T(128)}, u32[]{:S(2)}) copy-start(f32[64]{0:T(128)} %get-tuple-element.133) | copy-start | bytes 772
  158.5 13.2 %copy-start.20 = (f32[64]{0:T(128)S(1)}, f32[64]{0:T(128)}, u32[]{:S(2)}) copy-start(f32[64]{0:T(128)} %get-tuple-element.228) | copy-start | bytes 772
  158.5 13.2 %copy-start.54 = (f32[64]{0:T(128)S(1)}, f32[64]{0:T(128)}, u32[]{:S(2)}) copy-start(f32[64]{0:T(128)} %get-tuple-element.180) | copy-start | bytes 772
  158.5 13.2 %copy-start.107 = (f32[64]{0:T(128)S(1)}, f32[64]{0:T(128)}, u32[]{:S(2)}) copy-start(f32[64]{0:T(128)} %get-tuple-element.132) | copy-start | bytes 772
  159.3 12.5 %copy-start.18 = (f32[64]{0:T(128)S(1)}, f32[64]{0:T(128)}, u32[]{:S(2)}) copy-start(f32[64]{0:T(128)} %get-tuple-element.227) | copy-start | bytes 772
  159.3 12.5 %copy-start.44 = (f32[64]{0:T(128)S(1)}, f32[64]{0:T(128)}, u32[]{:S(2)}) copy-start(f32[64]{0:T(128)} %get-tuple-element.179) | copy-start | bytes 772
  159.3 12.5 %copy-start.96 = (f32[64]{0:T(128)S(1)}, f32[64]{0:T(128)}, u32[]{:S(2)}) copy-start(f32[64]{0:T(128)} %get-tuple-element.131) | copy-start | bytes 772
  159.3 12.5 %copy-start.142 = (f32[64]{0:T(128)S(1)}, f32[64]{0:T(128)}, u32[]{:S(2)}) copy-start(f32[64]{0:T(128)} %get-tuple-element.86) | copy-start | bytes 772
  166.5 11.1 %copy-start.234 = (f32[64]{0:T(128)S(1)}, f32[64]{0:T(128)}, u32[]{:S(2)}) copy-start(f32[64]{0:T(128)} %get-tuple-element.171) | copy-start | bytes 772
  166.5 11.9 %copy-start.231 = (f32[64]{0:T(128)S(1)}, f32[64]{0:T(128)}, u32[]{:S(2)}) copy-start(f32[64]{0:T(128)} %get-tuple-element.170) | copy-start | bytes 772
  167.4 11.8 %copy-start.228 = (f32[64]{0:T(128)S(1)}, f32[64]{0:T(128)}, u32[]{:S(2)}) copy-start(f32[64]{0:T(128)} %get-tuple-element.169) | copy-start | bytes 772
  167.4 11.8 %copy-start.239 = (f32[64]{0:T(128)S(1)}, f32[64]{0:T(128)}, u32[]{:S(2)}) copy-start(f32[64]{0:T(128)} %get-tuple-element.121) | copy-start | bytes 772
  168.2 10.2 %copy-start.241 = (f32[64]{0:T(128)S(1)}, f32[64]{0:T(128)}, u32[]{:S(2)}) copy-start(f32[64]{0:T(128)} %get-tuple-element.122) | copy-start | bytes 772
  168.2 11.2 %copy-start.227 = (f32[64]{0:T(128)S(1)}, f32[64]{0:T(128)}, u32[]{:S(2)}) copy-start(f32[64]{0:T(128)} %get-tuple-element.168) | copy-start | bytes 772
  168.2 11.2 %copy-start.236 = (f32[64]{0:T(128)S(1)}, f32[64]{0:T(128)}, u32[]{:S(2)}) copy-start(f32[64]{0:T(128)} %get-tuple-element.120) | copy-start | bytes 772
  169.0 10.2 %copy-start.244 = (f32[64]{0:T(128)S(1)}, f32[64]{0:T(128)}, u32[]{:S(2)}) copy-start(f32[64]{0:T(128)} %get-tuple-element.76) | copy-start | bytes 772
  169.0 10.4 %copy-start.243 = (f32[64]{0:T(128)S(1)}, f32[64]{0:T(128)}, u32[]{:S(2)}) copy-start(f32[64]{0:T(128)} %get-tuple-element.75) | copy-start | bytes 772
  169.1 10.5 %copy-start.226 = (f32[64]{0:T(128)S(1)}, f32[64]{0:T(128)}, u32[]{:S(2)}) copy-start(f32[64]{0:T(128)} %get-tuple-element.167) | copy-start | bytes 772
  169.1 10.5 %copy-start.233 = (f32[64]{0:T(128)S(1)}, f32[64]{0:T(128)}, u32[]{:S(2)}) copy-start(f32[64]{0:T(128)} %get-tuple-element.119) | copy-start | bytes 772
  169.1 10.5 %copy-start.242 = (f32[64]{0:T(128)S(1)}, f32[64]{0:T(128)}, u32[]{:S(2)}) copy-start(f32[64]{0:T(128)} %get-tuple-element.74) | copy-start | bytes 772
  (223 other events, 1106.7 us)
where the time goes:
time: 240 us; the launch traced here: 238 us
  local copies, waits for them, and re-layouts  85.1 us (35%)
  other arithmetic  73.1 us (30%)
  starting transfers between devices  30.3 us (13%)
  blocking collectives  27.3 us (11%)
  matrix products  8.93 us (4%)
  waiting for transfers between devices  7.63 us (3%)
  between operations  5.71 us (2%)
    unnamed x70, other arithmetic  48.4 us
    unnamed x583, local copies, waits for them, and re-layouts  33.3 us
    all_to_all x1, blocking collectives, body(): lax.all_to_all(projected.reshape(owners, span_chan, coeffs, atom_count),...  27.3 us
    all_to_all x1, starting transfers between devices, body(): lax.all_to_all(outgoing, 'graph', split_axis=2, concat_axis=2, tiled=True)  15.5 us
    slice x8, local copies, waits for them, and re-layouts, body(): weight = weight_full[degree].astype(jnp.bfloat16)  10.9 us
    mul x13, local copies, waits for them, and re-layouts, rotate(): wig_rows[first_row + position * span_cols + column][None, :]  8.54 us
    convert_element_type x2, local copies, waits for them, and re-layouts, body(): source = source.astype(jnp.float32)  8.33 us
    gather x1, local copies, waits for them, and re-layouts, body(): lookup[:, :, edge_source]  7.66 us
  transfers between devices with their start and end apart: 3, of which 1 were waited for; matrix products, arithmetic and copies ran while one was open for 20% of the time, Pallas kernels for 0%

commit v1 on v0

--- a/solution.py
+++ b/solution.py
@@ -3,6 +3,8 @@
 import numpy as np
 from jax import lax
 from jax.sharding import PartitionSpec as P
+from jax.experimental import pallas as pl
+from jax.experimental.pallas import tpu as pltpu
 
 CHANNELS = 128
 MAX_DEGREE = 6
@@ -155,6 +157,149 @@
     ).astype(jnp.bfloat16)
 
 
+def conv_kernel(
+    src_ref, gain_ref, wig_ref, length_ref, kind_ref, basis_in_ref, kind_table_ref, radial_out_ref,
+    zero_ref, one_ref, two_ref, onehot_ref, proj_ref, out_ref,
+):
+    levels = MAX_DEGREE + 1
+    channel_count = src_ref.shape[1]
+    num_edges = src_ref.shape[2]
+    basis_count = basis_in_ref.shape[1]
+    wig = wig_ref[...].astype(jnp.float32)
+    gain = gain_ref[...]
+
+    rows = [src_ref[j].astype(jnp.float32) for j in range(src_ref.shape[0])]
+    normed = [None] * len(rows)
+    for degree in range(levels):
+        span = range(degree * degree, (degree + 1) ** 2)
+        total = None
+        for j in span:
+            part = jnp.sum(rows[j] * rows[j], axis=0, keepdims=True)
+            total = part if total is None else total + part
+        inverse = 1.0 / jnp.sqrt(total / float((2 * degree + 1) * CHANNELS) + EPSILON)
+        scale = gain[:, degree : degree + 1]
+        for j in span:
+            normed[j] = (rows[j] * scale * inverse).astype(jnp.bfloat16).astype(jnp.float32)
+
+    rotated = [None] * ROTATED
+    for degree in range(levels):
+        reach_order = min(degree, MAX_ORDER)
+        span_cols = 2 * degree + 1
+        first_row = wigner_start(degree)
+        for position in range(2 * reach_order + 1):
+            total = None
+            for column in range(span_cols):
+                row = first_row + position * span_cols + column
+                term = wig[row : row + 1, :] * normed[degree * degree + column]
+                total = term if total is None else total + term
+            rotated[order_index(degree, position - reach_order)] = total.astype(jnp.bfloat16)
+
+    spacing = CUTOFF / (basis_count - 1)
+    centers = lax.broadcasted_iota(jnp.int32, (basis_count, num_edges), 0).astype(jnp.float32) * spacing
+    basis_rows = jnp.exp(
+        -0.5 * jnp.square((length_ref[...] - centers) / (2.0 * spacing))
+    ).astype(jnp.bfloat16)
+    hidden = jnp.dot(basis_in_ref[...], basis_rows, preferred_element_type=jnp.float32) + jnp.dot(
+        kind_table_ref[...], kind_ref[...], preferred_element_type=jnp.float32
+    )
+    hidden = (hidden * jax.nn.sigmoid(hidden)).astype(jnp.bfloat16)
+    radial = jnp.dot(radial_out_ref[...], hidden, preferred_element_type=jnp.float32)
+
+    lowest = jnp.concatenate(
+        [
+            (rotated[degree].astype(jnp.float32) * radial[degree * channel_count : (degree + 1) * channel_count]).astype(
+                jnp.bfloat16
+            )
+            for degree in range(levels)
+        ],
+        axis=0,
+    )
+    mixed0 = jnp.dot(zero_ref[...], lowest, preferred_element_type=jnp.float32)
+    mixed = [mixed0[degree * channel_count : (degree + 1) * channel_count] for degree in range(levels)]
+    first_row = levels
+    for harmonic, weight_ref in ((1, one_ref), (2, two_ref)):
+        span_rows = levels - harmonic
+        plus_rows = jnp.concatenate(rotated[first_row : first_row + span_rows], axis=0)
+        minus_rows = jnp.concatenate(rotated[first_row + span_rows : first_row + 2 * span_rows], axis=0)
+        real_plus = jnp.dot(weight_ref[0], plus_rows, preferred_element_type=jnp.float32)
+        real_minus = jnp.dot(weight_ref[0], minus_rows, preferred_element_type=jnp.float32)
+        cross_plus = jnp.dot(weight_ref[1], plus_rows, preferred_element_type=jnp.float32)
+        cross_minus = jnp.dot(weight_ref[1], minus_rows, preferred_element_type=jnp.float32)
+        new_plus = real_plus - cross_minus
+        new_minus = cross_plus + real_minus
+        mixed += [new_plus[k * channel_count : (k + 1) * channel_count] for k in range(span_rows)]
+        mixed += [new_minus[k * channel_count : (k + 1) * channel_count] for k in range(span_rows)]
+        first_row = first_row + 2 * span_rows
+
+    scalar = mixed[0]
+    gate = jax.nn.sigmoid(scalar)
+    gated = [(scalar * gate).astype(jnp.bfloat16).astype(jnp.float32)] + [
+        (piece * gate).astype(jnp.bfloat16).astype(jnp.float32) for piece in mixed[1:]
+    ]
+
+    messages = []
+    for degree in range(levels):
+        reach_order = min(degree, MAX_ORDER)
+        span_cols = 2 * degree + 1
+        first_row = wigner_start(degree)
+        for column in range(span_cols):
+            total = None
+            for position in range(2 * reach_order + 1):
+                row = first_row + position * span_cols + column
+                term = wig[row : row + 1, :] * gated[order_index(degree, position - reach_order)]
+                total = term if total is None else total + term
+            messages.append(total)
+    stacked = jnp.concatenate(messages, axis=0)
+    upper_part = stacked.astype(jnp.bfloat16)
+    lower_part = (stacked - upper_part.astype(jnp.float32)).astype(jnp.bfloat16)
+    onehot = onehot_ref[...]
+    summed = jnp.dot(upper_part, onehot, preferred_element_type=jnp.float32) + jnp.dot(
+        lower_part, onehot, preferred_element_type=jnp.float32
+    )
+    for degree in range(levels):
+        weight = proj_ref[degree]
+        for j in range(degree * degree, (degree + 1) ** 2):
+            piece = summed[j * channel_count : (j + 1) * channel_count]
+            high = piece.astype(jnp.bfloat16)
+            low = (piece - high.astype(jnp.float32)).astype(jnp.bfloat16)
+            out_ref[j] = jnp.dot(weight, high, preferred_element_type=jnp.float32) + jnp.dot(
+                weight, low, preferred_element_type=jnp.float32
+            )
+
+
+def convolve_edges(source, gain_cols, wig_mine, lengths, kind_onehot, radial_in, species_table, radial_out,
+                   order_zero, order_one, order_two, onehot, proj_t):
+    coeffs, channel_count, num_edges = source.shape
+    atom_count = onehot.shape[1]
+    operands = (
+        source,
+        gain_cols,
+        wig_mine,
+        lengths[None, :],
+        kind_onehot,
+        radial_in.T,
+        species_table.T,
+        radial_out.T,
+        order_zero.T,
+        jnp.transpose(order_one, (0, 2, 1)),
+        jnp.transpose(order_two, (0, 2, 1)),
+        onehot,
+        proj_t,
+    )
+    flops = 2 * num_edges * (order_zero.size + 2 * order_one.size + 2 * order_two.size + radial_out.size + radial_in.size)
+    return pl.pallas_call(
+        conv_kernel,
+        out_shape=jax.ShapeDtypeStruct((coeffs, channel_count, atom_count), jnp.float32),
+        in_specs=[pl.BlockSpec(memory_space=pltpu.VMEM)] * len(operands),
+        out_specs=pl.BlockSpec(memory_space=pltpu.VMEM),
+        cost_estimate=pl.CostEstimate(
+            flops=flops,
+            transcendentals=num_edges * (radial_in.shape[0] + 2 * channel_count),
+            bytes_accessed=sum(int(x.size) * x.dtype.itemsize for x in operands) + coeffs * channel_count * atom_count * 4,
+        ),
+    )(*operands)
+
+
 def split_dot(values, weight):
     upper_part = values.astype(jnp.bfloat16)
     lower_part = (values - upper_part.astype(jnp.float32)).astype(jnp.bfloat16)
@@ -206,20 +351,13 @@
     source = lax.all_to_all(
         lookup[:, :, edge_source], "irreps", split_axis=2, concat_axis=1, tiled=True
     )
-    source = source.astype(jnp.float32)
-    squares = jnp.sum(jnp.square(source), axis=1)
-    totals = degree_sums(squares)
-    normed = normalize_rows(source, gain_full, totals)
-
-    wig_mine = lax.dynamic_slice_in_dim(wigner, first_edge, per_owner, 1).astype(jnp.float32)
-    rotated = rotate(normed.astype(jnp.float32), wig_mine)
+    wig_mine = lax.dynamic_slice_in_dim(wigner, first_edge, per_owner, 1)
     targets_mine = lax.dynamic_slice_in_dim(edge_target, first_edge, per_owner)
     lengths_mine = lax.dynamic_slice_in_dim(edge_length, first_edge, per_owner)
-    radial = radial_weights(
-        lengths_mine, species[targets_mine], radial_in, species_table, radial_out
-    )
-    gated = convolve(rotated, radial, order_zero, order_one, order_two)
-    messages = unrotate(gated.astype(jnp.float32), wig_mine)
+    kinds = species[targets_mine]
+    kind_onehot = (
+        kinds[None, :] == jnp.arange(species_table.shape[0], dtype=jnp.int32)[:, None]
+    ).astype(jnp.bfloat16)
     edge_weight = jnp.where(
         first_edge + jnp.arange(per_owner, dtype=jnp.int32) < edge_count[0], 0.25, 0.0
     ).astype(jnp.float32)
@@ -228,18 +366,12 @@
         edge_weight[:, None],
         0.0,
     ).astype(jnp.bfloat16)
-    summed = split_dot(messages.reshape(-1, per_owner), onehot).reshape(coeffs, CHANNELS, atom_count)
-    upper_part = summed.astype(jnp.bfloat16)
-    lower_part = (summed - upper_part.astype(jnp.float32)).astype(jnp.bfloat16)
-    updates = []
-    for degree in range(levels):
-        rows = slice(degree * degree, (degree + 1) ** 2)
-        weight = weight_full[degree].astype(jnp.bfloat16)
-        updates.append(
-            jnp.einsum("io,jia->oja", weight, upper_part[rows], preferred_element_type=jnp.float32)
-            + jnp.einsum("io,jia->oja", weight, lower_part[rows], preferred_element_type=jnp.float32)
-        )
-    projected = jnp.concatenate(updates, axis=1)
+    proj_t = jnp.transpose(weight_full, (0, 2, 1)).astype(jnp.bfloat16)
+    projected = convolve_edges(
+        source, gain_full.T, wig_mine, lengths_mine, kind_onehot, radial_in, species_table, radial_out,
+        order_zero, order_one, order_two, onehot, proj_t,
+    )
+    projected = jnp.transpose(projected, (1, 0, 2))
     returned = lax.all_to_all(
         projected.reshape(owners, span_chan, coeffs, atom_count), "irreps", 0, 0, tiled=True
     )

time: 240 us -> 157 us (0.65)
  the two profiles are of different devices: /device:TPU:2 before, /device:TPU:64 now
where the time goes in v1:
time: 157 us; the launch traced here: 156 us
  local copies, waits for them, and re-layouts  66.1 us (42%)
  starting transfers between devices  29.2 us (19%)
  blocking collectives  26.7 us (17%)
  Pallas kernels  12.1 us (8%)
  other arithmetic  11.8 us (8%)
  waiting for transfers between devices  9.56 us (6%)
    unnamed x40, local copies, waits for them, and re-layouts  43.1 us
    all_to_all x1, blocking collectives, body(): lax.all_to_all(projected.reshape(owners, span_chan, coeffs, atom_count),...  26.7 us
    all_to_all x1, starting transfers between devices, body(): lax.all_to_all(outgoing, 'graph', split_axis=2, concat_axis=2, tiled=True)  14.9 us
    pallas_call x1, Pallas kernels, convolve_edges(): pl.pallas_call(conv_kernel, out_shape=jax.ShapeDtypeStruct((coeffs, chann...  12.1 us
    gather x1, local copies, waits for them, and re-layouts, body(): lookup[:, :, edge_source]  7.59 us
    all_to_all x1, starting transfers between devices, body(): lax.all_to_all(lookup[:, :, edge_source], 'irreps', split_axis=2, concat_...  7.22 us
    all_to_all x1, starting transfers between devices, body(): lax.all_to_all(jnp.broadcast_to(packed[None], (owners,) + packed.shape),...  7.03 us
    all_to_all x1, waiting for transfers between devices, body(): lax.all_to_all(lookup[:, :, edge_source], 'irreps', split_axis=2, concat_...  6.69 us
  transfers between devices with their start and end apart: 3, of which 2 were waited for; matrix products, arithmetic and copies ran while one was open for 25% of the time, Pallas kernels for 0%

profile of v1, /device:TPU:64, one launch (start us, length us, event | category | flops | bytes accessed | tf_op | source)
XLA Modules:
  0.0 156.3 jit_solution(5947018698541686291)
XLA Ops:
  0.0 0.0 copy-start
  0.0 1.2 copy.53
  1.2 0.7 compare_select_fusion.1
  1.9 1.6 %gather_fusion = bf16[256,49,8]{1,2,0:T(8,128)(2,1)} fusion(bf16[49,8,64]{0,1,2:T(8,128)(2,1)S(1)} %copy.53, s32[1024]{0:T(1024)S(1)} %pad_clamp_fusion.1), kind=kCustom, calls=%fused_computation | custom fusion | bytes 402432 | tf_op jit(solution)/shard_map/gather | solution.py:336
  3.5 1.1 bitcast_bitcast_fusion.1
  4.6 2.0 %reshape.58 = bf16[32,2,1568]{2,1,0:T(2,128)(2,1)} reshape(bf16[256,8,49]{2,1,0:T(8,128)(2,1)S(1)} %bitcast_bitcast_fusion.1) | data formatting | bytes 401408
  6.6 14.9 %all-to-all-start = ((bf16[32,2,1568]{2,1,0:T(2,128)(2,1)}), bf16[32,2,1568]{2,1,0:T(2,128)(2,1)}, u32[]{:S(2)}, u32[]{:S(2)}) async-start(bf16[32,2,1568]{2,1,0:T(2,128)(2,1)} %reshape.58), calls=%async_computation | async-start | bytes 425984 | tf_op jit(solution)/shard_map/all_to_all | solution.py:337
  22.2 0.0 copy-done.9
  22.2 0.1 copy.55
  22.4 0.2 reshape.30
  22.6 0.0 copy-done.2
  22.6 2.4 %copy.61 = bf16[2,768,768]{1,2,0:T(8,128)(2,1)} copy(bf16[2,768,768]{2,1,0:T(8,128)(2,1)S(1)} %copy-done.2) | data formatting | bytes 4718592 | tf_op args[13]
  25.1 3.7 %copy.62 = bf16[2,640,640]{1,2,0:T(8,128)(2,1)} copy(bf16[2,640,640]{2,1,0:T(8,128)(2,1)} %param.30) | data formatting | bytes 3276800 | tf_op args[14]
  28.7 0.0 copy-done.3
  28.7 0.0 copy-start.8
  28.7 0.0 copy-start.1
  28.8 0.0 copy-start.11
  28.8 0.0 copy-start.10
  28.8 2.3 %copy.60 = bf16[896,896]{0,1:T(8,128)(2,1)} copy(bf16[896,896]{1,0:T(8,128)(2,1)S(1)} %copy-done.3) | data formatting | bytes 3211264 | tf_op args[12]
  31.1 0.0 copy-done.6
  31.1 0.8 copy.59
  32.0 0.0 copy-done.7
  32.0 0.8 copy.57
  32.7 0.0 copy-done.8
  32.7 0.7 copy.58
  33.4 0.8 compare_select_fusion.2
  34.2 0.0 copy-done.1
  34.2 0.8 gather_fusion.2
  35.0 0.0 copy-done
  35.0 0.7 constant_dynamic-slice_fusion.wig_ref
  35.7 0.0 copy-done.11
  35.7 0.0 copy-done.10
  35.7 0.1 pad_maximum_fusion.1
  35.8 2.9 %all-to-all-done = bf16[32,2,1568]{2,1,0:T(2,128)(2,1)} async-done(((bf16[32,2,1568]{2,1,0:T(2,128)(2,1)}), bf16[32,2,1568]{2,1,0:T(2,128)(2,1)}, u32[]{:S(2)}, u32[]{:S(2)}) %all-to-all-start) | async-done | bytes 200736 | tf_op jit(solution)/shard_map/all_to_all | solution.py:337
  38.7 0.9 broadcast_in_dim.45
  39.6 7.0 %all-to-all-start.2 = ((f32[16,7,1032]{2,1,0:T(8,128)}), f32[16,7,1032]{2,1,0:T(8,128)S(1)}, u32[]{:S(2)}, u32[]{:S(2)}) async-start(f32[16,7,1032]{2,1,0:T(8,128)} %broadcast_in_dim.45), calls=%async_computation.2 | async-start | bytes 1179648 | tf_op jit(solution)/shard_map/all_to_all | solution.py:342
  46.6 2.5 %reshape.59 = bf16[256,8,49]{2,1,0:T(8,128)(2,1)S(1)} reshape(bf16[32,2,1568]{2,1,0:T(2,128)(2,1)} %all-to-all-done) | data formatting | bytes 401408
  49.1 0.1 pad_maximum_fusion
  49.3 7.6 %gather_fusion.1 = bf16[1024,49,8]{1,2,0:T(8,128)(2,1)} fusion(bf16[49,8,320]{0,1,2:T(8,128)(2,1)S(1)} %pad_maximum_fusion, s32[1024]{0:T(1024)S(1)} %fusion.2), kind=kCustom, calls=%fused_computation.1 | custom fusion | bytes 1609728 | tf_op jit(solution)/shard_map/gather | solution.py:352
  56.8 1.7 %bitcast_bitcast_fusion = bf16[1024,8,49]{2,1,0:T(8,128)(2,1)S(1)} fusion(bf16[1024,49,8]{1,2,0:T(8,128)(2,1)} %gather_fusion.1), kind=kLoop, calls=%fused_computation.24 | loop fusion | bytes 1605632
  58.6 5.1 %reshape.60 = bf16[16,2,12544]{2,1,0:T(2,128)(2,1)} reshape(bf16[1024,8,49]{2,1,0:T(8,128)(2,1)S(1)} %bitcast_bitcast_fusion) | data formatting | bytes 1605632
  63.7 0.0 all-to-all-done.2
  63.7 0.8 copy-done.4
  64.5 7.2 %all-to-all-start.1 = ((bf16[16,2,12544]{2,1,0:T(2,128)(2,1)}), bf16[16,2,12544]{2,1,0:T(2,128)(2,1)S(1)}, u32[]{:S(2)}, u32[]{:S(2)}) async-start(bf16[16,2,12544]{2,1,0:T(2,128)(2,1)} %reshape.60), calls=%async_computation.1 | async-start | bytes 1605632 | tf_op jit(solution)/shard_map/all_to_all | solution.py:351
  71.7 1.3 dynamic-slice_bitcast_fusion.length_ref
  73.1 0.7 select_convert_fusion.onehot_ref
  73.8 0.6 fusion.1.kind_ref
  74.4 1.2 slice.19
  75.6 0.9 copy.63
  76.5 2.1 %copy.64 = bf16[7,128,16,8]{1,3,2,0:T(8,128)(2,1)} copy(bf16[7,128,16,8]{2,3,1,0:T(8,128)(2,1)S(1)} %bitcast.50) | data formatting | bytes 458752 | tf_op jit(solution)/shard_map/convert_element_type | solution.py:369
  78.6 0.8 slice_bitcast_fusion
  79.4 0.8 copy.56
  80.2 6.7 %all-to-all-done.1 = bf16[16,2,12544]{2,1,0:T(2,128)(2,1)S(1)} async-done(((bf16[16,2,12544]{2,1,0:T(2,128)(2,1)}), bf16[16,2,12544]{2,1,0:T(2,128)(2,1)S(1)}, u32[]{:S(2)}, u32[]{:S(2)}) %all-to-all-start.1) | async-done | bytes 802848 | tf_op jit(solution)/shard_map/all_to_all | solution.py:351
  86.9 6.3 %reshape.61 = bf16[1024,8,49]{2,1,0:T(8,128)(2,1)S(1)} reshape(bf16[16,2,12544]{2,1,0:T(2,128)(2,1)S(1)} %all-to-all-done.1) | data formatting | bytes 1605632
  93.3 3.4 %copy.54 = bf16[49,8,16,64]{3,1,2,0:T(8,128)(2,1)} copy(bf16[49,8,16,64]{0,1,3,2:T(8,128)(2,1)S(1)} %bitcast.49) | data formatting | bytes 1605632 | tf_op jit(solution)/shard_map/all_to_all | solution.py:351
  96.7 12.1 %shard_map.154 = f32[49,128,64]{2,1,0:T(8,128)} custom-call(bf16[49,128,64]{2,1,0:T(8,128)(2,1)} %bitcast.52, f32[128,7]{1,0:T(8,128)} %bitcast.58, bf16[235,64]{1,0:T(8,128)(2,1)} %constant_dynamic-slice_fusion.wig_ref, f32[1,64]{1,0:T(1,128)} %dynamic-slice_bitcast_fusion.length_ref, bf16[90,64]{1,0:T(8,128)(2,1)} %fusion.1.kind_ref, ...), custom_call_target="tpu_custom_call" | custom-call | flops 637534208 | bytes 8678272 | tf_op jit(solution)/shard_map/pallas_call | solution.py:290
  108.8 3.8 %copy_bitcast_fusion = f32[16,49,8,64]{3,2,1,0:T(8,128)} fusion(f32[49,128,64]{2,1,0:T(8,128)} %shard_map.154), kind=kLoop, calls=%fused_computation.23 | loop fusion | bytes 3211264
  112.6 4.5 %reshape.62 = f32[16,1,25088]{2,1,0:T(1,128)} reshape(f32[16,49,8,64]{3,2,1,0:T(8,128)} %copy_bitcast_fusion) | data formatting | bytes 3211264
  117.1 26.7 %all_to_all.33 = f32[16,1,25088]{2,1,0:T(1,128)S(1)} all-to-all(f32[16,1,25088]{2,1,0:T(1,128)} %reshape.62), channel_id=1, replica_groups=mesh['graph'=32,'irreps'=16] {'irreps'}, dimensions={0} | all-to-all | bytes 3211264 | tf_op jit(solution)/shard_map/all_to_all | solution.py:375
  143.7 0.5 broadcast.31
  144.2 6.0 %reduce = f32[16,25088]{1,0:T(8,128)} reduce(f32[16,1,25088]{2,1,0:T(1,128)S(1)} %all_to_all.33, f32[]{:T(128)} %broadcast.31), dimensions={1}, to_apply=%all_to_all.28.reduce_sub_computation | reduce | bytes 3211268 | tf_op jit(solution)/shard_map/all_to_all | solution.py:375
  150.3 3.2 %reshape.63 = f32[16,49,8,64]{3,2,1,0:T(8,128)} reshape(f32[16,25088]{1,0:T(8,128)} %reduce) | data formatting | bytes 3211264
  153.4 2.2 %bitcast_reduce_fusion = f32[8,49,64]{2,0,1:T(8,128)S(1)} fusion(f32[16,49,8,64]{3,2,1,0:T(8,128)} %reshape.63), kind=kLoop, calls=%fused_computation.22 | loop fusion | flops 376320 | bytes 1705984 | tf_op jit(solution)/shard_map/reduce_sum | solution.py:378
  155.6 0.7 fusion
  (12 shorter events, 0.0 us)
Async XLA Ops:
  0.0 35.0 %copy-start = (bf16[235,1024]{1,0:T(8,128)(2,1)S(1)}, bf16[235,1024]{1,0:T(8,128)(2,1)}, u32[]{:S(2)}) copy-start(bf16[235,1024]{1,0:T(8,128)(2,1)} %param.24) | copy-start | bytes 1443844
  0.0 22.2 %copy-start.9 = (bf16[7,128,8]{1,2,0:T(8,128)(2,1)S(1)}, bf16[7,128,8]{1,2,0:T(8,128)(2,1)}, u32[]{:S(2)}) copy-start(bf16[7,128,8]{1,2,0:T(8,128)(2,1)} %param.31) | copy-start | bytes 43012
  0.0 22.6 %copy-start.2 = (bf16[2,768,768]{2,1,0:T(8,128)(2,1)S(1)}, bf16[2,768,768]{2,1,0:T(8,128)(2,1)}, u32[]{:S(2)}) copy-start(bf16[2,768,768]{2,1,0:T(8,128)(2,1)} %param.29) | copy-start | bytes 7077892
  6.6 32.1 %all-to-all-start = ((bf16[32,2,1568]{2,1,0:T(2,128)(2,1)}), bf16[32,2,1568]{2,1,0:T(2,128)(2,1)}, u32[]{:S(2)}, u32[]{:S(2)}) async-start(bf16[32,2,1568]{2,1,0:T(2,128)(2,1)} %reshape.58), calls=%async_computation | async-start | bytes 425984 | tf_op jit(solution)/shard_map/all_to_all | solution.py:337
  25.1 3.7 %copy-start.3 = (bf16[896,896]{1,0:T(8,128)(2,1)S(1)}, bf16[896,896]{1,0:T(8,128)(2,1)}, u32[]{:S(2)}) copy-start(bf16[896,896]{1,0:T(8,128)(2,1)} %param.28) | copy-start | bytes 4816900
  28.7 2.4 %copy-start.6 = (bf16[128,896]{1,0:T(8,128)(2,1)S(1)}, bf16[128,896]{1,0:T(8,128)(2,1)}, u32[]{:S(2)}) copy-start(bf16[128,896]{1,0:T(8,128)(2,1)} %param.27) | copy-start | bytes 688132
  28.7 3.2 %copy-start.7 = (bf16[512,128]{1,0:T(8,128)(2,1)S(1)}, bf16[512,128]{1,0:T(8,128)(2,1)}, u32[]{:S(2)}) copy-start(bf16[512,128]{1,0:T(8,128)(2,1)} %param.25) | copy-start | bytes 393220
  28.7 4.0 %copy-start.8 = (bf16[90,128]{1,0:T(8,128)(2,1)S(1)}, bf16[90,128]{1,0:T(8,128)(2,1)}, u32[]{:S(2)}) copy-start(bf16[90,128]{1,0:T(8,128)(2,1)} %param.26) | copy-start | bytes 69124
  28.7 5.5 %copy-start.1 = (s32[64]{0:T(128)S(1)}, s32[64]{0:T(128)}, u32[]{:S(2)}) copy-start(s32[64]{0:T(128)} %param.18) | copy-start | bytes 772
  28.8 7.0 %copy-start.11 = (s32[1024]{0:T(1024)S(1)}, s32[1024]{0:T(1024)}, u32[]{:S(2)}) copy-start(s32[1024]{0:T(1024)} %param.20) | copy-start | bytes 12292
  28.8 7.0 %copy-start.10 = (f32[7,8]{1,0:T(8,128)S(1)}, f32[7,8]{1,0:T(8,128)}, u32[]{:S(2)}) copy-start(f32[7,8]{1,0:T(8,128)} %param.17) | copy-start | bytes 676
  39.6 24.1 %all-to-all-start.2 = ((f32[16,7,1032]{2,1,0:T(8,128)}), f32[16,7,1032]{2,1,0:T(8,128)S(1)}, u32[]{:S(2)}, u32[]{:S(2)}) async-start(f32[16,7,1032]{2,1,0:T(8,128)} %broadcast_in_dim.45), calls=%async_computation.2 | async-start | bytes 1179648 | tf_op jit(solution)/shard_map/all_to_all | solution.py:342
  63.7 0.8 copy-start.4
  64.5 22.4 %all-to-all-start.1 = ((bf16[16,2,12544]{2,1,0:T(2,128)(2,1)}), bf16[16,2,12544]{2,1,0:T(2,128)(2,1)S(1)}, u32[]{:S(2)}, u32[]{:S(2)}) async-start(bf16[16,2,12544]{2,1,0:T(2,128)(2,1)} %reshape.60), calls=%async_computation.1 | async-start | bytes 1605632 | tf_op jit(solution)/shard_map/all_to_all | solution.py:351
  153.4 2.2 %copy-start.5 = (bf16[49,8,64]{2,1,0:T(8,128)(2,1)S(1)}, bf16[49,8,64]{2,1,0:T(8,128)(2,1)}, u32[]{:S(2)}) copy-start(bf16[49,8,64]{2,1,0:T(8,128)(2,1)} %param.16) | copy-start | bytes 150532

commit v2 on v1

--- a/solution.py
+++ b/solution.py
@@ -10,6 +10,7 @@
 MAX_DEGREE = 6
 MAX_ORDER = 2
 ROTATED = 29
+COEFFS = 49
 
 
 EPSILON = 1e-06
@@ -162,13 +163,18 @@
     zero_ref, one_ref, two_ref, onehot_ref, proj_ref, out_ref,
 ):
     levels = MAX_DEGREE + 1
-    channel_count = src_ref.shape[1]
-    num_edges = src_ref.shape[2]
+    channel_count = CHANNELS
+    num_edges = src_ref.shape[1]
     basis_count = basis_in_ref.shape[1]
     wig = wig_ref[...].astype(jnp.float32)
     gain = gain_ref[...]
 
-    rows = [src_ref[j].astype(jnp.float32) for j in range(src_ref.shape[0])]
+    turned = [src_ref[r].astype(jnp.float32).T for r in range(src_ref.shape[0])]
+    span_chan = CHANNELS // len(turned)
+    rows = [
+        jnp.concatenate([block[j * span_chan : (j + 1) * span_chan] for block in turned], axis=0)
+        for j in range(COEFFS)
+    ]
     normed = [None] * len(rows)
     for degree in range(levels):
         span = range(degree * degree, (degree + 1) ** 2)
@@ -269,7 +275,8 @@
 
 def convolve_edges(source, gain_cols, wig_mine, lengths, kind_onehot, radial_in, species_table, radial_out,
                    order_zero, order_one, order_two, onehot, proj_t):
-    coeffs, channel_count, num_edges = source.shape
+    coeffs, channel_count = COEFFS, CHANNELS
+    num_edges = source.shape[1]
     atom_count = onehot.shape[1]
     operands = (
         source,
@@ -333,8 +340,11 @@
     per_owner = edge_source.shape[0] // owners
     first_edge = quarter * per_owner
 
-    outgoing = node_feats[:, :, send_list]
-    arrived = lax.all_to_all(outgoing, "graph", split_axis=2, concat_axis=2, tiled=True)
+    row_width = 128 * pl.cdiv(coeffs * span_chan, 128)
+    node_rows = jnp.pad(
+        node_feats.reshape(coeffs * span_chan, atom_count).T, ((0, 0), (0, row_width - coeffs * span_chan))
+    )
+    arrived = lax.all_to_all(node_rows[send_list], "graph", 0, 0, tiled=True)
 
     packed = jnp.concatenate(
         [norm_gain, project_weight.astype(jnp.float32).reshape(levels, -1)], axis=1
@@ -347,9 +357,9 @@
         spread[:, :, span_chan:].reshape(owners, levels, CHANNELS, span_chan), (1, 2, 0, 3)
     ).reshape(levels, CHANNELS, owners * span_chan)
 
-    lookup = jnp.concatenate([node_feats, arrived], axis=2)
+    lookup = jnp.concatenate([node_rows, arrived], axis=0)
     source = lax.all_to_all(
-        lookup[:, :, edge_source], "irreps", split_axis=2, concat_axis=1, tiled=True
+        lookup[edge_source].reshape(owners, per_owner, row_width), "irreps", 0, 0, tiled=True
     )
     wig_mine = lax.dynamic_slice_in_dim(wigner, first_edge, per_owner, 1)
     targets_mine = lax.dynamic_slice_in_dim(edge_target, first_edge, per_owner)
@@ -373,9 +383,9 @@
     )
     projected = jnp.transpose(projected, (1, 0, 2))
     returned = lax.all_to_all(
-        projected.reshape(owners, span_chan, coeffs, atom_count), "irreps", 0, 0, tiled=True
-    )
-    total = jnp.transpose(jnp.sum(returned, axis=0), (1, 0, 2))
+        projected.reshape(owners, span_chan, coeffs, atom_count).astype(jnp.bfloat16), "irreps", 0, 0, tiled=True
+    )
+    total = jnp.transpose(jnp.sum(returned.astype(jnp.float32), axis=0), (1, 0, 2))
     return (node_feats.astype(jnp.float32) + total).astype(jnp.bfloat16)
 
 

time: 157 us -> 120 us (0.76)
  local copies, waits for them, and re-layouts: 66.1 us -> 33.5 us
  waiting for transfers between devices: 9.56 us -> 23.6 us
  blocking collectives: 26.7 us -> 17.8 us
  other arithmetic: 11.8 us -> 6.07 us
  starting transfers between devices: 29.2 us -> 25.8 us
    unnamed x40 -> x32, local copies, waits for them, and re-layouts: 43.1 us -> 15.9 us
    all_to_all x1, blocking collectives: 26.7 us -> 17.8 us  [body(): lax.all_to_all(projected.reshape(owners, span_chan, coeffs, atom_count).a...]
    all_to_all x1, waiting for transfers between devices: 0.01 us -> 8.27 us  [body(): lax.all_to_all(jnp.broadcast_to(packed[None], (owners,) + packed.shape),...]
    all_to_all x1 -> x0, other arithmetic: 6.03 us -> none  [body(): lax.all_to_all(projected.reshape(owners, span_chan, coeffs, atom_count),...]
    all_to_all x2, waiting for transfers between devices: 9.56 us -> 15.3 us  [the longest x1 9.24 us: body(): lax.all_to_all(lookup[edge_source].reshape(owners, per_owner, row_width),...]
    all_to_all x2, starting transfers between devices: 22.2 us -> 18.7 us  [the longest x1 14.9 us: body(): arrived = lax.all_to_all(node_rows[send_list], 'graph', 0, 0, tiled=True)]
    all_to_all x2 -> x1, local copies, waits for them, and re-layouts: 3.94 us -> 0.72 us  [body(): arrived = lax.all_to_all(node_rows[send_list], 'graph', 0, 0, tiled=True)]
    gather x2, local copies, waits for them, and re-layouts: 9.17 us -> 6.25 us  [the longest x1 5.1 us: body(): lookup[edge_source].reshape(owners, per_owner, row_width)]
  transfers between devices with their start and end apart: 3 -> 3, of which waited for: 2 -> 3; matrix products, arithmetic and copies ran while one was open for 25% -> 23% of each run, Pallas kernels for 0% -> 0%
where the time goes in v2:
time: 120 us; the launch traced here: 119 us
  local copies, waits for them, and re-layouts  33.5 us (28%)
  starting transfers between devices  25.8 us (22%)
  waiting for transfers between devices  23.6 us (20%)
  blocking collectives  17.8 us (15%)
  Pallas kernels  11.7 us (10%)
  other arithmetic  6.07 us (5%)
    all_to_all x1, blocking collectives, body(): lax.all_to_all(projected.reshape(owners, span_chan, coeffs, atom_count).a...  17.8 us
    unnamed x32, local copies, waits for them, and re-layouts  15.9 us
    all_to_all x1, starting transfers between devices, body(): arrived = lax.all_to_all(node_rows[send_list], 'graph', 0, 0, tiled=True)  14.9 us
    pallas_call x1, Pallas kernels, convolve_edges(): pl.pallas_call(conv_kernel, out_shape=jax.ShapeDtypeStruct((coeffs, chann...  11.7 us
    all_to_all x1, waiting for transfers between devices, body(): lax.all_to_all(lookup[edge_source].reshape(owners, per_owner, row_width),...  9.24 us
    all_to_all x1, waiting for transfers between devices, body(): lax.all_to_all(jnp.broadcast_to(packed[None], (owners,) + packed.shape),...  8.27 us
    all_to_all x1, starting transfers between devices, body(): lax.all_to_all(jnp.broadcast_to(packed[None], (owners,) + packed.shape),...  7.03 us
    all_to_all x1, waiting for transfers between devices, body(): arrived = lax.all_to_all(node_rows[send_list], 'graph', 0, 0, tiled=True)  6.05 us
  transfers between devices with their start and end apart: 3, of which 3 were waited for; matrix products, arithmetic and copies ran while one was open for 23% of the time, Pallas kernels for 0%

profile of v2, /device:TPU:64, one launch (start us, length us, event | category | flops | bytes accessed | tf_op | source)
XLA Modules:
  0.0 119.2 jit_solution(13342984048179934664)
XLA Ops:
  0.0 0.0 copy-start
  0.0 0.7 compare_select_fusion.1
  0.8 1.0 copy.35
  1.8 0.0 copy-start.8
  1.8 0.0 copy-start.7
  1.8 0.0 copy-start.6
  1.8 0.0 copy-start.9
  1.8 1.2 gather_fusion
  3.0 0.0 copy-start.4
  3.0 0.7 pad_bitcast_fusion
  3.7 14.9 %all-to-all-start = ((bf16[32,8,512]{2,1,0:T(8,128)(2,1)}), bf16[32,8,512]{2,1,0:T(8,128)(2,1)S(1)}, u32[]{:S(2)}, u32[]{:S(2)}) async-start(bf16[32,8,512]{2,1,0:T(8,128)(2,1)} %pad_bitcast_fusion), calls=%async_computation | async-start | bytes 524288 | tf_op jit(solution)/shard_map/all_to_all | solution.py:347
  19.3 0.0 copy-done.8
  19.3 0.7 copy.39
  20.0 0.0 copy-done.7
  20.0 0.8 copy.38
  20.8 0.0 copy-done.6
  20.8 0.8 copy.40
  21.6 0.0 copy-done.9
  21.6 0.1 copy.36
  21.7 0.2 reshape.38
  22.0 0.0 copy-done.4
  22.0 2.4 %copy.41 = bf16[896,896]{0,1:T(8,128)(2,1)} copy(bf16[896,896]{1,0:T(8,128)(2,1)S(1)} %copy-done.4) | data formatting | bytes 3211264 | tf_op args[12]
  24.3 0.0 copy-start.3
  24.3 3.7 %copy.43 = bf16[2,640,640]{1,2,0:T(8,128)(2,1)} copy(bf16[2,640,640]{2,1,0:T(8,128)(2,1)} %param.30) | data formatting | bytes 3276800 | tf_op args[14]
  28.1 0.0 copy-done.3
  28.1 0.0 copy-start.10
  28.1 2.5 %copy.42 = bf16[2,768,768]{1,2,0:T(8,128)(2,1)} copy(bf16[2,768,768]{2,1,0:T(8,128)(2,1)S(1)} %copy-done.3) | data formatting | bytes 4718592 | tf_op args[13]
  30.6 0.0 copy-start.1
  30.6 0.0 copy-start.11
  30.6 0.8 compare_select_fusion.2
  31.4 0.0 copy-done.10
  31.4 0.1 pad_maximum_fusion
  31.4 6.1 %all-to-all-done = bf16[32,8,512]{2,1,0:T(8,128)(2,1)S(1)} async-done(((bf16[32,8,512]{2,1,0:T(8,128)(2,1)}), bf16[32,8,512]{2,1,0:T(8,128)(2,1)S(1)}, u32[]{:S(2)}, u32[]{:S(2)}) %all-to-all-start) | async-done | bytes 262176 | tf_op jit(solution)/shard_map/all_to_all | solution.py:347
  37.5 0.9 broadcast_in_dim.45
  38.4 7.0 %all-to-all-start.2 = ((f32[16,7,1032]{2,1,0:T(8,128)}), f32[16,7,1032]{2,1,0:T(8,128)S(1)}, u32[]{:S(2)}, u32[]{:S(2)}) async-start(f32[16,7,1032]{2,1,0:T(8,128)} %broadcast_in_dim.45), calls=%async_computation.2 | async-start | bytes 1179648 | tf_op jit(solution)/shard_map/all_to_all | solution.py:352
  45.4 0.0 copy-done.1
  45.4 0.8 gather_fusion.2
  46.2 0.0 copy-done.11
  46.3 5.1 %gather_fusion.1 = bf16[1024,512]{1,0:T(8,128)(2,1)} fusion(bf16[320,512]{1,0:T(8,128)(2,1)S(1)} %fusion.1, s32[1024]{0:T(1024)S(1)} %fusion.4), kind=kCustom, calls=%fused_computation.1 | custom fusion | bytes 2101248 | tf_op jit(solution)/shard_map/gather | solution.py:362
  51.4 8.3 %all-to-all-done.2 = f32[16,7,1032]{2,1,0:T(8,128)S(1)} async-done(((f32[16,7,1032]{2,1,0:T(8,128)}), f32[16,7,1032]{2,1,0:T(8,128)S(1)}, u32[]{:S(2)}, u32[]{:S(2)}) %all-to-all-start.2) | async-done | bytes 462368 | tf_op jit(solution)/shard_map/all_to_all | solution.py:352
  59.6 3.8 %all-to-all-start.1 = ((bf16[16,64,512]{2,1,0:T(8,128)(2,1)}), bf16[16,64,512]{2,1,0:T(8,128)(2,1)S(1)}, u32[]{:S(2)}, u32[]{:S(2)}) async-start(bf16[16,64,512]{2,1,0:T(8,128)(2,1)} %bitcast.4), calls=%async_computation.1 | async-start | bytes 2097152 | tf_op jit(solution)/shard_map/all_to_all | solution.py:361
  63.5 1.3 %dynamic-slice_bitcast_fusion.length_ref = f32[1,64]{1,0:T(1,128)} fusion(f32[1024]{0:T(1024)} %param.23, s32[]{:T(128)S(6)} %select_n.28), kind=kLoop, calls=%fused_computation.25 | loop fusion | bytes 516 | tf_op jit(solution)/shard_map/broadcast_in_dim | solution.py:285
  64.8 0.0 copy-done
  64.8 0.7 constant_dynamic-slice_fusion.wig_ref
  65.5 0.7 select_convert_fusion.onehot_ref
  66.2 0.6 fusion.3.kind_ref
  66.8 0.8 copy.37
  67.6 0.9 slice.19
  68.5 1.8 %copy.44 = bf16[16,7,1024]{0,2,1:T(8,128)(2,1)S(1)} copy(bf16[16,7,1024]{2,1,0:T(8,128)(2,1)} %slice.19) | data formatting | bytes 458752 | tf_op jit(solution)/shard_map/slice | solution.py:357
  70.3 2.1 %copy.45 = bf16[7,128,16,8]{1,3,2,0:T(8,128)(2,1)} copy(bf16[7,128,16,8]{2,3,1,0:T(8,128)(2,1)S(1)} %bitcast.43) | data formatting | bytes 458752 | tf_op jit(solution)/shard_map/convert_element_type | solution.py:379
  72.3 9.2 %all-to-all-done.1.src_ref = bf16[16,64,512]{2,1,0:T(8,128)(2,1)S(1)} async-done(((bf16[16,64,512]{2,1,0:T(8,128)(2,1)}), bf16[16,64,512]{2,1,0:T(8,128)(2,1)S(1)}, u32[]{:S(2)}, u32[]{:S(2)}) %all-to-all-start.1) | async-done | bytes 1048608 | tf_op jit(solution)/shard_map/all_to_all | solution.py:361
  81.6 0.0 copy-start.2
  81.6 1.0 copy-done.2
  82.6 11.7 %shard_map.154 = f32[49,128,64]{2,1,0:T(8,128)} custom-call(bf16[16,64,512]{2,1,0:T(8,128)(2,1)} %copy-done.2, f32[128,7]{1,0:T(8,128)} %bitcast.51, bf16[235,64]{1,0:T(8,128)(2,1)} %constant_dynamic-slice_fusion.wig_ref, f32[1,64]{1,0:T(1,128)} %dynamic-slice_bitcast_fusion.length_ref, bf16[90,64]{1,0:T(8,128)(2,1)} %fusion.3.kind_ref, ...), custom_call_target="tpu_custom_call" | custom-call | flops 637534208 | bytes 8924032 | tf_op jit(solution)/shard_map/pallas_call | solution.py:297
  94.3 2.1 %copy_bitcast_fusion = bf16[16,49,8,64]{3,2,1,0:T(8,128)(2,1)S(1)} fusion(f32[49,128,64]{2,1,0:T(8,128)} %shard_map.154), kind=kLoop, calls=%fused_computation.27 | loop fusion | flops 401408 | bytes 2408448
  96.4 1.0 reshape.66
  97.4 17.8 %all_to_all.27 = bf16[16,2,12544]{2,1,0:T(2,128)(2,1)} all-to-all(bf16[16,2,12544]{2,1,0:T(2,128)(2,1)S(1)} %reshape.66), channel_id=1, replica_groups=mesh['graph'=32,'irreps'=16] {'irreps'}, dimensions={0} | all-to-all | bytes 1605632 | tf_op jit(solution)/shard_map/all_to_all | solution.py:385
  115.2 0.0 copy-start.5
  115.2 3.0 %reshape.67 = bf16[16,49,8,64]{3,2,1,0:T(8,128)(2,1)S(1)} reshape(bf16[16,2,12544]{2,1,0:T(2,128)(2,1)} %all_to_all.27) | data formatting | bytes 1605632
  118.2 0.3 convert_reduce_fusion
  118.5 0.0 copy-done.5
  118.5 0.7 fusion.2
  (6 shorter events, 0.1 us)
Async XLA Ops:
  0.0 64.8 %copy-start = (bf16[235,1024]{1,0:T(8,128)(2,1)S(1)}, bf16[235,1024]{1,0:T(8,128)(2,1)}, u32[]{:S(2)}) copy-start(bf16[235,1024]{1,0:T(8,128)(2,1)} %param.24) | copy-start | bytes 1443844
  1.8 17.5 %copy-start.8 = (bf16[90,128]{1,0:T(8,128)(2,1)S(1)}, bf16[90,128]{1,0:T(8,128)(2,1)}, u32[]{:S(2)}) copy-start(bf16[90,128]{1,0:T(8,128)(2,1)} %param.26) | copy-start | bytes 69124
  1.8 18.2 %copy-start.7 = (bf16[512,128]{1,0:T(8,128)(2,1)S(1)}, bf16[512,128]{1,0:T(8,128)(2,1)}, u32[]{:S(2)}) copy-start(bf16[512,128]{1,0:T(8,128)(2,1)} %param.25) | copy-start | bytes 393220
  1.8 19.0 %copy-start.6 = (bf16[128,896]{1,0:T(8,128)(2,1)S(1)}, bf16[128,896]{1,0:T(8,128)(2,1)}, u32[]{:S(2)}) copy-start(bf16[128,896]{1,0:T(8,128)(2,1)} %param.27) | copy-start | bytes 688132
  1.8 19.8 %copy-start.9 = (bf16[7,128,8]{1,2,0:T(8,128)(2,1)S(1)}, bf16[7,128,8]{1,2,0:T(8,128)(2,1)}, u32[]{:S(2)}) copy-start(bf16[7,128,8]{1,2,0:T(8,128)(2,1)} %param.31) | copy-start | bytes 43012
  3.0 19.0 %copy-start.4 = (bf16[896,896]{1,0:T(8,128)(2,1)S(1)}, bf16[896,896]{1,0:T(8,128)(2,1)}, u32[]{:S(2)}) copy-start(bf16[896,896]{1,0:T(8,128)(2,1)} %param.28) | copy-start | bytes 4816900
  3.7 33.8 %all-to-all-start = ((bf16[32,8,512]{2,1,0:T(8,128)(2,1)}), bf16[32,8,512]{2,1,0:T(8,128)(2,1)S(1)}, u32[]{:S(2)}, u32[]{:S(2)}) async-start(bf16[32,8,512]{2,1,0:T(8,128)(2,1)} %pad_bitcast_fusion), calls=%async_computation | async-start | bytes 524288 | tf_op jit(solution)/shard_map/all_to_all | solution.py:347
  24.3 3.7 %copy-start.3 = (bf16[2,768,768]{2,1,0:T(8,128)(2,1)S(1)}, bf16[2,768,768]{2,1,0:T(8,128)(2,1)}, u32[]{:S(2)}) copy-start(bf16[2,768,768]{2,1,0:T(8,128)(2,1)} %param.29) | copy-start | bytes 7077892
  28.1 3.3 %copy-start.10 = (f32[7,8]{1,0:T(8,128)S(1)}, f32[7,8]{1,0:T(8,128)}, u32[]{:S(2)}) copy-start(f32[7,8]{1,0:T(8,128)} %param.17) | copy-start | bytes 676
  30.6 14.9 %copy-start.1 = (s32[64]{0:T(128)S(1)}, s32[64]{0:T(128)}, u32[]{:S(2)}) copy-start(s32[64]{0:T(128)} %param.18) | copy-start | bytes 772
  30.6 15.6 %copy-start.11 = (s32[1024]{0:T(1024)S(1)}, s32[1024]{0:T(1024)}, u32[]{:S(2)}) copy-start(s32[1024]{0:T(1024)} %param.20) | copy-start | bytes 12292
  38.4 21.3 %all-to-all-start.2 = ((f32[16,7,1032]{2,1,0:T(8,128)}), f32[16,7,1032]{2,1,0:T(8,128)S(1)}, u32[]{:S(2)}, u32[]{:S(2)}) async-start(f32[16,7,1032]{2,1,0:T(8,128)} %broadcast_in_dim.45), calls=%async_computation.2 | async-start | bytes 1179648 | tf_op jit(solution)/shard_map/all_to_all | solution.py:352
  59.6 22.0 %all-to-all-start.1 = ((bf16[16,64,512]{2,1,0:T(8,128)(2,1)}), bf16[16,64,512]{2,1,0:T(8,128)(2,1)S(1)}, u32[]{:S(2)}, u32[]{:S(2)}) async-start(bf16[16,64,512]{2,1,0:T(8,128)(2,1)} %bitcast.4), calls=%async_computation.1 | async-start | bytes 2097152 | tf_op jit(solution)/shard_map/all_to_all | solution.py:361
  81.6 1.0 copy-start.2
  115.2 3.4 %copy-start.5 = (bf16[49,8,64]{2,1,0:T(8,128)(2,1)S(1)}, bf16[49,8,64]{2,1,0:T(8,128)(2,1)}, u32[]{:S(2)}) copy-start(bf16[49,8,64]{2,1,0:T(8,128)(2,1)} %param.16) | copy-start | bytes 150532

commit v3 on v2

--- a/solution.py
+++ b/solution.py
@@ -340,27 +340,40 @@
     per_owner = edge_source.shape[0] // owners
     first_edge = quarter * per_owner
 
-    row_width = 128 * pl.cdiv(coeffs * span_chan, 128)
-    node_rows = jnp.pad(
-        node_feats.reshape(coeffs * span_chan, atom_count).T, ((0, 0), (0, row_width - coeffs * span_chan))
-    )
+    row_used = coeffs * span_chan
+    row_width = 128 * pl.cdiv(row_used, 128)
+    node_rows = node_feats.reshape(row_used, atom_count).T
     arrived = lax.all_to_all(node_rows[send_list], "graph", 0, 0, tiled=True)
 
-    packed = jnp.concatenate(
-        [norm_gain, project_weight.astype(jnp.float32).reshape(levels, -1)], axis=1
-    )
-    spread = lax.all_to_all(
-        jnp.broadcast_to(packed[None], (owners,) + packed.shape), "irreps", 0, 0, tiled=True
-    )
-    gain_full = jnp.transpose(spread[:, :, :span_chan], (1, 0, 2)).reshape(levels, owners * span_chan)
-    weight_full = jnp.transpose(
-        spread[:, :, span_chan:].reshape(owners, levels, CHANNELS, span_chan), (1, 2, 0, 3)
-    ).reshape(levels, CHANNELS, owners * span_chan)
+    gain_high = norm_gain.astype(jnp.bfloat16)
+    gain_rest = norm_gain - gain_high.astype(jnp.float32)
+    gain_mid = gain_rest.astype(jnp.bfloat16)
+    gain_low = (gain_rest - gain_mid.astype(jnp.float32)).astype(jnp.bfloat16)
+    extra = jnp.concatenate(
+        [project_weight.reshape(-1), gain_high.reshape(-1), gain_mid.reshape(-1), gain_low.reshape(-1)]
+    )
+    extra_len = extra.shape[0]
+    spare = per_owner * (row_width - row_used)
+    extra = jnp.pad(extra, (0, spare - extra_len)).reshape(per_owner, row_width - row_used)
 
     lookup = jnp.concatenate([node_rows, arrived], axis=0)
-    source = lax.all_to_all(
-        lookup[edge_source].reshape(owners, per_owner, row_width), "irreps", 0, 0, tiled=True
-    )
+    outgoing = jnp.concatenate(
+        [
+            lookup[edge_source].reshape(owners, per_owner, row_used),
+            jnp.broadcast_to(extra[None], (owners,) + extra.shape),
+        ],
+        axis=2,
+    )
+    source = lax.all_to_all(outgoing, "irreps", 0, 0, tiled=True)
+    carried = source[:, :, row_used:].reshape(owners, -1)[:, :extra_len]
+    weight_len = project_weight.size
+    proj_t = jnp.transpose(
+        carried[:, :weight_len].reshape(owners, levels, CHANNELS, span_chan), (1, 0, 3, 2)
+    ).reshape(levels, owners * span_chan, CHANNELS)
+    gain_parts = carried[:, weight_len:].astype(jnp.float32).reshape(owners, 3, levels, span_chan)
+    gain_sum = gain_parts[:, 0] + gain_parts[:, 1] + gain_parts[:, 2]
+    gain_cols = jnp.transpose(gain_sum, (0, 2, 1)).reshape(owners * span_chan, levels)
+
     wig_mine = lax.dynamic_slice_in_dim(wigner, first_edge, per_owner, 1)
     targets_mine = lax.dynamic_slice_in_dim(edge_target, first_edge, per_owner)
     lengths_mine = lax.dynamic_slice_in_dim(edge_length, first_edge, per_owner)
@@ -376,9 +389,8 @@
         edge_weight[:, None],
         0.0,
     ).astype(jnp.bfloat16)
-    proj_t = jnp.transpose(weight_full, (0, 2, 1)).astype(jnp.bfloat16)
     projected = convolve_edges(
-        source, gain_full.T, wig_mine, lengths_mine, kind_onehot, radial_in, species_table, radial_out,
+        source, gain_cols, wig_mine, lengths_mine, kind_onehot, radial_in, species_table, radial_out,
         order_zero, order_one, order_two, onehot, proj_t,
     )
     projected = jnp.transpose(projected, (1, 0, 2))

time: 120 us -> 117 us (0.975)
  starting transfers between devices: 25.8 us -> 21.9 us
    all_to_all x2 -> x1, starting transfers between devices: 10.9 us -> 7.04 us  [body(): source = lax.all_to_all(outgoing, 'irreps', 0, 0, tiled=True)]
    transpose x2, local copies, waits for them, and re-layouts: 0.8 us -> 3.82 us  [the longest x1 3.07 us: body(): jnp.transpose(carried[:, :weight_len].reshape(owners, levels, CHANNELS, s...]
    convert_element_type x1 -> x0, local copies, waits for them, and re-layouts: 2.08 us -> none  [body(): proj_t = jnp.transpose(weight_full, (0, 2, 1)).astype(jnp.bfloat16)]
    reshape x3 -> x6, local copies, waits for them, and re-layouts: 1.39 us -> 3.33 us  [the longest x1 1.84 us: body(): carried = source[:, :, row_used:].reshape(owners, -1)[:, :extra_len]]
    all_to_all x2 -> x1, waiting for transfers between devices: 17.5 us -> 16.1 us  [body(): source = lax.all_to_all(outgoing, 'irreps', 0, 0, tiled=True)]
    unnamed x32 -> x33, local copies, waits for them, and re-layouts: 15.9 us -> 15.1 us
    slice x2 -> x3, local copies, waits for them, and re-layouts: 2.67 us -> 2.45 us  [the longest x1 1.39 us: body(): carried[:, :weight_len].reshape(owners, levels, CHANNELS, span_chan)]
  transfers between devices with their start and end apart: 3 -> 2, of which waited for: 3 -> 2; matrix products, arithmetic and copies ran while one was open for 23% -> 14% of each run, Pallas kernels for 0% -> 0%
where the time goes in v3:
time: 117 us; the launch traced here: 116 us
  local copies, waits for them, and re-layouts  33.6 us (29%)
  waiting for transfers between devices  22.5 us (19%)
  starting transfers between devices  21.9 us (19%)
  blocking collectives  18.4 us (16%)
  Pallas kernels  11.7 us (10%)
  other arithmetic  7.19 us (6%)
    all_to_all x1, blocking collectives, body(): lax.all_to_all(projected.reshape(owners, span_chan, coeffs, atom_count).a...  18.4 us
    all_to_all x1, waiting for transfers between devices, body(): source = lax.all_to_all(outgoing, 'irreps', 0, 0, tiled=True)  16.1 us
    unnamed x33, local copies, waits for them, and re-layouts  15.1 us
    all_to_all x1, starting transfers between devices, body(): arrived = lax.all_to_all(node_rows[send_list], 'graph', 0, 0, tiled=True)  14.9 us
    pallas_call x1, Pallas kernels, convolve_edges(): pl.pallas_call(conv_kernel, out_shape=jax.ShapeDtypeStruct((coeffs, chann...  11.7 us
    all_to_all x1, starting transfers between devices, body(): source = lax.all_to_all(outgoing, 'irreps', 0, 0, tiled=True)  7.04 us
    all_to_all x1, waiting for transfers between devices, body(): arrived = lax.all_to_all(node_rows[send_list], 'graph', 0, 0, tiled=True)  6.44 us
    gather x1, local copies, waits for them, and re-layouts, body(): lookup[edge_source].reshape(owners, per_owner, row_used)  3.97 us
  transfers between devices with their start and end apart: 2, of which 2 were waited for; matrix products, arithmetic and copies ran while one was open for 14% of the time, Pallas kernels for 0%

profile of v3, /device:TPU:64, one launch (start us, length us, event | category | flops | bytes accessed | tf_op | source)
XLA Modules:
  0.0 116.1 jit_solution(18078662909070157838)
XLA Ops:
  0.0 0.0 copy-start
  0.0 0.0 copy-start.10
  0.0 0.0 copy-start.8
  0.0 0.0 copy-start.7
  0.0 0.0 copy-start.6
  0.0 0.8 compare_select_fusion.1
  0.8 1.0 copy.36
  1.8 0.0 copy-start.9
  1.8 0.0 copy-start.4
  1.8 1.9 %gather_fusion = bf16[256,392]{1,0:T(8,128)(2,1)} fusion(bf16[64,392]{1,0:T(8,128)(2,1)S(1)} %bitcast.40, s32[1024]{0:T(1024)S(1)} %pad_clamp_fusion.1), kind=kCustom, calls=%fused_computation | custom fusion | bytes 402432 | tf_op jit(solution)/shard_map/gather | solution.py:346
  3.7 14.9 %all-to-all-start = ((bf16[32,8,392]{2,1,0:T(8,128)(2,1)}), bf16[32,8,392]{2,1,0:T(8,128)(2,1)S(1)}, u32[]{:S(2)}, u32[]{:S(2)}) async-start(bf16[32,8,392]{2,1,0:T(8,128)(2,1)} %bitcast.2), calls=%async_computation | async-start | bytes 524288 | tf_op jit(solution)/shard_map/all_to_all | solution.py:346
  19.2 0.0 copy-done.10
  19.3 0.1 reshape.56
  19.4 0.1 reshape.55
  19.4 0.1 reshape.54
  19.5 0.0 copy-done.8
  19.5 0.7 copy.41
  20.2 0.0 copy-done.7
  20.3 0.8 copy.40
  21.0 0.0 copy-done.6
  21.0 0.8 copy.42
  21.8 0.0 copy-done.9
  21.9 0.2 copy.37
  22.0 0.2 reshape.53
  22.3 0.1 concatenate.10
  22.4 0.1 broadcast_in_dim.46
  22.5 0.0 copy-done.4
  22.5 2.3 %copy.43 = bf16[896,896]{0,1:T(8,128)(2,1)} copy(bf16[896,896]{1,0:T(8,128)(2,1)S(1)} %copy-done.4) | data formatting | bytes 3211264 | tf_op args[12]
  24.8 0.0 copy-start.3
  24.8 3.7 %copy.45 = bf16[2,640,640]{1,2,0:T(8,128)(2,1)} copy(bf16[2,640,640]{2,1,0:T(8,128)(2,1)} %param.30) | data formatting | bytes 3276800 | tf_op args[14]
  28.5 0.0 copy-done.3
  28.5 0.0 copy-start.11
  28.5 2.5 %copy.44 = bf16[2,768,768]{1,2,0:T(8,128)(2,1)} copy(bf16[2,768,768]{2,1,0:T(8,128)(2,1)S(1)} %copy-done.3) | data formatting | bytes 4718592 | tf_op args[13]
  31.0 0.0 copy-done.11
  31.0 6.4 %all-to-all-done = bf16[32,8,392]{2,1,0:T(8,128)(2,1)S(1)} async-done(((bf16[32,8,392]{2,1,0:T(8,128)(2,1)}), bf16[32,8,392]{2,1,0:T(8,128)(2,1)S(1)}, u32[]{:S(2)}, u32[]{:S(2)}) %all-to-all-start) | async-done | bytes 200736 | tf_op jit(solution)/shard_map/all_to_all | solution.py:346
  37.5 4.0 %gather_fusion.1 = bf16[1024,392]{1,0:T(8,128)(2,1)S(1)} fusion(bf16[320,392]{1,0:T(8,128)(2,1)S(1)} %pad_maximum_fusion.1, s32[1024]{0:T(1024)S(1)} %fusion.3), kind=kCustom, calls=%fused_computation.1 | custom fusion | bytes 1609728 | tf_op jit(solution)/shard_map/gather | solution.py:362
  41.5 0.0 copy-start.1
  41.5 1.2 %pad_maximum_fusion = bf16[16,64,512]{2,1,0:T(8,128)(2,1)} fusion(bf16[16,64,120]{2,1,0:T(8,128)(2,1)S(1)} %broadcast_in_dim.47, bf16[16,64,392]{2,1,0:T(8,128)(2,1)S(1)} %bitcast.48), kind=kLoop, calls=%fused_computation.5 | loop fusion | flops 2097152 | bytes 2097152 | tf_op jit(solution)/shard_map/concatenate | solution.py:360
  42.7 7.0 %all-to-all-start.1 = ((bf16[16,64,512]{2,1,0:T(8,128)(2,1)}), bf16[16,64,512]{2,1,0:T(8,128)(2,1)S(1)}, u32[]{:S(2)}, u32[]{:S(2)}) async-start(bf16[16,64,512]{2,1,0:T(8,128)(2,1)} %pad_maximum_fusion), calls=%async_computation.1 | async-start | bytes 2097152 | tf_op jit(solution)/shard_map/all_to_all | solution.py:367
  49.8 0.8 compare_select_fusion.2
  50.6 0.0 copy-done.1
  50.6 0.8 gather_fusion.2
  51.3 1.3 %dynamic-slice_bitcast_fusion.length_ref = f32[1,64]{1,0:T(1,128)} fusion(f32[1024]{0:T(1024)} %param.23, s32[]{:T(128)S(6)} %select_n.28), kind=kLoop, calls=%fused_computation.26 | loop fusion | bytes 516 | tf_op jit(solution)/shard_map/broadcast_in_dim | solution.py:285
  52.7 0.0 copy-done
  52.7 0.7 constant_dynamic-slice_fusion.wig_ref
  53.4 0.7 select_convert_fusion.onehot_ref
  54.1 0.6 fusion.1.kind_ref
  54.7 16.1 %all-to-all-done.1.src_ref = bf16[16,64,512]{2,1,0:T(8,128)(2,1)S(1)} async-done(((bf16[16,64,512]{2,1,0:T(8,128)(2,1)}), bf16[16,64,512]{2,1,0:T(8,128)(2,1)S(1)}, u32[]{:S(2)}, u32[]{:S(2)}) %all-to-all-start.1) | async-done | bytes 1048608 | tf_op jit(solution)/shard_map/all_to_all | solution.py:367
  70.7 0.0 copy-start.2
  70.7 1.0 slice.33
  71.8 1.8 %copy.49 = bf16[16,64,120]{0,2,1:T(8,128)(2,1)S(1)} copy(bf16[16,64,120]{2,1,0:T(8,128)(2,1)} %slice.33) | data formatting | bytes 491520 | tf_op jit(solution)/shard_map/reshape | solution.py:368
  73.6 1.4 %slice.38 = bf16[16,7168]{0,1:T(8,128)(2,1)} slice(bf16[16,7680]{0,1:T(8,128)(2,1)S(1)} %bitcast.44), slice={[0:16], [0:7168]} | slice | bytes 458752 | tf_op jit(solution)/shard_map/slice | solution.py:371
  75.0 0.0 copy-done.2
  75.0 3.1 %copy.47 = bf16[7,16,8,128]{3,2,1,0:T(8,128)(2,1)} copy(bf16[7,16,8,128]{1,2,3,0:T(8,128)(2,1)} %bitcast.45) | data formatting | bytes 458752 | tf_op jit(solution)/shard_map/transpose | solution.py:370
  78.1 0.8 copy.39
  78.9 11.7 %shard_map.154 = f32[49,128,64]{2,1,0:T(8,128)} custom-call(bf16[16,64,512]{2,1,0:T(8,128)(2,1)} %copy-done.2, f32[128,7]{1,0:T(8,128)} %bitcast.54, bf16[235,64]{1,0:T(8,128)(2,1)} %constant_dynamic-slice_fusion.wig_ref, f32[1,64]{1,0:T(1,128)} %dynamic-slice_bitcast_fusion.length_ref, bf16[90,64]{1,0:T(8,128)(2,1)} %fusion.1.kind_ref, ...), custom_call_target="tpu_custom_call" | custom-call | flops 637534208 | bytes 8924032 | tf_op jit(solution)/shard_map/pallas_call | solution.py:297
  90.6 2.1 %copy_bitcast_fusion = bf16[16,49,8,64]{3,2,1,0:T(8,128)(2,1)S(1)} fusion(f32[49,128,64]{2,1,0:T(8,128)} %shard_map.154), kind=kLoop, calls=%fused_computation.28 | loop fusion | flops 401408 | bytes 2408448
  92.7 1.0 reshape.92
  93.7 18.4 %all_to_all.22 = bf16[16,2,12544]{2,1,0:T(2,128)(2,1)} all-to-all(bf16[16,2,12544]{2,1,0:T(2,128)(2,1)S(1)} %reshape.92), channel_id=1, replica_groups=mesh['graph'=32,'irreps'=16] {'irreps'}, dimensions={0} | all-to-all | bytes 1605632 | tf_op jit(solution)/shard_map/all_to_all | solution.py:397
  112.1 0.0 copy-start.5
  112.1 3.0 %reshape.93 = bf16[16,49,8,64]{3,2,1,0:T(8,128)(2,1)S(1)} reshape(bf16[16,2,12544]{2,1,0:T(2,128)(2,1)} %all_to_all.22) | data formatting | bytes 1605632
  115.1 0.3 convert_reduce_fusion
  115.5 0.0 copy-done.5
  115.5 0.7 fusion
  (11 shorter events, 0.1 us)
Async XLA Ops:
  0.0 52.7 %copy-start = (bf16[235,1024]{1,0:T(8,128)(2,1)S(1)}, bf16[235,1024]{1,0:T(8,128)(2,1)}, u32[]{:S(2)}) copy-start(bf16[235,1024]{1,0:T(8,128)(2,1)} %param.24) | copy-start | bytes 1443844
  0.0 19.2 %copy-start.10 = (f32[7,8]{1,0:T(8,128)S(1)}, f32[7,8]{1,0:T(8,128)}, u32[]{:S(2)}) copy-start(f32[7,8]{1,0:T(8,128)} %param.17) | copy-start | bytes 676
  0.0 19.5 %copy-start.8 = (bf16[90,128]{1,0:T(8,128)(2,1)S(1)}, bf16[90,128]{1,0:T(8,128)(2,1)}, u32[]{:S(2)}) copy-start(bf16[90,128]{1,0:T(8,128)(2,1)} %param.26) | copy-start | bytes 69124
  0.0 20.2 %copy-start.7 = (bf16[512,128]{1,0:T(8,128)(2,1)S(1)}, bf16[512,128]{1,0:T(8,128)(2,1)}, u32[]{:S(2)}) copy-start(bf16[512,128]{1,0:T(8,128)(2,1)} %param.25) | copy-start | bytes 393220
  0.0 21.0 %copy-start.6 = (bf16[128,896]{1,0:T(8,128)(2,1)S(1)}, bf16[128,896]{1,0:T(8,128)(2,1)}, u32[]{:S(2)}) copy-start(bf16[128,896]{1,0:T(8,128)(2,1)} %param.27) | copy-start | bytes 688132
  1.8 20.0 %copy-start.9 = (bf16[7,128,8]{1,2,0:T(8,128)(2,1)S(1)}, bf16[7,128,8]{1,2,0:T(8,128)(2,1)}, u32[]{:S(2)}) copy-start(bf16[7,128,8]{1,2,0:T(8,128)(2,1)} %param.31) | copy-start | bytes 43012
  1.8 20.7 %copy-start.4 = (bf16[896,896]{1,0:T(8,128)(2,1)S(1)}, bf16[896,896]{1,0:T(8,128)(2,1)}, u32[]{:S(2)}) copy-start(bf16[896,896]{1,0:T(8,128)(2,1)} %param.28) | copy-start | bytes 4816900
  3.7 33.8 %all-to-all-start = ((bf16[32,8,392]{2,1,0:T(8,128)(2,1)}), bf16[32,8,392]{2,1,0:T(8,128)(2,1)S(1)}, u32[]{:S(2)}, u32[]{:S(2)}) async-start(bf16[32,8,392]{2,1,0:T(8,128)(2,1)} %bitcast.2), calls=%async_computation | async-start | bytes 524288 | tf_op jit(solution)/shard_map/all_to_all | solution.py:346
  24.8 3.7 %copy-start.3 = (bf16[2,768,768]{2,1,0:T(8,128)(2,1)S(1)}, bf16[2,768,768]{2,1,0:T(8,128)(2,1)}, u32[]{:S(2)}) copy-start(bf16[2,768,768]{2,1,0:T(8,128)(2,1)} %param.29) | copy-start | bytes 7077892
  28.5 2.5 %copy-start.11 = (s32[1024]{0:T(1024)S(1)}, s32[1024]{0:T(1024)}, u32[]{:S(2)}) copy-start(s32[1024]{0:T(1024)} %param.20) | copy-start | bytes 12292
  41.5 9.0 %copy-start.1 = (s32[64]{0:T(128)S(1)}, s32[64]{0:T(128)}, u32[]{:S(2)}) copy-start(s32[64]{0:T(128)} %param.18) | copy-start | bytes 772
  42.7 28.0 %all-to-all-start.1 = ((bf16[16,64,512]{2,1,0:T(8,128)(2,1)}), bf16[16,64,512]{2,1,0:T(8,128)(2,1)S(1)}, u32[]{:S(2)}, u32[]{:S(2)}) async-start(bf16[16,64,512]{2,1,0:T(8,128)(2,1)} %pad_maximum_fusion), calls=%async_computation.1 | async-start | bytes 2097152 | tf_op jit(solution)/shard_map/all_to_all | solution.py:367
  70.7 4.3 %copy-start.2 = (bf16[16,64,512]{2,1,0:T(8,128)(2,1)}, bf16[16,64,512]{2,1,0:T(8,128)(2,1)S(1)}, u32[]{:S(2)}) copy-start(bf16[16,64,512]{2,1,0:T(8,128)(2,1)S(1)} %all-to-all-done.1.src_ref) | copy-start | bytes 3145732
  112.1 3.4 %copy-start.5 = (bf16[49,8,64]{2,1,0:T(8,128)(2,1)S(1)}, bf16[49,8,64]{2,1,0:T(8,128)(2,1)}, u32[]{:S(2)}) copy-start(bf16[49,8,64]{2,1,0:T(8,128)(2,1)} %param.16) | copy-start | bytes 150532

commit v4 on v2

--- a/solution.py
+++ b/solution.py
@@ -159,18 +159,48 @@
 
 
 def conv_kernel(
-    src_ref, gain_ref, wig_ref, length_ref, kind_ref, basis_in_ref, kind_table_ref, radial_out_ref,
-    zero_ref, one_ref, two_ref, onehot_ref, proj_ref, out_ref,
+    src_ref, wig_ref, length_ref, kind_ref, basis_in_ref, kind_table_ref, radial_out_ref,
+    zero_ref, one_ref, two_ref, onehot_ref, out_ref,
 ):
     levels = MAX_DEGREE + 1
     channel_count = CHANNELS
-    num_edges = src_ref.shape[1]
+    num_edges = onehot_ref.shape[0]
     basis_count = basis_in_ref.shape[1]
     wig = wig_ref[...].astype(jnp.float32)
-    gain = gain_ref[...]
-
-    turned = [src_ref[r].astype(jnp.float32).T for r in range(src_ref.shape[0])]
-    span_chan = CHANNELS // len(turned)
+    owners = src_ref.shape[0]
+    span_chan = CHANNELS // owners
+    pick = (
+        lax.broadcasted_iota(jnp.int32, (CHANNELS, span_chan), 0) % span_chan
+        == lax.broadcasted_iota(jnp.int32, (CHANNELS, span_chan), 1)
+    ) & (lax.broadcasted_iota(jnp.int32, (CHANNELS, span_chan), 0) < 3 * span_chan)
+    pick = pick.astype(jnp.bfloat16)
+    gain = jnp.concatenate(
+        [
+            jnp.dot(
+                src_ref[r, num_edges + span_chan : num_edges + 2 * span_chan, 3 * CHANNELS : 4 * CHANNELS],
+                pick,
+                preferred_element_type=jnp.float32,
+            )
+            for r in range(owners)
+        ],
+        axis=0,
+    )
+    projection = [
+        jnp.concatenate(
+            [
+                src_ref[
+                    r,
+                    num_edges + (degree // 4) * span_chan : num_edges + (degree // 4 + 1) * span_chan,
+                    (degree % 4) * CHANNELS : (degree % 4 + 1) * CHANNELS,
+                ].astype(jnp.float32)
+                for r in range(owners)
+            ],
+            axis=0,
+        ).astype(jnp.bfloat16)
+        for degree in range(levels)
+    ]
+
+    turned = [src_ref[r, 0:num_edges].astype(jnp.float32).T for r in range(owners)]
     rows = [
         jnp.concatenate([block[j * span_chan : (j + 1) * span_chan] for block in turned], axis=0)
         for j in range(COEFFS)
@@ -263,7 +293,7 @@
         lower_part, onehot, preferred_element_type=jnp.float32
     )
     for degree in range(levels):
-        weight = proj_ref[degree]
+        weight = projection[degree]
         for j in range(degree * degree, (degree + 1) ** 2):
             piece = summed[j * channel_count : (j + 1) * channel_count]
             high = piece.astype(jnp.bfloat16)
@@ -273,14 +303,13 @@
             )
 
 
-def convolve_edges(source, gain_cols, wig_mine, lengths, kind_onehot, radial_in, species_table, radial_out,
-                   order_zero, order_one, order_two, onehot, proj_t):
+def convolve_edges(source, wig_mine, lengths, kind_onehot, radial_in, species_table, radial_out,
+                   order_zero, order_one, order_two, onehot, per_owner):
     coeffs, channel_count = COEFFS, CHANNELS
-    num_edges = source.shape[1]
+    num_edges = per_owner
     atom_count = onehot.shape[1]
     operands = (
         source,
-        gain_cols,
         wig_mine,
         lengths[None, :],
         kind_onehot,
@@ -291,7 +320,6 @@
         jnp.transpose(order_one, (0, 2, 1)),
         jnp.transpose(order_two, (0, 2, 1)),
         onehot,
-        proj_t,
     )
     flops = 2 * num_edges * (order_zero.size + 2 * order_one.size + 2 * order_two.size + radial_out.size + radial_in.size)
     return pl.pallas_call(
@@ -340,27 +368,32 @@
     per_owner = edge_source.shape[0] // owners
     first_edge = quarter * per_owner
 
-    row_width = 128 * pl.cdiv(coeffs * span_chan, 128)
-    node_rows = jnp.pad(
-        node_feats.reshape(coeffs * span_chan, atom_count).T, ((0, 0), (0, row_width - coeffs * span_chan))
-    )
+    row_used = coeffs * span_chan
+    row_width = 128 * pl.cdiv(row_used, 128)
+    node_rows = node_feats.reshape(row_used, atom_count).T
     arrived = lax.all_to_all(node_rows[send_list], "graph", 0, 0, tiled=True)
 
-    packed = jnp.concatenate(
-        [norm_gain, project_weight.astype(jnp.float32).reshape(levels, -1)], axis=1
-    )
-    spread = lax.all_to_all(
-        jnp.broadcast_to(packed[None], (owners,) + packed.shape), "irreps", 0, 0, tiled=True
-    )
-    gain_full = jnp.transpose(spread[:, :, :span_chan], (1, 0, 2)).reshape(levels, owners * span_chan)
-    weight_full = jnp.transpose(
-        spread[:, :, span_chan:].reshape(owners, levels, CHANNELS, span_chan), (1, 2, 0, 3)
-    ).reshape(levels, CHANNELS, owners * span_chan)
+    gain_high = lax.reduce_precision(norm_gain, exponent_bits=8, mantissa_bits=7)
+    gain_rest = norm_gain - gain_high
+    gain_mid = lax.reduce_precision(gain_rest, exponent_bits=8, mantissa_bits=7)
+    gain_low = gain_rest - gain_mid
+    gain_block = jnp.transpose(jnp.stack([gain_high, gain_mid, gain_low]), (2, 0, 1))
+    gain_block = jnp.pad(gain_block, ((0, 0), (0, 0), (0, 1))).reshape(span_chan, 3 * (levels + 1))
+    gain_block = jnp.pad(gain_block, ((0, 0), (0, CHANNELS - gain_block.shape[1]))).astype(jnp.bfloat16)
+    weight_block = jnp.concatenate(
+        [jnp.transpose(project_weight, (2, 0, 1)), gain_block[:, None, :]], axis=1
+    )
+    extra = jnp.transpose(weight_block.reshape(span_chan, 2, 4, CHANNELS), (1, 0, 2, 3)).reshape(
+        2 * span_chan, 4 * CHANNELS
+    )
 
     lookup = jnp.concatenate([node_rows, arrived], axis=0)
-    source = lax.all_to_all(
-        lookup[edge_source].reshape(owners, per_owner, row_width), "irreps", 0, 0, tiled=True
-    )
+    gathered = jnp.pad(
+        lookup[edge_source].reshape(owners, per_owner, row_used), ((0, 0), (0, 0), (0, row_width - row_used))
+    )
+    outgoing = jnp.concatenate([gathered, jnp.broadcast_to(extra[None], (owners,) + extra.shape)], axis=1)
+    source = lax.all_to_all(outgoing, "irreps", 0, 0, tiled=True)
+
     wig_mine = lax.dynamic_slice_in_dim(wigner, first_edge, per_owner, 1)
     targets_mine = lax.dynamic_slice_in_dim(edge_target, first_edge, per_owner)
     lengths_mine = lax.dynamic_slice_in_dim(edge_length, first_edge, per_owner)
@@ -376,10 +409,9 @@
         edge_weight[:, None],
         0.0,
     ).astype(jnp.bfloat16)
-    proj_t = jnp.transpose(weight_full, (0, 2, 1)).astype(jnp.bfloat16)
     projected = convolve_edges(
-        source, gain_full.T, wig_mine, lengths_mine, kind_onehot, radial_in, species_table, radial_out,
-        order_zero, order_one, order_two, onehot, proj_t,
+        source, wig_mine, lengths_mine, kind_onehot, radial_in, species_table, radial_out,
+        order_zero, order_one, order_two, onehot, per_owner,
     )
     projected = jnp.transpose(projected, (1, 0, 2))
     returned = lax.all_to_all(

time: 120 us -> 113 us (0.942)
  local copies, waits for them, and re-layouts: 33.5 us -> 27.4 us
  starting transfers between devices: 25.8 us -> 22.1 us
  waiting for transfers between devices: 23.6 us -> 25.1 us
    all_to_all x1, waiting for transfers between devices: 6.05 us -> 18.7 us  [body(): arrived = lax.all_to_all(node_rows[send_list], 'graph', 0, 0, tiled=True)]
    all_to_all x2 -> x1, waiting for transfers between devices: 17.5 us -> 6.42 us  [body(): source = lax.all_to_all(outgoing, 'irreps', 0, 0, tiled=True)]
    all_to_all x2 -> x1, starting transfers between devices: 10.9 us -> 7.17 us  [body(): source = lax.all_to_all(outgoing, 'irreps', 0, 0, tiled=True)]
    slice x2 -> x0, local copies, waits for them, and re-layouts: 2.67 us -> none  [body(): spread[:, :, span_chan:].reshape(owners, levels, CHANNELS, span_chan)]
    convert_element_type x1 -> x0, local copies, waits for them, and re-layouts: 2.08 us -> none  [body(): proj_t = jnp.transpose(weight_full, (0, 2, 1)).astype(jnp.bfloat16)]
    unnamed x32 -> x30, local copies, waits for them, and re-layouts: 15.9 us -> 17.7 us
  transfers between devices with their start and end apart: 3 -> 2, of which waited for: 3 -> 2; matrix products, arithmetic and copies ran while one was open for 23% -> 16% of each run, Pallas kernels for 0% -> 0%
where the time goes in v4:
time: 113 us
  local copies, waits for them, and re-layouts  27.4 us (24%)
  waiting for transfers between devices  25.1 us (22%)
  starting transfers between devices  22.1 us (20%)
  blocking collectives  18.4 us (16%)
  Pallas kernels  11.7 us (10%)
  other arithmetic  7.25 us (6%)
    all_to_all x1, waiting for transfers between devices, body(): arrived = lax.all_to_all(node_rows[send_list], 'graph', 0, 0, tiled=True)  18.7 us
    all_to_all x1, blocking collectives, body(): lax.all_to_all(projected.reshape(owners, span_chan, coeffs, atom_count).a...  18.4 us
    unnamed x30, local copies, waits for them, and re-layouts  17.7 us
    all_to_all x1, starting transfers between devices, body(): arrived = lax.all_to_all(node_rows[send_list], 'graph', 0, 0, tiled=True)  14.9 us
    pallas_call x1, Pallas kernels, convolve_edges(): pl.pallas_call(conv_kernel, out_shape=jax.ShapeDtypeStruct((coeffs, chann...  11.7 us
    all_to_all x1, starting transfers between devices, body(): source = lax.all_to_all(outgoing, 'irreps', 0, 0, tiled=True)  7.17 us
    all_to_all x1, waiting for transfers between devices, body(): source = lax.all_to_all(outgoing, 'irreps', 0, 0, tiled=True)  6.42 us
    gather x1, local copies, waits for them, and re-layouts, body(): lookup[edge_source].reshape(owners, per_owner, row_used)  3.97 us
  transfers between devices with their start and end apart: 2, of which 2 were waited for; matrix products, arithmetic and copies ran while one was open for 16% of the time, Pallas kernels for 0%

profile of v4, /device:TPU:64, one launch (start us, length us, event | category | flops | bytes accessed | tf_op | source)
XLA Modules:
  0.0 112.7 jit_solution(8176313376409439846)
XLA Ops:
  0.0 0.0 copy-start
  0.0 0.0 copy-start.9
  0.0 0.0 copy-start.8
  0.0 0.0 copy-start.10
  0.0 0.7 compare_select_fusion.1
  0.8 1.0 copy.33
  1.8 1.9 %gather_fusion = bf16[256,392]{1,0:T(8,128)(2,1)} fusion(bf16[64,392]{1,0:T(8,128)(2,1)S(1)} %bitcast.46, s32[1024]{0:T(1024)S(1)} %pad_clamp_fusion.1), kind=kCustom, calls=%fused_computation | custom fusion | bytes 402432 | tf_op jit(solution)/shard_map/gather | solution.py:374
  3.6 14.9 %all-to-all-start = ((bf16[32,8,392]{2,1,0:T(8,128)(2,1)}), bf16[32,8,392]{2,1,0:T(8,128)(2,1)S(1)}, u32[]{:S(2)}, u32[]{:S(2)}) async-start(bf16[32,8,392]{2,1,0:T(8,128)(2,1)} %bitcast.2), calls=%async_computation | async-start | bytes 524288 | tf_op jit(solution)/shard_map/all_to_all | solution.py:374
  18.5 0.0 copy-done.9
  18.6 0.1 copy.34
  18.7 0.0 copy-done.8
  18.7 0.0 copy-done.10
  18.7 18.7 %all-to-all-done = bf16[32,8,392]{2,1,0:T(8,128)(2,1)S(1)} async-done(((bf16[32,8,392]{2,1,0:T(8,128)(2,1)}), bf16[32,8,392]{2,1,0:T(8,128)(2,1)S(1)}, u32[]{:S(2)}, u32[]{:S(2)}) %all-to-all-start) | async-done | bytes 200736 | tf_op jit(solution)/shard_map/all_to_all | solution.py:374
  37.5 4.0 %gather_fusion.1 = bf16[1024,392]{1,0:T(8,128)(2,1)S(1)} fusion(bf16[320,392]{1,0:T(8,128)(2,1)S(1)} %pad_maximum_fusion, s32[1024]{0:T(1024)S(1)} %fusion.5), kind=kCustom, calls=%fused_computation.1 | custom fusion | bytes 1609728 | tf_op jit(solution)/shard_map/gather | solution.py:392
  41.5 1.3 %fusion.1 = bf16[16,80,512]{2,1,0:T(8,128)(2,1)} fusion(bf16[16,64,392]{2,1,0:T(8,128)(2,1)S(1)} %bitcast.51, bf16[16,16,512]{2,1,0:T(8,128)(2,1)S(1)} %broadcast_in_dim.51), kind=kLoop, calls=%fused_computation.7 | loop fusion | flops 3932160 | bytes 2375680 | tf_op jit(solution)/shard_map/concatenate | solution.py:394
  42.7 0.0 copy-start.7
  42.7 0.0 copy-start.6
  42.7 0.0 copy-start.5
  42.7 7.2 %all-to-all-start.1 = ((bf16[16,80,512]{2,1,0:T(8,128)(2,1)}), bf16[16,80,512]{2,1,0:T(8,128)(2,1)S(1)}, u32[]{:S(2)}, u32[]{:S(2)}) async-start(bf16[16,80,512]{2,1,0:T(8,128)(2,1)} %fusion.1), calls=%async_computation.1 | async-start | bytes 2621440 | tf_op jit(solution)/shard_map/all_to_all | solution.py:395
  50.6 0.0 copy-done.7
  50.6 0.7 copy.36
  51.3 0.0 copy-done.6
  51.3 0.8 copy.35
  52.1 0.0 copy-done.5
  52.1 0.8 copy.37
  52.9 0.0 copy-start.3
  52.9 3.7 %copy.38 = bf16[896,896]{0,1:T(8,128)(2,1)} copy(bf16[896,896]{1,0:T(8,128)(2,1)} %param.28) | data formatting | bytes 3211264 | tf_op args[12]
  56.6 0.0 copy-done.3
  56.6 2.2 %copy.40 = bf16[2,640,640]{1,2,0:T(8,128)(2,1)} copy(bf16[2,640,640]{2,1,0:T(8,128)(2,1)S(1)} %copy-done.3) | data formatting | bytes 3276800 | tf_op args[14]
  58.8 0.0 copy-start.1
  58.8 4.3 %copy.39 = bf16[2,768,768]{1,2,0:T(8,128)(2,1)} copy(bf16[2,768,768]{2,1,0:T(8,128)(2,1)} %param.29) | data formatting | bytes 4718592 | tf_op args[13]
  63.1 0.8 compare_select_fusion.2
  63.9 0.0 copy-done.1
  63.9 0.8 gather_fusion.2
  64.7 1.3 %dynamic-slice_bitcast_fusion.length_ref = f32[1,64]{1,0:T(1,128)} fusion(f32[1024]{0:T(1024)} %param.23, s32[]{:T(128)S(6)} %select_n.28), kind=kLoop, calls=%fused_computation.34 | loop fusion | bytes 516 | tf_op jit(solution)/shard_map/broadcast_in_dim | solution.py:314
  65.9 0.0 copy-done
  65.9 0.7 constant_dynamic-slice_fusion.wig_ref
  66.6 0.7 select_convert_fusion.onehot_ref
  67.3 0.6 fusion.3.kind_ref
  67.9 6.4 %all-to-all-done.1.src_ref = bf16[16,80,512]{2,1,0:T(8,128)(2,1)S(1)} async-done(((bf16[16,80,512]{2,1,0:T(8,128)(2,1)}), bf16[16,80,512]{2,1,0:T(8,128)(2,1)S(1)}, u32[]{:S(2)}, u32[]{:S(2)}) %all-to-all-start.1) | async-done | bytes 1310752 | tf_op jit(solution)/shard_map/all_to_all | solution.py:395
  74.4 0.0 copy-start.2
  74.4 1.1 copy-done.2
  75.5 11.7 %shard_map.154 = f32[49,128,64]{2,1,0:T(8,128)} custom-call(bf16[16,80,512]{2,1,0:T(8,128)(2,1)} %copy-done.2, bf16[235,64]{1,0:T(8,128)(2,1)} %constant_dynamic-slice_fusion.wig_ref, f32[1,64]{1,0:T(1,128)} %dynamic-slice_bitcast_fusion.length_ref, bf16[90,64]{1,0:T(8,128)(2,1)} %fusion.3.kind_ref, bf16[128,512]{1,0:T(8,128)(2,1)} %bitcast.54, ...), custom_call_target="tpu_custom_call" | custom-call | flops 637534208 | bytes 8953216 | tf_op jit(solution)/shard_map/pallas_call | solution.py:325
  87.2 2.1 %copy_bitcast_fusion = bf16[16,49,8,64]{3,2,1,0:T(8,128)(2,1)S(1)} fusion(f32[49,128,64]{2,1,0:T(8,128)} %shard_map.154), kind=kLoop, calls=%fused_computation.36 | loop fusion | flops 401408 | bytes 2408448
  89.3 1.0 reshape.57
  90.3 18.4 %all_to_all.22 = bf16[16,2,12544]{2,1,0:T(2,128)(2,1)} all-to-all(bf16[16,2,12544]{2,1,0:T(2,128)(2,1)S(1)} %reshape.57), channel_id=1, replica_groups=mesh['graph'=32,'irreps'=16] {'irreps'}, dimensions={0} | all-to-all | bytes 1605632 | tf_op jit(solution)/shard_map/all_to_all | solution.py:417
  108.7 0.0 copy-start.4
  108.7 3.0 %reshape.58 = bf16[16,49,8,64]{3,2,1,0:T(8,128)(2,1)S(1)} reshape(bf16[16,2,12544]{2,1,0:T(2,128)(2,1)} %all_to_all.22) | data formatting | bytes 1605632
  111.7 0.3 convert_reduce_fusion
  112.0 0.0 copy-done.4
  112.0 0.7 fusion.2
  (11 shorter events, 0.1 us)
Async XLA Ops:
  0.0 65.9 %copy-start = (bf16[235,1024]{1,0:T(8,128)(2,1)S(1)}, bf16[235,1024]{1,0:T(8,128)(2,1)}, u32[]{:S(2)}) copy-start(bf16[235,1024]{1,0:T(8,128)(2,1)} %param.24) | copy-start | bytes 1443844
  0.0 18.5 %copy-start.9 = (f32[7,8]{1,0:T(8,128)S(1)}, f32[7,8]{1,0:T(8,128)}, u32[]{:S(2)}) copy-start(f32[7,8]{1,0:T(8,128)} %param.17) | copy-start | bytes 676
  0.0 18.7 %copy-start.8 = (bf16[7,128,8]{1,2,0:T(8,128)(2,1)S(1)}, bf16[7,128,8]{1,2,0:T(8,128)(2,1)}, u32[]{:S(2)}) copy-start(bf16[7,128,8]{1,2,0:T(8,128)(2,1)} %param.31) | copy-start | bytes 43012
  0.0 18.7 %copy-start.10 = (s32[1024]{0:T(1024)S(1)}, s32[1024]{0:T(1024)}, u32[]{:S(2)}) copy-start(s32[1024]{0:T(1024)} %param.20) | copy-start | bytes 12292
  3.6 33.8 %all-to-all-start = ((bf16[32,8,392]{2,1,0:T(8,128)(2,1)}), bf16[32,8,392]{2,1,0:T(8,128)(2,1)S(1)}, u32[]{:S(2)}, u32[]{:S(2)}) async-start(bf16[32,8,392]{2,1,0:T(8,128)(2,1)} %bitcast.2), calls=%async_computation | async-start | bytes 524288 | tf_op jit(solution)/shard_map/all_to_all | solution.py:374
  42.7 7.8 %copy-start.7 = (bf16[90,128]{1,0:T(8,128)(2,1)S(1)}, bf16[90,128]{1,0:T(8,128)(2,1)}, u32[]{:S(2)}) copy-start(bf16[90,128]{1,0:T(8,128)(2,1)} %param.26) | copy-start | bytes 69124
  42.7 8.6 %copy-start.6 = (bf16[512,128]{1,0:T(8,128)(2,1)S(1)}, bf16[512,128]{1,0:T(8,128)(2,1)}, u32[]{:S(2)}) copy-start(bf16[512,128]{1,0:T(8,128)(2,1)} %param.25) | copy-start | bytes 393220
  42.7 9.3 %copy-start.5 = (bf16[128,896]{1,0:T(8,128)(2,1)S(1)}, bf16[128,896]{1,0:T(8,128)(2,1)}, u32[]{:S(2)}) copy-start(bf16[128,896]{1,0:T(8,128)(2,1)} %param.27) | copy-start | bytes 688132
  42.7 31.6 %all-to-all-start.1 = ((bf16[16,80,512]{2,1,0:T(8,128)(2,1)}), bf16[16,80,512]{2,1,0:T(8,128)(2,1)S(1)}, u32[]{:S(2)}, u32[]{:S(2)}) async-start(bf16[16,80,512]{2,1,0:T(8,128)(2,1)} %fusion.1), calls=%async_computation.1 | async-start | bytes 2621440 | tf_op jit(solution)/shard_map/all_to_all | solution.py:395
  52.9 3.7 %copy-start.3 = (bf16[2,640,640]{2,1,0:T(8,128)(2,1)S(1)}, bf16[2,640,640]{2,1,0:T(8,128)(2,1)}, u32[]{:S(2)}) copy-start(bf16[2,640,640]{2,1,0:T(8,128)(2,1)} %param.30) | copy-start | bytes 4915204
  58.8 5.1 %copy-start.1 = (s32[64]{0:T(128)S(1)}, s32[64]{0:T(128)}, u32[]{:S(2)}) copy-start(s32[64]{0:T(128)} %param.18) | copy-start | bytes 772
  74.4 1.1 copy-start.2
  108.7 3.4 %copy-start.4 = (bf16[49,8,64]{2,1,0:T(8,128)(2,1)S(1)}, bf16[49,8,64]{2,1,0:T(8,128)(2,1)}, u32[]{:S(2)}) copy-start(bf16[49,8,64]{2,1,0:T(8,128)(2,1)} %param.16) | copy-start | bytes 150532

commit v5 on v4

--- a/solution.py
+++ b/solution.py
@@ -414,10 +414,10 @@
         order_zero, order_one, order_two, onehot, per_owner,
     )
     projected = jnp.transpose(projected, (1, 0, 2))
-    returned = lax.all_to_all(
-        projected.reshape(owners, span_chan, coeffs, atom_count).astype(jnp.bfloat16), "irreps", 0, 0, tiled=True
-    )
-    total = jnp.transpose(jnp.sum(returned.astype(jnp.float32), axis=0), (1, 0, 2))
+    total = jnp.transpose(
+        lax.psum_scatter(projected.reshape(owners * span_chan, coeffs, atom_count), "irreps", scatter_dimension=0, tiled=True),
+        (1, 0, 2),
+    )
     return (node_feats.astype(jnp.float32) + total).astype(jnp.bfloat16)
 
 

time: 113 us -> 186 us (1.65)
  the two profiles are of different devices: /device:TPU:64 before, /device:TPU:2 now
where the time goes in v5:
time: 186 us
  waiting for transfers between devices  108 us (58%)
  local copies, waits for them, and re-layouts  23.4 us (13%)
  starting transfers between devices  23.1 us (12%)
  between operations  14.2 us (8%)
  Pallas kernels  11.7 us (6%)
  other arithmetic  5.72 us (3%)
    reduce_scatter x1, waiting for transfers between devices, body(): lax.psum_scatter(projected.reshape(owners * span_chan, coeffs, atom_count...  84.8 us
    all_to_all x1, waiting for transfers between devices, body(): arrived = lax.all_to_all(node_rows[send_list], 'graph', 0, 0, tiled=True)  22.6 us
    all_to_all x1, starting transfers between devices, body(): arrived = lax.all_to_all(node_rows[send_list], 'graph', 0, 0, tiled=True)  15.5 us
    unnamed x28, local copies, waits for them, and re-layouts  13.6 us
    pallas_call x1, Pallas kernels, convolve_edges(): pl.pallas_call(conv_kernel, out_shape=jax.ShapeDtypeStruct((coeffs, chann...  11.7 us
    all_to_all x1, starting transfers between devices, body(): source = lax.all_to_all(outgoing, 'irreps', 0, 0, tiled=True)  7.61 us
    gather x1, local copies, waits for them, and re-layouts, body(): lookup[edge_source].reshape(owners, per_owner, row_used)  3.97 us
  transfers between devices with their start and end apart: 3, of which 3 were waited for; matrix products, arithmetic and copies ran while one was open for 9% of the time, Pallas kernels for 0%

profile of v5, /device:TPU:2, one launch (start us, length us, event | category | flops | bytes accessed | tf_op | source)
XLA Modules:
  0.0 185.7 jit_solution(5972837675324667223)
XLA Ops:
  6.5 0.0 copy-start
  6.5 0.0 copy-start.9
  6.5 0.0 copy-start.8
  6.5 0.0 copy-start.10
  6.5 0.7 compare_select_fusion.1
  7.3 1.0 copy.25
  8.3 1.8 gather_fusion
  10.1 15.5 %all-to-all-start = ((bf16[32,8,392]{2,1,0:T(8,128)(2,1)}), bf16[32,8,392]{2,1,0:T(8,128)(2,1)S(1)}, u32[]{:S(2)}, u32[]{:S(2)}) async-start(bf16[32,8,392]{2,1,0:T(8,128)(2,1)} %bitcast.2), calls=%async_computation | async-start | bytes 524288 | tf_op jit(solution)/shard_map/all_to_all | solution.py:374
  25.6 0.0 copy-done.9
  25.7 0.1 copy.26
  25.8 0.0 copy-done.8
  25.8 0.0 copy-done.10
  25.8 22.6 %all-to-all-done = bf16[32,8,392]{2,1,0:T(8,128)(2,1)S(1)} async-done(((bf16[32,8,392]{2,1,0:T(8,128)(2,1)}), bf16[32,8,392]{2,1,0:T(8,128)(2,1)S(1)}, u32[]{:S(2)}, u32[]{:S(2)}) %all-to-all-start) | async-done | bytes 200736 | tf_op jit(solution)/shard_map/all_to_all | solution.py:374
  48.4 4.0 %gather_fusion.1 = bf16[1024,392]{1,0:T(8,128)(2,1)S(1)} fusion(bf16[320,392]{1,0:T(8,128)(2,1)S(1)} %pad_maximum_fusion, s32[1024]{0:T(1024)S(1)} %fusion.5), kind=kCustom, calls=%fused_computation.1 | custom fusion | bytes 1609728 | tf_op jit(solution)/shard_map/gather | solution.py:392
  52.4 1.3 fusion.1
  53.7 0.0 copy-start.7
  53.7 0.0 copy-start.6
  53.7 0.0 copy-start.5
  53.7 7.6 %all-to-all-start.1 = ((bf16[16,80,512]{2,1,0:T(8,128)(2,1)}), bf16[16,80,512]{2,1,0:T(8,128)(2,1)S(1)}, u32[]{:S(2)}, u32[]{:S(2)}) async-start(bf16[16,80,512]{2,1,0:T(8,128)(2,1)} %fusion.1), calls=%async_computation.1 | async-start | bytes 2621440 | tf_op jit(solution)/shard_map/all_to_all | solution.py:395
  61.3 0.0 reduce-scatter.2.cloned.1.call-start
  62.0 0.0 copy-done.7
  62.0 0.7 copy.28
  62.7 0.0 copy-done.6
  62.7 0.8 copy.27
  63.5 0.0 copy-done.5
  63.5 0.8 copy.29
  64.3 0.0 copy-start.3
  64.3 3.7 %copy.30 = bf16[896,896]{0,1:T(8,128)(2,1)} copy(bf16[896,896]{1,0:T(8,128)(2,1)} %param.28) | data formatting | bytes 3211264 | tf_op args[12]
  68.0 0.0 copy-done.3
  68.0 2.2 %copy.32 = bf16[2,640,640]{1,2,0:T(8,128)(2,1)} copy(bf16[2,640,640]{2,1,0:T(8,128)(2,1)S(1)} %copy-done.3) | data formatting | bytes 3276800 | tf_op args[14]
  70.2 0.0 copy-start.1
  70.2 4.3 %copy.31 = bf16[2,768,768]{1,2,0:T(8,128)(2,1)} copy(bf16[2,768,768]{2,1,0:T(8,128)(2,1)} %param.29) | data formatting | bytes 4718592 | tf_op args[13]
  74.5 0.8 compare_select_fusion.2
  75.3 0.0 copy-done.1
  75.3 0.8 gather_fusion.2
  76.1 1.3 dynamic-slice_bitcast_fusion.length_ref
  77.4 0.0 copy-done
  77.4 0.7 constant_dynamic-slice_fusion.wig_ref
  78.1 0.7 select_convert_fusion.onehot_ref
  78.8 0.6 fusion.3.kind_ref
  79.4 0.1 all-to-all-done.1.src_ref
  79.6 0.0 copy-start.2
  79.6 1.1 copy-done.2
  80.6 11.7 %shard_map.154 = f32[49,128,64]{2,1,0:T(8,128)} custom-call(bf16[16,80,512]{2,1,0:T(8,128)(2,1)} %copy-done.2, bf16[235,64]{1,0:T(8,128)(2,1)} %constant_dynamic-slice_fusion.wig_ref, f32[1,64]{1,0:T(1,128)} %dynamic-slice_bitcast_fusion.length_ref, bf16[90,64]{1,0:T(8,128)(2,1)} %fusion.3.kind_ref, bf16[128,512]{1,0:T(8,128)(2,1)} %bitcast.47, ...), custom_call_target="tpu_custom_call" | custom-call | flops 637534208 | bytes 8953216 | tf_op jit(solution)/shard_map/pallas_call | solution.py:325
  92.4 0.0 copy-start.4
  92.4 0.0 reduce-scatter.2.cloned.1.call-update
  92.4 84.8 %reduce-scatter.2.cloned.1.call-done = f32[8,49,64]{2,0,1:T(8,128)} async-done(((f32[128,49,64]{2,0,1:T(8,128)}), f32[8,49,64]{2,0,1:T(8,128)}) %reduce-scatter.2.cloned.1.call-update) | async-done | bytes 100368 | tf_op jit(solution)/shard_map/reduce_scatter | solution.py:418
  177.2 0.0 copy-done.4
  177.2 1.6 fusion.2
  (11 shorter events, 0.1 us)
Async XLA Ops:
  6.5 70.9 %copy-start = (bf16[235,1024]{1,0:T(8,128)(2,1)S(1)}, bf16[235,1024]{1,0:T(8,128)(2,1)}, u32[]{:S(2)}) copy-start(bf16[235,1024]{1,0:T(8,128)(2,1)} %param.24) | copy-start | bytes 1443844
  6.5 19.1 %copy-start.9 = (f32[7,8]{1,0:T(8,128)S(1)}, f32[7,8]{1,0:T(8,128)}, u32[]{:S(2)}) copy-start(f32[7,8]{1,0:T(8,128)} %param.17) | copy-start | bytes 676
  6.5 19.2 %copy-start.8 = (bf16[7,128,8]{1,2,0:T(8,128)(2,1)S(1)}, bf16[7,128,8]{1,2,0:T(8,128)(2,1)}, u32[]{:S(2)}) copy-start(bf16[7,128,8]{1,2,0:T(8,128)(2,1)} %param.31) | copy-start | bytes 43012
  6.5 19.3 %copy-start.10 = (s32[1024]{0:T(1024)S(1)}, s32[1024]{0:T(1024)}, u32[]{:S(2)}) copy-start(s32[1024]{0:T(1024)} %param.20) | copy-start | bytes 12292
  10.1 38.2 %all-to-all-start = ((bf16[32,8,392]{2,1,0:T(8,128)(2,1)}), bf16[32,8,392]{2,1,0:T(8,128)(2,1)S(1)}, u32[]{:S(2)}, u32[]{:S(2)}) async-start(bf16[32,8,392]{2,1,0:T(8,128)(2,1)} %bitcast.2), calls=%async_computation | async-start | bytes 524288 | tf_op jit(solution)/shard_map/all_to_all | solution.py:374
  53.7 8.3 %copy-start.7 = (bf16[90,128]{1,0:T(8,128)(2,1)S(1)}, bf16[90,128]{1,0:T(8,128)(2,1)}, u32[]{:S(2)}) copy-start(bf16[90,128]{1,0:T(8,128)(2,1)} %param.26) | copy-start | bytes 69124
  53.7 9.0 %copy-start.6 = (bf16[512,128]{1,0:T(8,128)(2,1)S(1)}, bf16[512,128]{1,0:T(8,128)(2,1)}, u32[]{:S(2)}) copy-start(bf16[512,128]{1,0:T(8,128)(2,1)} %param.25) | copy-start | bytes 393220
  53.7 9.8 %copy-start.5 = (bf16[128,896]{1,0:T(8,128)(2,1)S(1)}, bf16[128,896]{1,0:T(8,128)(2,1)}, u32[]{:S(2)}) copy-start(bf16[128,896]{1,0:T(8,128)(2,1)} %param.27) | copy-start | bytes 688132
  53.7 25.9 %all-to-all-start.1 = ((bf16[16,80,512]{2,1,0:T(8,128)(2,1)}), bf16[16,80,512]{2,1,0:T(8,128)(2,1)S(1)}, u32[]{:S(2)}, u32[]{:S(2)}) async-start(bf16[16,80,512]{2,1,0:T(8,128)(2,1)} %fusion.1), calls=%async_computation.1 | async-start | bytes 2621440 | tf_op jit(solution)/shard_map/all_to_all | solution.py:395
  61.3 115.9 %reduce-scatter.2.cloned.1.call-start = ((), (), s32[]{:S(2)}) async-start(), calls=%async_computation.3 | async-start | bytes 3411968 | tf_op jit(solution)/shard_map/reduce_scatter | solution.py:418
  64.3 3.7 %copy-start.3 = (bf16[2,640,640]{2,1,0:T(8,128)(2,1)S(1)}, bf16[2,640,640]{2,1,0:T(8,128)(2,1)}, u32[]{:S(2)}) copy-start(bf16[2,640,640]{2,1,0:T(8,128)(2,1)} %param.30) | copy-start | bytes 4915204
  70.2 5.1 %copy-start.1 = (s32[64]{0:T(128)S(1)}, s32[64]{0:T(128)}, u32[]{:S(2)}) copy-start(s32[64]{0:T(128)} %param.18) | copy-start | bytes 772
  79.6 1.1 copy-start.2
  92.4 84.9 %copy-start.4 = (bf16[49,8,64]{2,1,0:T(8,128)(2,1)S(1)}, bf16[49,8,64]{2,1,0:T(8,128)(2,1)}, u32[]{:S(2)}) copy-start(bf16[49,8,64]{2,1,0:T(8,128)(2,1)} %param.16) | copy-start | bytes 150532
Sparse Core Ops, SparseCore 0:
  92.5 84.6 reduce-scatter.1

commit v6 on v5

--- a/solution.py
+++ b/solution.py
@@ -292,15 +292,25 @@
     summed = jnp.dot(upper_part, onehot, preferred_element_type=jnp.float32) + jnp.dot(
         lower_part, onehot, preferred_element_type=jnp.float32
     )
+    half = span_chan // 2
+    pieces = [[] for _ in range(owners)]
     for degree in range(levels):
         weight = projection[degree]
         for j in range(degree * degree, (degree + 1) ** 2):
             piece = summed[j * channel_count : (j + 1) * channel_count]
             high = piece.astype(jnp.bfloat16)
             low = (piece - high.astype(jnp.float32)).astype(jnp.bfloat16)
-            out_ref[j] = jnp.dot(weight, high, preferred_element_type=jnp.float32) + jnp.dot(
+            result = jnp.dot(weight, high, preferred_element_type=jnp.float32) + jnp.dot(
                 weight, low, preferred_element_type=jnp.float32
             )
+            for r in range(owners):
+                block = result[r * span_chan : (r + 1) * span_chan]
+                pieces[r].append(jnp.concatenate([block[:half], block[half:]], axis=1))
+    fill = out_ref.shape[1] - COEFFS * half
+    for r in range(owners):
+        out_ref[r] = jnp.concatenate(
+            pieces[r] + [jnp.zeros((fill, out_ref.shape[2]), jnp.float32)], axis=0
+        ).astype(out_ref.dtype)
 
 
 def convolve_edges(source, wig_mine, lengths, kind_onehot, radial_in, species_table, radial_out,
@@ -308,6 +318,8 @@
     coeffs, channel_count = COEFFS, CHANNELS
     num_edges = per_owner
     atom_count = onehot.shape[1]
+    owners = source.shape[0]
+    out_rows = 16 * pl.cdiv(coeffs * (channel_count // owners) // 2, 16)
     operands = (
         source,
         wig_mine,
@@ -324,13 +336,13 @@
     flops = 2 * num_edges * (order_zero.size + 2 * order_one.size + 2 * order_two.size + radial_out.size + radial_in.size)
     return pl.pallas_call(
         conv_kernel,
-        out_shape=jax.ShapeDtypeStruct((coeffs, channel_count, atom_count), jnp.float32),
+        out_shape=jax.ShapeDtypeStruct((owners, out_rows, 2 * atom_count), jnp.bfloat16),
         in_specs=[pl.BlockSpec(memory_space=pltpu.VMEM)] * len(operands),
         out_specs=pl.BlockSpec(memory_space=pltpu.VMEM),
         cost_estimate=pl.CostEstimate(
             flops=flops,
             transcendentals=num_edges * (radial_in.shape[0] + 2 * channel_count),
-            bytes_accessed=sum(int(x.size) * x.dtype.itemsize for x in operands) + coeffs * channel_count * atom_count * 4,
+            bytes_accessed=sum(int(x.size) * x.dtype.itemsize for x in operands) + owners * out_rows * atom_count * 4,
         ),
     )(*operands)
 
@@ -380,8 +392,9 @@
     gain_block = jnp.transpose(jnp.stack([gain_high, gain_mid, gain_low]), (2, 0, 1))
     gain_block = jnp.pad(gain_block, ((0, 0), (0, 0), (0, 1))).reshape(span_chan, 3 * (levels + 1))
     gain_block = jnp.pad(gain_block, ((0, 0), (0, CHANNELS - gain_block.shape[1]))).astype(jnp.bfloat16)
+    pair_order = np.concatenate([np.arange(0, span_chan, 2), np.arange(1, span_chan, 2)])
     weight_block = jnp.concatenate(
-        [jnp.transpose(project_weight, (2, 0, 1)), gain_block[:, None, :]], axis=1
+        [jnp.transpose(project_weight[:, :, pair_order], (2, 0, 1)), gain_block[:, None, :]], axis=1
     )
     extra = jnp.transpose(weight_block.reshape(span_chan, 2, 4, CHANNELS), (1, 0, 2, 3)).reshape(
         2 * span_chan, 4 * CHANNELS
@@ -413,11 +426,9 @@
         source, wig_mine, lengths_mine, kind_onehot, radial_in, species_table, radial_out,
         order_zero, order_one, order_two, onehot, per_owner,
     )
-    projected = jnp.transpose(projected, (1, 0, 2))
-    total = jnp.transpose(
-        lax.psum_scatter(projected.reshape(owners * span_chan, coeffs, atom_count), "irreps", scatter_dimension=0, tiled=True),
-        (1, 0, 2),
-    )
+    returned = lax.all_to_all(projected, "irreps", 0, 0, tiled=True)
+    total = jnp.sum(returned.astype(jnp.float32), axis=0)[: coeffs * span_chan // 2]
+    total = total.reshape(coeffs, span_chan // 2, 2, atom_count).reshape(coeffs, span_chan, atom_count)
     return (node_feats.astype(jnp.float32) + total).astype(jnp.bfloat16)
 
 

time: 186 us -> 107 us (0.58)
  the two profiles are of different devices: /device:TPU:2 before, /device:TPU:64 now
where the time goes in v6:
time: 107 us
  waiting for transfers between devices  24.5 us (23%)
  local copies, waits for them, and re-layouts  24.1 us (23%)
  starting transfers between devices  22.2 us (21%)
  blocking collectives  19.3 us (18%)
  Pallas kernels  11.1 us (10%)
  other arithmetic  4.93 us (5%)
    all_to_all x1, blocking collectives, body(): returned = lax.all_to_all(projected, 'irreps', 0, 0, tiled=True)  19.3 us
    all_to_all x1, waiting for transfers between devices, body(): arrived = lax.all_to_all(node_rows[send_list], 'graph', 0, 0, tiled=True)  18.1 us
    all_to_all x1, starting transfers between devices, body(): arrived = lax.all_to_all(node_rows[send_list], 'graph', 0, 0, tiled=True)  15 us
    unnamed x30, local copies, waits for them, and re-layouts  13.6 us
    pallas_call x1, Pallas kernels, convolve_edges(): pl.pallas_call(conv_kernel, out_shape=jax.ShapeDtypeStruct((owners, out_r...  11.1 us
    all_to_all x1, starting transfers between devices, body(): source = lax.all_to_all(outgoing, 'irreps', 0, 0, tiled=True)  7.17 us
    all_to_all x1, waiting for transfers between devices, body(): source = lax.all_to_all(outgoing, 'irreps', 0, 0, tiled=True)  6.39 us
    gather x1, local copies, waits for them, and re-layouts, body(): lookup[edge_source].reshape(owners, per_owner, row_used)  3.97 us
  transfers between devices with their start and end apart: 2, of which 2 were waited for; matrix products, arithmetic and copies ran while one was open for 17% of the time, Pallas kernels for 0%

profile of v6, /device:TPU:64, one launch (start us, length us, event | category | flops | bytes accessed | tf_op | source)
XLA Modules:
  0.0 106.9 jit_solution(1034099207226678547)
XLA Ops:
  0.0 0.0 copy-start
  0.0 0.0 copy-start.11
  0.0 0.0 copy-start.9
  0.0 0.0 copy-start.2
  0.0 0.8 compare_select_fusion.1
  0.8 1.0 copy.35
  1.8 1.9 %gather_fusion = bf16[256,392]{1,0:T(8,128)(2,1)} fusion(bf16[64,392]{1,0:T(8,128)(2,1)S(1)} %bitcast.32, s32[1024]{0:T(1024)S(1)} %pad_clamp_fusion.2), kind=kCustom, calls=%fused_computation | custom fusion | bytes 402432 | tf_op jit(solution)/shard_map/gather | solution.py:386
  3.6 0.0 copy-start.10
  3.6 15.0 %all-to-all-start = ((bf16[32,8,392]{2,1,0:T(8,128)(2,1)}), bf16[32,8,392]{2,1,0:T(8,128)(2,1)S(1)}, u32[]{:S(2)}, u32[]{:S(2)}) async-start(bf16[32,8,392]{2,1,0:T(8,128)(2,1)} %bitcast.2), calls=%async_computation | async-start | bytes 524288 | tf_op jit(solution)/shard_map/all_to_all | solution.py:386
  18.7 0.0 copy-done.9
  18.7 0.1 copy.43
  18.8 0.0 copy-done.11
  18.8 0.0 copy-done.2
  18.8 0.6 gather_fusion.2
  19.5 0.0 copy-done.10
  19.5 18.1 %all-to-all-done = bf16[32,8,392]{2,1,0:T(8,128)(2,1)S(1)} async-done(((bf16[32,8,392]{2,1,0:T(8,128)(2,1)}), bf16[32,8,392]{2,1,0:T(8,128)(2,1)S(1)}, u32[]{:S(2)}, u32[]{:S(2)}) %all-to-all-start) | async-done | bytes 200736 | tf_op jit(solution)/shard_map/all_to_all | solution.py:386
  37.6 4.0 %gather_fusion.1 = bf16[1024,392]{1,0:T(8,128)(2,1)S(1)} fusion(bf16[320,392]{1,0:T(8,128)(2,1)S(1)} %pad_maximum_fusion, s32[1024]{0:T(1024)S(1)} %fusion.4), kind=kCustom, calls=%fused_computation.1 | custom fusion | bytes 1609728 | tf_op jit(solution)/shard_map/gather | solution.py:405
  41.6 1.2 %fusion.1 = bf16[16,80,512]{2,1,0:T(8,128)(2,1)} fusion(bf16[16,64,392]{2,1,0:T(8,128)(2,1)S(1)} %bitcast.37, bf16[16,16,512]{2,1,0:T(8,128)(2,1)S(1)} %broadcast_in_dim.55), kind=kLoop, calls=%fused_computation.7 | loop fusion | flops 3932160 | bytes 2375680 | tf_op jit(solution)/shard_map/concatenate | solution.py:407
  42.9 0.0 copy-start.8
  42.9 0.0 copy-start.7
  42.9 0.0 copy-start.6
  42.9 7.2 %all-to-all-start.1 = ((bf16[16,80,512]{2,1,0:T(8,128)(2,1)}), bf16[16,80,512]{2,1,0:T(8,128)(2,1)S(1)}, u32[]{:S(2)}, u32[]{:S(2)}) async-start(bf16[16,80,512]{2,1,0:T(8,128)(2,1)} %fusion.1), calls=%async_computation.1 | async-start | bytes 2621440 | tf_op jit(solution)/shard_map/all_to_all | solution.py:408
  50.7 0.0 copy-done.8
  50.7 0.7 copy.38
  51.4 0.0 copy-done.7
  51.4 0.8 copy.37
  52.2 0.0 copy-done.6
  52.2 0.8 copy.39
  53.0 0.0 copy-start.4
  53.0 3.7 %copy.40 = bf16[896,896]{0,1:T(8,128)(2,1)} copy(bf16[896,896]{1,0:T(8,128)(2,1)} %param.30) | data formatting | bytes 3211264 | tf_op args[12]
  56.7 0.0 copy-done.4
  56.7 2.2 %copy.42 = bf16[2,640,640]{1,2,0:T(8,128)(2,1)} copy(bf16[2,640,640]{2,1,0:T(8,128)(2,1)S(1)} %copy-done.4) | data formatting | bytes 3276800 | tf_op args[14]
  58.9 0.0 copy-start.1
  58.9 4.3 %copy.41 = bf16[2,768,768]{1,2,0:T(8,128)(2,1)} copy(bf16[2,768,768]{2,1,0:T(8,128)(2,1)} %param.31) | data formatting | bytes 4718592 | tf_op args[13]
  63.2 0.8 compare_select_fusion.2
  64.0 0.0 copy-done.1
  64.0 0.8 gather_fusion.3
  64.8 1.3 %dynamic-slice_bitcast_fusion.length_ref = f32[1,64]{1,0:T(1,128)} fusion(f32[1024]{0:T(1024)} %param.25, s32[]{:T(128)S(6)} %select_n.32), kind=kLoop, calls=%fused_computation.34 | loop fusion | bytes 516 | tf_op jit(solution)/shard_map/broadcast_in_dim | solution.py:326
  66.1 0.0 copy-done
  66.1 0.7 constant_dynamic-slice_fusion.wig_ref
  66.8 0.7 select_convert_fusion.onehot_ref
  67.5 0.6 fusion.2.kind_ref
  68.1 6.4 %all-to-all-done.1.src_ref = bf16[16,80,512]{2,1,0:T(8,128)(2,1)S(1)} async-done(((bf16[16,80,512]{2,1,0:T(8,128)(2,1)}), bf16[16,80,512]{2,1,0:T(8,128)(2,1)S(1)}, u32[]{:S(2)}, u32[]{:S(2)}) %all-to-all-start.1) | async-done | bytes 1310752 | tf_op jit(solution)/shard_map/all_to_all | solution.py:408
  74.5 0.0 copy-start.3
  74.5 1.1 %copy-done.3 = bf16[16,80,512]{2,1,0:T(8,128)(2,1)} copy-done((bf16[16,80,512]{2,1,0:T(8,128)(2,1)}, bf16[16,80,512]{2,1,0:T(8,128)(2,1)S(1)}, u32[]{:S(2)}) %copy-start.3) | copy-done | bytes 1310744
  75.6 11.1 %shard_map.172 = bf16[16,208,128]{2,1,0:T(8,128)(2,1)} custom-call(bf16[16,80,512]{2,1,0:T(8,128)(2,1)} %copy-done.3, bf16[235,64]{1,0:T(8,128)(2,1)} %constant_dynamic-slice_fusion.wig_ref, f32[1,64]{1,0:T(1,128)} %dynamic-slice_bitcast_fusion.length_ref, bf16[90,64]{1,0:T(8,128)(2,1)} %fusion.2.kind_ref, bf16[128,512]{1,0:T(8,128)(2,1)} %bitcast.40, ...), custom_call_target="tpu_custom_call" | custom-call | flops 637534208 | bytes 8199552 | tf_op jit(solution)/shard_map/pallas_call | solution.py:337
  86.6 0.0 copy-start.5
  86.6 19.3 %all_to_all.22 = bf16[16,208,128]{2,1,0:T(8,128)(2,1)S(1)} all-to-all(bf16[16,208,128]{2,1,0:T(8,128)(2,1)} %shard_map.172), channel_id=1, replica_groups=mesh['graph'=32,'irreps'=16] {'irreps'}, dimensions={0} | all-to-all | bytes 1703936 | tf_op jit(solution)/shard_map/all_to_all | solution.py:429
  106.0 0.1 convert_reduce_fusion
  106.1 0.1 reshape_reshape.3
  106.2 0.0 copy-done.5
  106.2 0.7 add_convert_fusion
  (13 shorter events, 0.1 us)
Async XLA Ops:
  0.0 66.1 %copy-start = (bf16[235,1024]{1,0:T(8,128)(2,1)S(1)}, bf16[235,1024]{1,0:T(8,128)(2,1)}, u32[]{:S(2)}) copy-start(bf16[235,1024]{1,0:T(8,128)(2,1)} %param.26) | copy-start | bytes 1443844
  0.0 18.8 %copy-start.11 = (s32[8]{0:T(128)S(1)}, s32[8]{0:T(128)}, u32[]{:S(2)}) copy-start(s32[8]{0:T(128)} %constant.44) | copy-start | bytes 100
  0.0 18.7 %copy-start.9 = (f32[7,8]{1,0:T(8,128)S(1)}, f32[7,8]{1,0:T(8,128)}, u32[]{:S(2)}) copy-start(f32[7,8]{1,0:T(8,128)} %param.19) | copy-start | bytes 676
  0.0 18.8 %copy-start.2 = (bf16[7,128,8]{1,2,0:T(8,128)(2,1)S(1)}, bf16[7,128,8]{1,2,0:T(8,128)(2,1)}, u32[]{:S(2)}) copy-start(bf16[7,128,8]{1,2,0:T(8,128)(2,1)} %param.33) | copy-start | bytes 43012
  3.6 15.8 %copy-start.10 = (s32[1024]{0:T(1024)S(1)}, s32[1024]{0:T(1024)}, u32[]{:S(2)}) copy-start(s32[1024]{0:T(1024)} %param.22) | copy-start | bytes 12292
  3.6 33.9 %all-to-all-start = ((bf16[32,8,392]{2,1,0:T(8,128)(2,1)}), bf16[32,8,392]{2,1,0:T(8,128)(2,1)S(1)}, u32[]{:S(2)}, u32[]{:S(2)}) async-start(bf16[32,8,392]{2,1,0:T(8,128)(2,1)} %bitcast.2), calls=%async_computation | async-start | bytes 524288 | tf_op jit(solution)/shard_map/all_to_all | solution.py:386
  42.9 7.8 %copy-start.8 = (bf16[90,128]{1,0:T(8,128)(2,1)S(1)}, bf16[90,128]{1,0:T(8,128)(2,1)}, u32[]{:S(2)}) copy-start(bf16[90,128]{1,0:T(8,128)(2,1)} %param.28) | copy-start | bytes 69124
  42.9 8.6 %copy-start.7 = (bf16[512,128]{1,0:T(8,128)(2,1)S(1)}, bf16[512,128]{1,0:T(8,128)(2,1)}, u32[]{:S(2)}) copy-start(bf16[512,128]{1,0:T(8,128)(2,1)} %param.27) | copy-start | bytes 393220
  42.9 9.3 %copy-start.6 = (bf16[128,896]{1,0:T(8,128)(2,1)S(1)}, bf16[128,896]{1,0:T(8,128)(2,1)}, u32[]{:S(2)}) copy-start(bf16[128,896]{1,0:T(8,128)(2,1)} %param.29) | copy-start | bytes 688132
  42.9 31.6 %all-to-all-start.1 = ((bf16[16,80,512]{2,1,0:T(8,128)(2,1)}), bf16[16,80,512]{2,1,0:T(8,128)(2,1)S(1)}, u32[]{:S(2)}, u32[]{:S(2)}) async-start(bf16[16,80,512]{2,1,0:T(8,128)(2,1)} %fusion.1), calls=%async_computation.1 | async-start | bytes 2621440 | tf_op jit(solution)/shard_map/all_to_all | solution.py:408
  53.0 3.7 %copy-start.4 = (bf16[2,640,640]{2,1,0:T(8,128)(2,1)S(1)}, bf16[2,640,640]{2,1,0:T(8,128)(2,1)}, u32[]{:S(2)}) copy-start(bf16[2,640,640]{2,1,0:T(8,128)(2,1)} %param.32) | copy-start | bytes 4915204
  58.9 5.1 %copy-start.1 = (s32[64]{0:T(128)S(1)}, s32[64]{0:T(128)}, u32[]{:S(2)}) copy-start(s32[64]{0:T(128)} %param.20) | copy-start | bytes 772
  74.5 1.1 %copy-start.3 = (bf16[16,80,512]{2,1,0:T(8,128)(2,1)}, bf16[16,80,512]{2,1,0:T(8,128)(2,1)S(1)}, u32[]{:S(2)}) copy-start(bf16[16,80,512]{2,1,0:T(8,128)(2,1)S(1)} %all-to-all-done.1.src_ref) | copy-start | bytes 3932164
  86.6 19.5 %copy-start.5 = (bf16[49,8,64]{2,1,0:T(8,128)(2,1)S(1)}, bf16[49,8,64]{2,1,0:T(8,128)(2,1)}, u32[]{:S(2)}) copy-start(bf16[49,8,64]{2,1,0:T(8,128)(2,1)} %param.18) | copy-start | bytes 150532

commit v7 on v6

--- a/solution.py
+++ b/solution.py
@@ -347,6 +347,40 @@
     )(*operands)
 
 
+def gather_kernel(index_ref, local_ref, arrived_ref, extra_ref, out_ref):
+    owners, _, row_width = out_ref.shape
+    per_owner = out_ref.shape[1] - extra_ref.shape[0]
+    row_used = local_ref.shape[1]
+    table = jnp.concatenate([local_ref[...], arrived_ref[...]], axis=0)
+    hot = (
+        index_ref[...] == lax.broadcasted_iota(jnp.int32, (index_ref.shape[0], table.shape[0]), 1)
+    ).astype(jnp.bfloat16)
+    picked = jnp.dot(hot, table, preferred_element_type=jnp.float32).astype(out_ref.dtype)
+    blank = jnp.zeros((per_owner, row_width - row_used), out_ref.dtype)
+    extra = extra_ref[...]
+    for q in range(owners):
+        out_ref[q, 0:per_owner, 0:row_used] = picked[q * per_owner : (q + 1) * per_owner]
+        out_ref[q, 0:per_owner, row_used:row_width] = blank
+        out_ref[q, per_owner:, :] = extra
+
+
+def gather_rows(edge_source, node_rows, arrived, extra, owners, row_width):
+    per_owner = edge_source.shape[0] // owners
+    operands = (edge_source[:, None], node_rows, arrived, extra)
+    return pl.pallas_call(
+        gather_kernel,
+        out_shape=jax.ShapeDtypeStruct((owners, per_owner + extra.shape[0], row_width), jnp.bfloat16),
+        in_specs=[pl.BlockSpec(memory_space=pltpu.VMEM)] * len(operands),
+        out_specs=pl.BlockSpec(memory_space=pltpu.VMEM),
+        cost_estimate=pl.CostEstimate(
+            flops=2 * edge_source.shape[0] * (node_rows.shape[0] + arrived.shape[0]) * node_rows.shape[1],
+            transcendentals=0,
+            bytes_accessed=sum(int(x.size) * x.dtype.itemsize for x in operands)
+            + owners * (per_owner + extra.shape[0]) * row_width * 2,
+        ),
+    )(*operands)
+
+
 def split_dot(values, weight):
     upper_part = values.astype(jnp.bfloat16)
     lower_part = (values - upper_part.astype(jnp.float32)).astype(jnp.bfloat16)
@@ -400,11 +434,7 @@
         2 * span_chan, 4 * CHANNELS
     )
 
-    lookup = jnp.concatenate([node_rows, arrived], axis=0)
-    gathered = jnp.pad(
-        lookup[edge_source].reshape(owners, per_owner, row_used), ((0, 0), (0, 0), (0, row_width - row_used))
-    )
-    outgoing = jnp.concatenate([gathered, jnp.broadcast_to(extra[None], (owners,) + extra.shape)], axis=1)
+    outgoing = gather_rows(edge_source, node_rows, arrived, extra, owners, row_width)
     source = lax.all_to_all(outgoing, "irreps", 0, 0, tiled=True)
 
     wig_mine = lax.dynamic_slice_in_dim(wigner, first_edge, per_owner, 1)

time: 107 us -> 106 us (level)
  Pallas kernels: 11.1 us -> 14.1 us
  local copies, waits for them, and re-layouts: 24.1 us -> 21.8 us
  waiting for transfers between devices: 24.5 us -> 22.9 us
    gather x1 -> x0, local copies, waits for them, and re-layouts: 3.97 us -> none  [body(): lookup[edge_source].reshape(owners, per_owner, row_used)]
    pallas_call x0 -> x1, Pallas kernels: none -> 3 us  [gather_rows(): pl.pallas_call(gather_kernel, out_shape=jax.ShapeDtypeStruct((owners, per...]
    all_to_all x1, waiting for transfers between devices: 18.1 us -> 16.5 us  [body(): arrived = lax.all_to_all(node_rows[send_list], 'graph', 0, 0, tiled=True)]
    concatenate x2 -> x0, other arithmetic: 1.28 us -> none  [the longest x1 1.25 us: body(): jnp.concatenate([gathered, jnp.broadcast_to(extra[None], (owners,) + extr...]
    unnamed x30 -> x34, local copies, waits for them, and re-layouts: 13.6 us -> 14.4 us
  transfers between devices with their start and end apart: 2 -> 2, of which waited for: 2 -> 2; matrix products, arithmetic and copies ran while one was open for 17% -> 19% of each run, Pallas kernels for 0% -> 0%
where the time goes in v7:
time: 106 us; the launch traced here: 105 us
  waiting for transfers between devices  22.9 us (22%)
  starting transfers between devices  22.1 us (21%)
  local copies, waits for them, and re-layouts  21.8 us (21%)
  blocking collectives  19.3 us (18%)
  Pallas kernels  14.1 us (13%)
  other arithmetic  4.22 us (4%)
    all_to_all x1, blocking collectives, body(): returned = lax.all_to_all(projected, 'irreps', 0, 0, tiled=True)  19.3 us
    all_to_all x1, waiting for transfers between devices, body(): arrived = lax.all_to_all(node_rows[send_list], 'graph', 0, 0, tiled=True)  16.5 us
    all_to_all x1, starting transfers between devices, body(): arrived = lax.all_to_all(node_rows[send_list], 'graph', 0, 0, tiled=True)  14.9 us
    unnamed x34, local copies, waits for them, and re-layouts  14.4 us
    pallas_call x1, Pallas kernels, convolve_edges(): pl.pallas_call(conv_kernel, out_shape=jax.ShapeDtypeStruct((owners, out_r...  11.1 us
    all_to_all x1, starting transfers between devices, body(): source = lax.all_to_all(outgoing, 'irreps', 0, 0, tiled=True)  7.17 us
    all_to_all x1, waiting for transfers between devices, body(): source = lax.all_to_all(outgoing, 'irreps', 0, 0, tiled=True)  6.4 us
    pallas_call x1, Pallas kernels, gather_rows(): pl.pallas_call(gather_kernel, out_shape=jax.ShapeDtypeStruct((owners, per...  3 us
  transfers between devices with their start and end apart: 2, of which 2 were waited for; matrix products, arithmetic and copies ran while one was open for 19% of the time, Pallas kernels for 0%

profile of v7, /device:TPU:64, one launch (start us, length us, event | category | flops | bytes accessed | tf_op | source)
XLA Modules:
  0.0 105.2 jit_solution(2415212353882375215)
XLA Ops:
  0.0 0.0 copy-start
  0.0 0.0 copy-start.12
  0.0 0.0 copy-start.11
  0.0 0.7 compare_select_fusion
  0.8 1.0 copy.36
  1.8 0.0 copy-start.3
  1.8 0.0 copy-start.13
  1.8 0.0 copy-start.2
  1.8 1.9 %gather_fusion = bf16[256,392]{1,0:T(8,128)(2,1)} fusion(bf16[64,392]{1,0:T(8,128)(2,1)S(1)} %bitcast.32, s32[1024]{0:T(1024)S(1)} %pad_clamp_fusion.2), kind=kCustom, calls=%fused_computation | custom fusion | bytes 402432 | tf_op jit(solution)/shard_map/gather | solution.py:420
  3.7 14.9 %all-to-all-start = ((bf16[32,8,392]{2,1,0:T(8,128)(2,1)}), bf16[32,8,392]{2,1,0:T(8,128)(2,1)S(1)}, u32[]{:S(2)}, u32[]{:S(2)}) async-start(bf16[32,8,392]{2,1,0:T(8,128)(2,1)} %bitcast.3), calls=%async_computation | async-start | bytes 524288 | tf_op jit(solution)/shard_map/all_to_all | solution.py:420
  18.6 0.0 copy-done.12
  18.6 0.1 copy.45
  18.7 0.0 copy-done.11
  18.7 1.0 copy.38.index_ref
  19.7 0.0 copy-done.3
  19.7 0.0 copy-done.13
  19.7 0.0 copy-done.2
  19.8 0.6 gather_fusion.1
  20.4 0.6 pad_maximum_fusion
  21.0 16.5 %all-to-all-done = bf16[32,8,392]{2,1,0:T(8,128)(2,1)S(1)} async-done(((bf16[32,8,392]{2,1,0:T(8,128)(2,1)}), bf16[32,8,392]{2,1,0:T(8,128)(2,1)S(1)}, u32[]{:S(2)}, u32[]{:S(2)}) %all-to-all-start) | async-done | bytes 200736 | tf_op jit(solution)/shard_map/all_to_all | solution.py:420
  37.4 0.0 copy-start.6
  37.5 0.7 copy-done.6
  38.2 3.0 %shard_map.172 = bf16[16,80,512]{2,1,0:T(8,128)(2,1)} custom-call(s32[1024,1]{1,0:T(8,128)} %copy.38.index_ref, bf16[64,392]{1,0:T(8,128)(2,1)} %bitcast.33, bf16[256,392]{1,0:T(8,128)(2,1)} %bitcast.37, bf16[16,512]{1,0:T(8,128)(2,1)} %bitcast.42), custom_call_target="tpu_custom_call" | custom-call | flops 256901120 | bytes 1582080 | tf_op jit(solution)/shard_map/pallas_call | solution.py:370
  41.1 0.0 copy-start.10
  41.1 0.0 copy-start.9
  41.2 0.0 copy-start.8
  41.2 7.2 %all-to-all-start.1 = ((bf16[16,80,512]{2,1,0:T(8,128)(2,1)}), bf16[16,80,512]{2,1,0:T(8,128)(2,1)S(1)}, u32[]{:S(2)}, u32[]{:S(2)}) async-start(bf16[16,80,512]{2,1,0:T(8,128)(2,1)} %shard_map.172), calls=%async_computation.1 | async-start | bytes 2621440 | tf_op jit(solution)/shard_map/all_to_all | solution.py:438
  49.0 0.0 copy-done.10
  49.0 0.7 copy.40
  49.7 0.0 copy-done.9
  49.7 0.8 copy.39
  50.5 0.0 copy-done.8
  50.5 0.8 copy.41
  51.3 0.0 copy-start.5
  51.3 3.7 %copy.42 = bf16[896,896]{0,1:T(8,128)(2,1)} copy(bf16[896,896]{1,0:T(8,128)(2,1)} %param.30) | data formatting | bytes 3211264 | tf_op args[12]
  55.0 0.0 copy-done.5
  55.0 2.2 %copy.44 = bf16[2,640,640]{1,2,0:T(8,128)(2,1)} copy(bf16[2,640,640]{2,1,0:T(8,128)(2,1)S(1)} %copy-done.5) | data formatting | bytes 3276800 | tf_op args[14]
  57.2 0.0 copy-start.1
  57.2 4.3 %copy.43 = bf16[2,768,768]{1,2,0:T(8,128)(2,1)} copy(bf16[2,768,768]{2,1,0:T(8,128)(2,1)} %param.31) | data formatting | bytes 4718592 | tf_op args[13]
  61.5 0.8 compare_select_fusion.1
  62.3 0.0 copy-done.1
  62.3 0.8 gather_fusion.2
  63.1 1.3 %dynamic-slice_bitcast_fusion.length_ref = f32[1,64]{1,0:T(1,128)} fusion(f32[1024]{0:T(1024)} %param.25, s32[]{:T(128)S(6)} %select_n.28), kind=kLoop, calls=%fused_computation.27 | loop fusion | bytes 516 | tf_op jit(solution)/shard_map/broadcast_in_dim | solution.py:326
  64.4 0.0 copy-done
  64.4 0.7 constant_dynamic-slice_fusion.wig_ref
  65.1 0.7 select_convert_fusion.onehot_ref
  65.8 0.6 fusion.kind_ref
  66.4 6.4 %all-to-all-done.1.src_ref = bf16[16,80,512]{2,1,0:T(8,128)(2,1)S(1)} async-done(((bf16[16,80,512]{2,1,0:T(8,128)(2,1)}), bf16[16,80,512]{2,1,0:T(8,128)(2,1)S(1)}, u32[]{:S(2)}, u32[]{:S(2)}) %all-to-all-start.1) | async-done | bytes 1310752 | tf_op jit(solution)/shard_map/all_to_all | solution.py:438
  72.8 0.0 copy-start.4
  72.8 1.1 %copy-done.4 = bf16[16,80,512]{2,1,0:T(8,128)(2,1)} copy-done((bf16[16,80,512]{2,1,0:T(8,128)(2,1)}, bf16[16,80,512]{2,1,0:T(8,128)(2,1)S(1)}, u32[]{:S(2)}) %copy-start.4) | copy-done | bytes 1310744
  73.9 11.1 %shard_map.173 = bf16[16,208,128]{2,1,0:T(8,128)(2,1)} custom-call(bf16[16,80,512]{2,1,0:T(8,128)(2,1)} %copy-done.4, bf16[235,64]{1,0:T(8,128)(2,1)} %constant_dynamic-slice_fusion.wig_ref, f32[1,64]{1,0:T(1,128)} %dynamic-slice_bitcast_fusion.length_ref, bf16[90,64]{1,0:T(8,128)(2,1)} %fusion.kind_ref, bf16[128,512]{1,0:T(8,128)(2,1)} %bitcast.39, ...), custom_call_target="tpu_custom_call" | custom-call | flops 637534208 | bytes 8199552 | tf_op jit(solution)/shard_map/pallas_call | solution.py:337
  84.9 0.0 copy-start.7
  84.9 19.3 %all_to_all.21 = bf16[16,208,128]{2,1,0:T(8,128)(2,1)S(1)} all-to-all(bf16[16,208,128]{2,1,0:T(8,128)(2,1)} %shard_map.173), channel_id=1, replica_groups=mesh['graph'=32,'irreps'=16] {'irreps'}, dimensions={0} | all-to-all | bytes 1703936 | tf_op jit(solution)/shard_map/all_to_all | solution.py:459
  104.3 0.1 convert_reduce_fusion
  104.4 0.1 reshape_reshape.3
  104.5 0.0 copy-done.7
  104.5 0.7 add_convert_fusion
  (9 shorter events, 0.1 us)
Async XLA Ops:
  0.0 64.4 %copy-start = (bf16[235,1024]{1,0:T(8,128)(2,1)S(1)}, bf16[235,1024]{1,0:T(8,128)(2,1)}, u32[]{:S(2)}) copy-start(bf16[235,1024]{1,0:T(8,128)(2,1)} %param.26) | copy-start | bytes 1443844
  0.0 18.6 %copy-start.12 = (f32[7,8]{1,0:T(8,128)S(1)}, f32[7,8]{1,0:T(8,128)}, u32[]{:S(2)}) copy-start(f32[7,8]{1,0:T(8,128)} %param.19) | copy-start | bytes 676
  0.0 18.7 %copy-start.11 = (s32[1024]{0:T(1024)S(1)}, s32[1024]{0:T(1024)}, u32[]{:S(2)}) copy-start(s32[1024]{0:T(1024)} %param.22) | copy-start | bytes 12292
  1.8 18.0 %copy-start.3 = (bf16[392,64]{0,1:T(8,128)(2,1)}, bf16[392,64]{0,1:T(8,128)(2,1)S(1)}, u32[]{:S(2)}) copy-start(bf16[392,64]{0,1:T(8,128)(2,1)S(1)} %copy.36) | copy-start | bytes 150532
  1.8 18.0 %copy-start.13 = (s32[8]{0:T(128)S(1)}, s32[8]{0:T(128)}, u32[]{:S(2)}) copy-start(s32[8]{0:T(128)} %constant.38) | copy-start | bytes 100
  1.8 18.0 %copy-start.2 = (bf16[7,128,8]{1,2,0:T(8,128)(2,1)S(1)}, bf16[7,128,8]{1,2,0:T(8,128)(2,1)}, u32[]{:S(2)}) copy-start(bf16[7,128,8]{1,2,0:T(8,128)(2,1)} %param.33) | copy-start | bytes 43012
  3.7 33.8 %all-to-all-start = ((bf16[32,8,392]{2,1,0:T(8,128)(2,1)}), bf16[32,8,392]{2,1,0:T(8,128)(2,1)S(1)}, u32[]{:S(2)}, u32[]{:S(2)}) async-start(bf16[32,8,392]{2,1,0:T(8,128)(2,1)} %bitcast.3), calls=%async_computation | async-start | bytes 524288 | tf_op jit(solution)/shard_map/all_to_all | solution.py:420
  37.4 0.7 copy-start.6
  41.1 7.8 %copy-start.10 = (bf16[90,128]{1,0:T(8,128)(2,1)S(1)}, bf16[90,128]{1,0:T(8,128)(2,1)}, u32[]{:S(2)}) copy-start(bf16[90,128]{1,0:T(8,128)(2,1)} %param.28) | copy-start | bytes 69124
  41.1 8.6 %copy-start.9 = (bf16[512,128]{1,0:T(8,128)(2,1)S(1)}, bf16[512,128]{1,0:T(8,128)(2,1)}, u32[]{:S(2)}) copy-start(bf16[512,128]{1,0:T(8,128)(2,1)} %param.27) | copy-start | bytes 393220
  41.2 9.4 %copy-start.8 = (bf16[128,896]{1,0:T(8,128)(2,1)S(1)}, bf16[128,896]{1,0:T(8,128)(2,1)}, u32[]{:S(2)}) copy-start(bf16[128,896]{1,0:T(8,128)(2,1)} %param.29) | copy-start | bytes 688132
  41.2 31.6 %all-to-all-start.1 = ((bf16[16,80,512]{2,1,0:T(8,128)(2,1)}), bf16[16,80,512]{2,1,0:T(8,128)(2,1)S(1)}, u32[]{:S(2)}, u32[]{:S(2)}) async-start(bf16[16,80,512]{2,1,0:T(8,128)(2,1)} %shard_map.172), calls=%async_computation.1 | async-start | bytes 2621440 | tf_op jit(solution)/shard_map/all_to_all | solution.py:438
  51.3 3.7 %copy-start.5 = (bf16[2,640,640]{2,1,0:T(8,128)(2,1)S(1)}, bf16[2,640,640]{2,1,0:T(8,128)(2,1)}, u32[]{:S(2)}) copy-start(bf16[2,640,640]{2,1,0:T(8,128)(2,1)} %param.32) | copy-start | bytes 4915204
  57.2 5.1 %copy-start.1 = (s32[64]{0:T(128)S(1)}, s32[64]{0:T(128)}, u32[]{:S(2)}) copy-start(s32[64]{0:T(128)} %param.20) | copy-start | bytes 772
  72.8 1.1 %copy-start.4 = (bf16[16,80,512]{2,1,0:T(8,128)(2,1)}, bf16[16,80,512]{2,1,0:T(8,128)(2,1)S(1)}, u32[]{:S(2)}) copy-start(bf16[16,80,512]{2,1,0:T(8,128)(2,1)S(1)} %all-to-all-done.1.src_ref) | copy-start | bytes 3932164
  84.9 19.6 %copy-start.7 = (bf16[49,8,64]{2,1,0:T(8,128)(2,1)S(1)}, bf16[49,8,64]{2,1,0:T(8,128)(2,1)}, u32[]{:S(2)}) copy-start(bf16[49,8,64]{2,1,0:T(8,128)(2,1)} %param.18) | copy-start | bytes 150532

commit v8 on v7

--- a/solution.py
+++ b/solution.py
@@ -313,15 +313,9 @@
         ).astype(out_ref.dtype)
 
 
-def convolve_edges(source, wig_mine, lengths, kind_onehot, radial_in, species_table, radial_out,
-                   order_zero, order_one, order_two, onehot, per_owner):
-    coeffs, channel_count = COEFFS, CHANNELS
-    num_edges = per_owner
-    atom_count = onehot.shape[1]
-    owners = source.shape[0]
-    out_rows = 16 * pl.cdiv(coeffs * (channel_count // owners) // 2, 16)
-    operands = (
-        source,
+def edge_operands(wig_mine, lengths, kind_onehot, radial_in, species_table, radial_out,
+                  order_zero, order_one, order_two, onehot):
+    return (
         wig_mine,
         lengths[None, :],
         kind_onehot,
@@ -333,6 +327,17 @@
         jnp.transpose(order_two, (0, 2, 1)),
         onehot,
     )
+
+
+def convolve_edges(source, side):
+    coeffs, channel_count = COEFFS, CHANNELS
+    onehot = side[-1]
+    num_edges, atom_count = onehot.shape
+    owners = source.shape[0]
+    out_rows = 16 * pl.cdiv(coeffs * (channel_count // owners) // 2, 16)
+    operands = (source,) + tuple(side)
+    radial_in, radial_out = side[4], side[6]
+    order_zero, order_one, order_two = side[7], side[8], side[9]
     flops = 2 * num_edges * (order_zero.size + 2 * order_one.size + 2 * order_two.size + radial_out.size + radial_in.size)
     return pl.pallas_call(
         conv_kernel,
@@ -341,13 +346,14 @@
         out_specs=pl.BlockSpec(memory_space=pltpu.VMEM),
         cost_estimate=pl.CostEstimate(
             flops=flops,
-            transcendentals=num_edges * (radial_in.shape[0] + 2 * channel_count),
+            transcendentals=num_edges * (radial_in.shape[1] + 2 * channel_count),
             bytes_accessed=sum(int(x.size) * x.dtype.itemsize for x in operands) + owners * out_rows * atom_count * 4,
         ),
     )(*operands)
 
 
-def gather_kernel(index_ref, local_ref, arrived_ref, extra_ref, out_ref):
+def gather_kernel(index_ref, local_ref, arrived_ref, extra_ref, *refs):
+    out_ref = refs[-1]
     owners, _, row_width = out_ref.shape
     per_owner = out_ref.shape[1] - extra_ref.shape[0]
     row_used = local_ref.shape[1]
@@ -364,13 +370,14 @@
         out_ref[q, per_owner:, :] = extra
 
 
-def gather_rows(edge_source, node_rows, arrived, extra, owners, row_width):
+def gather_rows(edge_source, node_rows, arrived, extra, owners, row_width, side):
     per_owner = edge_source.shape[0] // owners
     operands = (edge_source[:, None], node_rows, arrived, extra)
     return pl.pallas_call(
         gather_kernel,
         out_shape=jax.ShapeDtypeStruct((owners, per_owner + extra.shape[0], row_width), jnp.bfloat16),
-        in_specs=[pl.BlockSpec(memory_space=pltpu.VMEM)] * len(operands),
+        in_specs=[pl.BlockSpec(memory_space=pltpu.VMEM)] * len(operands)
+        + [pl.BlockSpec(memory_space=pl.ANY)] * len(side),
         out_specs=pl.BlockSpec(memory_space=pltpu.VMEM),
         cost_estimate=pl.CostEstimate(
             flops=2 * edge_source.shape[0] * (node_rows.shape[0] + arrived.shape[0]) * node_rows.shape[1],
@@ -378,7 +385,7 @@
             bytes_accessed=sum(int(x.size) * x.dtype.itemsize for x in operands)
             + owners * (per_owner + extra.shape[0]) * row_width * 2,
         ),
-    )(*operands)
+    )(*operands, *side)
 
 
 def split_dot(values, weight):
@@ -434,9 +441,6 @@
         2 * span_chan, 4 * CHANNELS
     )
 
-    outgoing = gather_rows(edge_source, node_rows, arrived, extra, owners, row_width)
-    source = lax.all_to_all(outgoing, "irreps", 0, 0, tiled=True)
-
     wig_mine = lax.dynamic_slice_in_dim(wigner, first_edge, per_owner, 1)
     targets_mine = lax.dynamic_slice_in_dim(edge_target, first_edge, per_owner)
     lengths_mine = lax.dynamic_slice_in_dim(edge_length, first_edge, per_owner)
@@ -452,10 +456,13 @@
         edge_weight[:, None],
         0.0,
     ).astype(jnp.bfloat16)
-    projected = convolve_edges(
-        source, wig_mine, lengths_mine, kind_onehot, radial_in, species_table, radial_out,
-        order_zero, order_one, order_two, onehot, per_owner,
-    )
+    side = edge_operands(
+        wig_mine, lengths_mine, kind_onehot, radial_in, species_table, radial_out,
+        order_zero, order_one, order_two, onehot,
+    )
+    outgoing = gather_rows(edge_source, node_rows, arrived, extra, owners, row_width, side)
+    source = lax.all_to_all(outgoing, "irreps", 0, 0, tiled=True)
+    projected = convolve_edges(source, side)
     returned = lax.all_to_all(projected, "irreps", 0, 0, tiled=True)
     total = jnp.sum(returned.astype(jnp.float32), axis=0)[: coeffs * span_chan // 2]
     total = total.reshape(coeffs, span_chan // 2, 2, atom_count).reshape(coeffs, span_chan, atom_count)

time: 106 us -> 102 us (0.962)
  blocking collectives: 19.3 us -> 48.7 us
  waiting for transfers between devices: 22.9 us -> 0.21 us
  starting transfers between devices: 22.1 us -> 14.9 us
  local copies, waits for them, and re-layouts: 21.8 us -> 18.9 us
    all_to_all x0 -> x1, blocking collectives: none -> 29.4 us  [body(): source = lax.all_to_all(outgoing, 'irreps', 0, 0, tiled=True)]
    all_to_all x1, waiting for transfers between devices: 16.5 us -> 0.21 us  [body(): arrived = lax.all_to_all(node_rows[send_list], 'graph', 0, 0, tiled=True)]
    all_to_all x1 -> x0, starting transfers between devices: 7.17 us -> none  [body(): source = lax.all_to_all(outgoing, 'irreps', 0, 0, tiled=True)]
    all_to_all x1 -> x0, waiting for transfers between devices: 6.4 us -> none  [body(): source = lax.all_to_all(outgoing, 'irreps', 0, 0, tiled=True)]
    unnamed x34, local copies, waits for them, and re-layouts: 14.4 us -> 11.5 us
  transfers between devices with their start and end apart: 2 -> 1, of which waited for: 2 -> 1; matrix products, arithmetic and copies ran while one was open for 19% -> 18% of each run, Pallas kernels for 0% -> 0%
where the time goes in v8:
time: 102 us
  blocking collectives  48.7 us (48%)
  local copies, waits for them, and re-layouts  18.9 us (19%)
  starting transfers between devices  14.9 us (15%)
  Pallas kernels  14.1 us (14%)
  other arithmetic  4.24 us (4%)
    all_to_all x1, blocking collectives, body(): source = lax.all_to_all(outgoing, 'irreps', 0, 0, tiled=True)  29.4 us
    all_to_all x1, blocking collectives, body(): returned = lax.all_to_all(projected, 'irreps', 0, 0, tiled=True)  19.3 us
    all_to_all x1, starting transfers between devices, body(): arrived = lax.all_to_all(node_rows[send_list], 'graph', 0, 0, tiled=True)  14.9 us
    unnamed x34, local copies, waits for them, and re-layouts  11.5 us
    pallas_call x1, Pallas kernels, convolve_edges(): pl.pallas_call(conv_kernel, out_shape=jax.ShapeDtypeStruct((owners, out_r...  11.1 us
    pallas_call x1, Pallas kernels, gather_rows(): pl.pallas_call(gather_kernel, out_shape=jax.ShapeDtypeStruct((owners, per...  3 us
  transfers between devices with their start and end apart: 1, of which 1 were waited for; matrix products, arithmetic and copies ran while one was open for 18% of the time, Pallas kernels for 0%

profile of v8, /device:TPU:64, one launch (start us, length us, event | category | flops | bytes accessed | tf_op | source)
XLA Modules:
  0.0 101.9 jit_solution(11352258957571227677)
XLA Ops:
  0.0 0.0 copy-start
  0.0 0.0 copy-start.13
  0.0 0.0 copy-start.12
  0.0 0.0 copy-start.10
  0.0 0.0 copy-start.9
  0.0 0.7 compare_select_fusion
  0.8 1.0 copy.36
  1.8 0.0 copy-start.3
  1.8 0.0 copy-start.8
  1.8 0.0 copy-start.11
  1.8 0.0 copy-start.5
  1.8 1.8 %gather_fusion = bf16[256,392]{1,0:T(8,128)(2,1)} fusion(bf16[64,392]{1,0:T(8,128)(2,1)S(1)} %bitcast.32, s32[1024]{0:T(1024)S(1)} %pad_clamp_fusion.2), kind=kCustom, calls=%fused_computation | custom fusion | bytes 402432 | tf_op jit(solution)/shard_map/gather | solution.py:427
  3.7 14.9 %all-to-all-start = ((bf16[32,8,392]{2,1,0:T(8,128)(2,1)}), bf16[32,8,392]{2,1,0:T(8,128)(2,1)S(1)}, u32[]{:S(2)}, u32[]{:S(2)}) async-start(bf16[32,8,392]{2,1,0:T(8,128)(2,1)} %bitcast.3), calls=%async_computation | async-start | bytes 524288 | tf_op jit(solution)/shard_map/all_to_all | solution.py:427
  19.3 0.8 compare_select_fusion.1
  20.0 0.0 copy-done.13
  20.1 0.0 copy-done.12
  20.1 0.1 copy.45
  20.2 0.0 copy-done.10
  20.2 0.7 copy.39
  20.9 0.0 copy-done.9
  20.9 0.8 copy.38
  21.7 0.0 copy-done.3
  21.7 0.0 copy-done.8
  21.7 0.9 copy.40
  22.5 0.0 copy-done.11
  22.5 1.0 copy.44.index_ref
  23.6 0.0 copy-done.5
  23.6 2.3 %copy.41 = bf16[896,896]{0,1:T(8,128)(2,1)} copy(bf16[896,896]{1,0:T(8,128)(2,1)S(1)} %copy-done.5) | data formatting | bytes 3211264 | tf_op args[12]
  25.9 0.0 copy-start.4
  25.9 3.7 %copy.43 = bf16[2,640,640]{1,2,0:T(8,128)(2,1)} copy(bf16[2,640,640]{2,1,0:T(8,128)(2,1)} %param.32) | data formatting | bytes 3276800 | tf_op args[14]
  29.5 0.0 copy-done.4
  29.5 0.0 copy-start.1
  29.5 0.0 copy-start.2
  29.5 2.5 %copy.42 = bf16[2,768,768]{1,2,0:T(8,128)(2,1)} copy(bf16[2,768,768]{2,1,0:T(8,128)(2,1)S(1)} %copy-done.4) | data formatting | bytes 4718592 | tf_op args[13]
  32.0 0.0 copy-done.1
  32.0 0.8 gather_fusion.2
  32.8 0.0 copy-done.2
  32.8 0.6 gather_fusion.1
  33.4 1.2 %dynamic-slice_bitcast_fusion.refs_1_.length_ref = f32[1,64]{1,0:T(1,128)} fusion(f32[1024]{0:T(1024)} %param.25, s32[]{:T(128)S(6)} %select_n.28), kind=kLoop, calls=%fused_computation.27 | loop fusion | bytes 516 | tf_op jit(solution)/shard_map/broadcast_in_dim | solution.py:320
  34.7 0.6 pad_maximum_fusion
  35.3 0.0 copy-done
  35.3 0.7 constant_dynamic-slice_fusion.refs_0_.wig_ref
  36.0 0.7 select_convert_fusion.refs_9_.onehot_ref
  36.7 0.6 fusion.refs_2_.kind_ref
  37.3 0.2 all-to-all-done
  37.5 0.0 copy-start.6
  37.5 0.7 copy-done.6
  38.2 3.0 %shard_map.172 = bf16[16,80,512]{2,1,0:T(8,128)(2,1)} custom-call(s32[1024,1]{1,0:T(8,128)} %copy.44.index_ref, bf16[64,392]{1,0:T(8,128)(2,1)} %bitcast.33, bf16[256,392]{1,0:T(8,128)(2,1)} %bitcast.44, bf16[16,512]{1,0:T(8,128)(2,1)} %bitcast.48, bf16[235,64]{1,0:T(8,128)(2,1)} %constant_dynamic-slice_fusion.refs_0_.wig_ref, ...), custom_call_target="tpu_custom_call" | custom-call | flops 256901120 | bytes 1582080 | tf_op jit(solution)/shard_map/pallas_call | solution.py:376
  41.2 29.4 %all_to_all.21.src_ref = bf16[16,80,512]{2,1,0:T(8,128)(2,1)} all-to-all(bf16[16,80,512]{2,1,0:T(8,128)(2,1)} %shard_map.172), channel_id=1, replica_groups=mesh['graph'=32,'irreps'=16] {'irreps'}, dimensions={0} | all-to-all | bytes 2621440 | tf_op jit(solution)/shard_map/all_to_all | solution.py:464
  70.6 11.1 %shard_map.173 = bf16[16,208,128]{2,1,0:T(8,128)(2,1)} custom-call(bf16[16,80,512]{2,1,0:T(8,128)(2,1)} %all_to_all.21.src_ref, bf16[235,64]{1,0:T(8,128)(2,1)} %constant_dynamic-slice_fusion.refs_0_.wig_ref, f32[1,64]{1,0:T(1,128)} %dynamic-slice_bitcast_fusion.refs_1_.length_ref, bf16[90,64]{1,0:T(8,128)(2,1)} %fusion.refs_2_.kind_ref, ...), custom_call_target="tpu_custom_call" | custom-call | flops 465993728 | bytes 8199552 | tf_op jit(solution)/shard_map/pallas_call | solution.py:342
  81.6 0.0 copy-start.7
  81.6 19.3 %all_to_all.22 = bf16[16,208,128]{2,1,0:T(8,128)(2,1)S(1)} all-to-all(bf16[16,208,128]{2,1,0:T(8,128)(2,1)} %shard_map.173), channel_id=1, replica_groups=mesh['graph'=32,'irreps'=16] {'irreps'}, dimensions={0} | all-to-all | bytes 1703936 | tf_op jit(solution)/shard_map/all_to_all | solution.py:466
  100.9 0.1 convert_reduce_fusion
  101.1 0.1 reshape_reshape.3
  101.2 0.0 copy-done.7
  101.2 0.7 add_convert_fusion
  (9 shorter events, 0.1 us)
Async XLA Ops:
  0.0 35.3 %copy-start = (bf16[235,1024]{1,0:T(8,128)(2,1)S(1)}, bf16[235,1024]{1,0:T(8,128)(2,1)}, u32[]{:S(2)}) copy-start(bf16[235,1024]{1,0:T(8,128)(2,1)} %param.26) | copy-start | bytes 1443844
  0.0 20.0 %copy-start.13 = (s32[8]{0:T(128)S(1)}, s32[8]{0:T(128)}, u32[]{:S(2)}) copy-start(s32[8]{0:T(128)} %constant.38) | copy-start | bytes 100
  0.0 20.0 %copy-start.12 = (f32[7,8]{1,0:T(8,128)S(1)}, f32[7,8]{1,0:T(8,128)}, u32[]{:S(2)}) copy-start(f32[7,8]{1,0:T(8,128)} %param.19) | copy-start | bytes 676
  0.0 20.2 %copy-start.10 = (bf16[90,128]{1,0:T(8,128)(2,1)S(1)}, bf16[90,128]{1,0:T(8,128)(2,1)}, u32[]{:S(2)}) copy-start(bf16[90,128]{1,0:T(8,128)(2,1)} %param.28) | copy-start | bytes 69124
  0.0 20.9 %copy-start.9 = (bf16[512,128]{1,0:T(8,128)(2,1)S(1)}, bf16[512,128]{1,0:T(8,128)(2,1)}, u32[]{:S(2)}) copy-start(bf16[512,128]{1,0:T(8,128)(2,1)} %param.27) | copy-start | bytes 393220
  1.8 19.9 %copy-start.3 = (bf16[392,64]{0,1:T(8,128)(2,1)}, bf16[392,64]{0,1:T(8,128)(2,1)S(1)}, u32[]{:S(2)}) copy-start(bf16[392,64]{0,1:T(8,128)(2,1)S(1)} %copy.36) | copy-start | bytes 150532
  1.8 19.9 %copy-start.8 = (bf16[128,896]{1,0:T(8,128)(2,1)S(1)}, bf16[128,896]{1,0:T(8,128)(2,1)}, u32[]{:S(2)}) copy-start(bf16[128,896]{1,0:T(8,128)(2,1)} %param.29) | copy-start | bytes 688132
  1.8 20.7 %copy-start.11 = (s32[1024]{0:T(1024)S(1)}, s32[1024]{0:T(1024)}, u32[]{:S(2)}) copy-start(s32[1024]{0:T(1024)} %param.22) | copy-start | bytes 12292
  1.8 21.7 %copy-start.5 = (bf16[896,896]{1,0:T(8,128)(2,1)S(1)}, bf16[896,896]{1,0:T(8,128)(2,1)}, u32[]{:S(2)}) copy-start(bf16[896,896]{1,0:T(8,128)(2,1)} %param.30) | copy-start | bytes 4816900
  3.7 33.8 %all-to-all-start = ((bf16[32,8,392]{2,1,0:T(8,128)(2,1)}), bf16[32,8,392]{2,1,0:T(8,128)(2,1)S(1)}, u32[]{:S(2)}, u32[]{:S(2)}) async-start(bf16[32,8,392]{2,1,0:T(8,128)(2,1)} %bitcast.3), calls=%async_computation | async-start | bytes 524288 | tf_op jit(solution)/shard_map/all_to_all | solution.py:427
  25.9 3.7 %copy-start.4 = (bf16[2,768,768]{2,1,0:T(8,128)(2,1)S(1)}, bf16[2,768,768]{2,1,0:T(8,128)(2,1)}, u32[]{:S(2)}) copy-start(bf16[2,768,768]{2,1,0:T(8,128)(2,1)} %param.31) | copy-start | bytes 7077892
  29.5 2.5 %copy-start.1 = (s32[64]{0:T(128)S(1)}, s32[64]{0:T(128)}, u32[]{:S(2)}) copy-start(s32[64]{0:T(128)} %param.20) | copy-start | bytes 772
  29.5 3.3 %copy-start.2 = (bf16[7,128,8]{1,2,0:T(8,128)(2,1)S(1)}, bf16[7,128,8]{1,2,0:T(8,128)(2,1)}, u32[]{:S(2)}) copy-start(bf16[7,128,8]{1,2,0:T(8,128)(2,1)} %param.33) | copy-start | bytes 43012
  37.5 0.7 copy-start.6
  81.6 19.5 %copy-start.7 = (bf16[49,8,64]{2,1,0:T(8,128)(2,1)S(1)}, bf16[49,8,64]{2,1,0:T(8,128)(2,1)}, u32[]{:S(2)}) copy-start(bf16[49,8,64]{2,1,0:T(8,128)(2,1)} %param.18) | copy-start | bytes 150532

commit v9 on v8

--- a/solution.py
+++ b/solution.py
@@ -169,38 +169,38 @@
     wig = wig_ref[...].astype(jnp.float32)
     owners = src_ref.shape[0]
     span_chan = CHANNELS // owners
+    turned = [src_ref[r].astype(jnp.float32).T for r in range(owners)]
+    base = COEFFS * span_chan
+    half = num_edges
     pick = (
-        lax.broadcasted_iota(jnp.int32, (CHANNELS, span_chan), 0) % span_chan
-        == lax.broadcasted_iota(jnp.int32, (CHANNELS, span_chan), 1)
-    ) & (lax.broadcasted_iota(jnp.int32, (CHANNELS, span_chan), 0) < 3 * span_chan)
-    pick = pick.astype(jnp.bfloat16)
+        lax.broadcasted_iota(jnp.int32, (half, span_chan), 0) % span_chan
+        == lax.broadcasted_iota(jnp.int32, (half, span_chan), 1)
+    ) & (lax.broadcasted_iota(jnp.int32, (half, span_chan), 0) < 3 * span_chan)
+    pick = pick.astype(jnp.float32)
+    gain_at = base + levels * 2 * span_chan
     gain = jnp.concatenate(
         [
-            jnp.dot(
-                src_ref[r, num_edges + span_chan : num_edges + 2 * span_chan, 3 * CHANNELS : 4 * CHANNELS],
-                pick,
-                preferred_element_type=jnp.float32,
-            )
-            for r in range(owners)
+            jnp.dot(block[gain_at : gain_at + span_chan], pick, preferred_element_type=jnp.float32)
+            for block in turned
         ],
         axis=0,
     )
-    projection = [
-        jnp.concatenate(
-            [
-                src_ref[
-                    r,
-                    num_edges + (degree // 4) * span_chan : num_edges + (degree // 4 + 1) * span_chan,
-                    (degree % 4) * CHANNELS : (degree % 4 + 1) * CHANNELS,
-                ].astype(jnp.float32)
-                for r in range(owners)
-            ],
-            axis=0,
-        ).astype(jnp.bfloat16)
-        for degree in range(levels)
-    ]
-
-    turned = [src_ref[r, 0:num_edges].astype(jnp.float32).T for r in range(owners)]
+    projection = []
+    for degree in range(levels):
+        start = base + degree * 2 * span_chan
+        projection.append(
+            jnp.concatenate(
+                [
+                    jnp.concatenate(
+                        [block[start : start + span_chan], block[start + span_chan : start + 2 * span_chan]],
+                        axis=1,
+                    )
+                    for block in turned
+                ],
+                axis=0,
+            ).astype(jnp.bfloat16)
+        )
+
     rows = [
         jnp.concatenate([block[j * span_chan : (j + 1) * span_chan] for block in turned], axis=0)
         for j in range(COEFFS)
@@ -354,20 +354,17 @@
 
 def gather_kernel(index_ref, local_ref, arrived_ref, extra_ref, *refs):
     out_ref = refs[-1]
-    owners, _, row_width = out_ref.shape
-    per_owner = out_ref.shape[1] - extra_ref.shape[0]
+    owners, per_owner, row_width = out_ref.shape
     row_used = local_ref.shape[1]
     table = jnp.concatenate([local_ref[...], arrived_ref[...]], axis=0)
     hot = (
         index_ref[...] == lax.broadcasted_iota(jnp.int32, (index_ref.shape[0], table.shape[0]), 1)
     ).astype(jnp.bfloat16)
     picked = jnp.dot(hot, table, preferred_element_type=jnp.float32).astype(out_ref.dtype)
-    blank = jnp.zeros((per_owner, row_width - row_used), out_ref.dtype)
     extra = extra_ref[...]
     for q in range(owners):
-        out_ref[q, 0:per_owner, 0:row_used] = picked[q * per_owner : (q + 1) * per_owner]
-        out_ref[q, 0:per_owner, row_used:row_width] = blank
-        out_ref[q, per_owner:, :] = extra
+        out_ref[q, :, 0:row_used] = picked[q * per_owner : (q + 1) * per_owner]
+        out_ref[q, :, row_used:row_width] = extra
 
 
 def gather_rows(edge_source, node_rows, arrived, extra, owners, row_width, side):
@@ -375,7 +372,7 @@
     operands = (edge_source[:, None], node_rows, arrived, extra)
     return pl.pallas_call(
         gather_kernel,
-        out_shape=jax.ShapeDtypeStruct((owners, per_owner + extra.shape[0], row_width), jnp.bfloat16),
+        out_shape=jax.ShapeDtypeStruct((owners, per_owner, row_width), jnp.bfloat16),
         in_specs=[pl.BlockSpec(memory_space=pltpu.VMEM)] * len(operands)
         + [pl.BlockSpec(memory_space=pl.ANY)] * len(side),
         out_specs=pl.BlockSpec(memory_space=pltpu.VMEM),
@@ -383,7 +380,7 @@
             flops=2 * edge_source.shape[0] * (node_rows.shape[0] + arrived.shape[0]) * node_rows.shape[1],
             transcendentals=0,
             bytes_accessed=sum(int(x.size) * x.dtype.itemsize for x in operands)
-            + owners * (per_owner + extra.shape[0]) * row_width * 2,
+            + owners * per_owner * row_width * 2,
         ),
     )(*operands, *side)
 
@@ -432,14 +429,12 @@
     gain_low = gain_rest - gain_mid
     gain_block = jnp.transpose(jnp.stack([gain_high, gain_mid, gain_low]), (2, 0, 1))
     gain_block = jnp.pad(gain_block, ((0, 0), (0, 0), (0, 1))).reshape(span_chan, 3 * (levels + 1))
-    gain_block = jnp.pad(gain_block, ((0, 0), (0, CHANNELS - gain_block.shape[1]))).astype(jnp.bfloat16)
+    gain_block = jnp.pad(gain_block, ((0, 0), (0, per_owner - gain_block.shape[1]))).astype(jnp.bfloat16)
     pair_order = np.concatenate([np.arange(0, span_chan, 2), np.arange(1, span_chan, 2)])
-    weight_block = jnp.concatenate(
-        [jnp.transpose(project_weight[:, :, pair_order], (2, 0, 1)), gain_block[:, None, :]], axis=1
-    )
-    extra = jnp.transpose(weight_block.reshape(span_chan, 2, 4, CHANNELS), (1, 0, 2, 3)).reshape(
-        2 * span_chan, 4 * CHANNELS
-    )
+    weight_block = jnp.transpose(
+        project_weight[:, :, pair_order].reshape(levels, CHANNELS // per_owner, per_owner, span_chan), (0, 1, 3, 2)
+    ).reshape(-1, per_owner)
+    extra = jnp.concatenate([weight_block, gain_block], axis=0).T
 
     wig_mine = lax.dynamic_slice_in_dim(wigner, first_edge, per_owner, 1)
     targets_mine = lax.dynamic_slice_in_dim(edge_target, first_edge, per_owner)

time: 102 us -> 99.5 us (0.975)
  blocking collectives: 48.7 us -> 45.6 us
    all_to_all x1, blocking collectives: 29.4 us -> 26.3 us  [body(): source = lax.all_to_all(outgoing, 'irreps', 0, 0, tiled=True)]
  transfers between devices with their start and end apart: 1 -> 1, of which waited for: 1 -> 0; matrix products, arithmetic and copies ran while one was open for 18% -> 18% of each run, Pallas kernels for 0% -> 0%
where the time goes in v9:
time: 99.5 us; the launch traced here: 99 us
  blocking collectives  45.6 us (46%)
  local copies, waits for them, and re-layouts  19.1 us (19%)
  starting transfers between devices  15 us (15%)
  Pallas kernels  14.1 us (14%)
  other arithmetic  4.3 us (4%)
    all_to_all x1, blocking collectives, body(): source = lax.all_to_all(outgoing, 'irreps', 0, 0, tiled=True)  26.3 us
    all_to_all x1, blocking collectives, body(): returned = lax.all_to_all(projected, 'irreps', 0, 0, tiled=True)  19.3 us
    all_to_all x1, starting transfers between devices, body(): arrived = lax.all_to_all(node_rows[send_list], 'graph', 0, 0, tiled=True)  15 us
    unnamed x34, local copies, waits for them, and re-layouts  11.5 us
    pallas_call x1, Pallas kernels, convolve_edges(): pl.pallas_call(conv_kernel, out_shape=jax.ShapeDtypeStruct((owners, out_r...  11.3 us
    pallas_call x1, Pallas kernels, gather_rows(): pl.pallas_call(gather_kernel, out_shape=jax.ShapeDtypeStruct((owners, per...  2.87 us
  transfers between devices with their start and end apart: 1, of which 0 were waited for; matrix products, arithmetic and copies ran while one was open for 18% of the time, Pallas kernels for 0%

profile of v9, /device:TPU:64, one launch (start us, length us, event | category | flops | bytes accessed | tf_op | source)
XLA Modules:
  0.0 99.0 jit_solution(14463329576168577945)
XLA Ops:
  0.0 0.0 copy-start
  0.0 0.0 copy-start.13
  0.0 0.0 copy-start.12
  0.0 0.0 copy-start.2
  0.0 0.7 compare_select_fusion
  0.8 1.0 %copy.27 = bf16[392,64]{0,1:T(8,128)(2,1)S(1)} copy(bf16[392,64]{1,0:T(8,128)(2,1)} %bitcast.47) | data formatting | bytes 100352 | tf_op jit(solution)/shard_map/reshape | solution.py:423
  1.8 0.0 copy-start.3
  1.8 1.8 %gather_fusion = bf16[256,392]{1,0:T(8,128)(2,1)} fusion(bf16[64,392]{1,0:T(8,128)(2,1)S(1)} %bitcast.33, s32[1024]{0:T(1024)S(1)} %pad_clamp_fusion.2), kind=kCustom, calls=%fused_computation | custom fusion | bytes 402432 | tf_op jit(solution)/shard_map/gather | solution.py:424
  3.6 0.0 copy-start.10
  3.6 0.0 copy-start.9
  3.6 0.0 copy-start.8
  3.6 15.0 %all-to-all-start = ((bf16[32,8,392]{2,1,0:T(8,128)(2,1)}), bf16[32,8,392]{2,1,0:T(8,128)(2,1)S(1)}, u32[]{:S(2)}, u32[]{:S(2)}) async-start(bf16[32,8,392]{2,1,0:T(8,128)(2,1)} %bitcast.3), calls=%async_computation | async-start | bytes 524288 | tf_op jit(solution)/shard_map/all_to_all | solution.py:424
  18.7 0.0 copy-start.11
  19.4 0.8 compare_select_fusion.1
  20.1 0.0 copy-done.13
  20.2 0.0 copy-done.12
  20.2 0.0 copy-done.2
  20.2 0.0 copy-start.5
  20.2 0.6 gather_fusion.1
  20.8 0.0 copy-done.3
  20.8 0.1 reshape.24
  20.9 0.1 copy.29
  21.0 0.0 copy-done.10
  21.0 0.7 copy.31
  21.8 0.0 copy-done.9
  21.8 0.8 copy.30
  22.5 0.0 copy-done.8
  22.5 0.8 copy.32
  23.4 0.0 copy-done.11
  23.4 1.0 %copy.36.index_ref = s32[1024,1]{1,0:T(8,128)} copy(s32[1024,1]{0,1:T(1,128)S(1)} %bitcast.51) | data formatting | bytes 8192 | tf_op jit(solution)/shard_map/broadcast_in_dim | solution.py:372
  24.4 0.0 copy-done.5
  24.4 2.3 %copy.33 = bf16[896,896]{0,1:T(8,128)(2,1)} copy(bf16[896,896]{1,0:T(8,128)(2,1)S(1)} %copy-done.5) | data formatting | bytes 3211264 | tf_op args[12]
  26.7 0.0 copy-start.4
  26.7 3.7 %copy.35 = bf16[2,640,640]{1,2,0:T(8,128)(2,1)} copy(bf16[2,640,640]{2,1,0:T(8,128)(2,1)} %param.32) | data formatting | bytes 3276800 | tf_op args[14]
  30.4 0.0 copy-done.4
  30.4 0.0 copy-start.1
  30.4 2.5 %copy.34 = bf16[2,768,768]{1,2,0:T(8,128)(2,1)} copy(bf16[2,768,768]{2,1,0:T(8,128)(2,1)S(1)} %copy-done.4) | data formatting | bytes 4718592 | tf_op args[13]
  32.8 0.0 copy-done.1
  32.8 0.8 gather_fusion.2
  33.6 1.3 %dynamic-slice_bitcast_fusion.refs_1_.length_ref = f32[1,64]{1,0:T(1,128)} fusion(f32[1024]{0:T(1024)} %param.25, s32[]{:T(128)S(6)} %select_n.28), kind=kLoop, calls=%fused_computation.29 | loop fusion | bytes 516 | tf_op jit(solution)/shard_map/broadcast_in_dim | solution.py:320
  35.0 0.7 fusion.3.extra_ref
  35.6 0.0 copy-done
  35.6 0.7 constant_dynamic-slice_fusion.refs_0_.wig_ref
  36.4 0.7 select_convert_fusion.refs_9_.onehot_ref
  37.0 0.6 fusion.refs_2_.kind_ref
  37.7 0.0 all-to-all-done
  37.7 0.0 copy-start.6
  37.7 0.7 copy-done.6
  38.3 2.9 %shard_map.172 = bf16[16,64,512]{2,1,0:T(8,128)(2,1)} custom-call(s32[1024,1]{1,0:T(8,128)} %copy.36.index_ref, bf16[64,392]{1,0:T(8,128)(2,1)} %bitcast.34, bf16[256,392]{1,0:T(8,128)(2,1)} %bitcast.46, bf16[64,120]{1,0:T(8,128)(2,1)} %fusion.3.extra_ref, bf16[235,64]{1,0:T(8,128)(2,1)} %constant_dynamic-slice_fusion.refs_0_.wig_ref, ...), custom_call_target="tpu_custom_call" | custom-call | flops 256901120 | bytes 1318912 | tf_op jit(solution)/shard_map/pallas_call | solution.py:373
  41.2 26.3 %all_to_all.21.src_ref = bf16[16,64,512]{2,1,0:T(8,128)(2,1)} all-to-all(bf16[16,64,512]{2,1,0:T(8,128)(2,1)} %shard_map.172), channel_id=1, replica_groups=mesh['graph'=32,'irreps'=16] {'irreps'}, dimensions={0} | all-to-all | bytes 2097152 | tf_op jit(solution)/shard_map/all_to_all | solution.py:459
  67.6 11.3 %shard_map.173 = bf16[16,208,128]{2,1,0:T(8,128)(2,1)} custom-call(bf16[16,64,512]{2,1,0:T(8,128)(2,1)} %all_to_all.21.src_ref, bf16[235,64]{1,0:T(8,128)(2,1)} %constant_dynamic-slice_fusion.refs_0_.wig_ref, f32[1,64]{1,0:T(1,128)} %dynamic-slice_bitcast_fusion.refs_1_.length_ref, bf16[90,64]{1,0:T(8,128)(2,1)} %fusion.refs_2_.kind_ref, ...), custom_call_target="tpu_custom_call" | custom-call | flops 465993728 | bytes 7937408 | tf_op jit(solution)/shard_map/pallas_call | solution.py:342
  78.8 0.0 copy-start.7
  78.8 19.3 %all_to_all.22 = bf16[16,208,128]{2,1,0:T(8,128)(2,1)S(1)} all-to-all(bf16[16,208,128]{2,1,0:T(8,128)(2,1)} %shard_map.173), channel_id=1, replica_groups=mesh['graph'=32,'irreps'=16] {'irreps'}, dimensions={0} | all-to-all | bytes 1703936 | tf_op jit(solution)/shard_map/all_to_all | solution.py:461
  98.1 0.1 convert_reduce_fusion
  98.2 0.1 reshape_reshape.3
  98.3 0.0 copy-done.7
  98.3 0.7 add_convert_fusion
  (9 shorter events, 0.1 us)
Async XLA Ops:
  0.0 35.6 %copy-start = (bf16[235,1024]{1,0:T(8,128)(2,1)S(1)}, bf16[235,1024]{1,0:T(8,128)(2,1)}, u32[]{:S(2)}) copy-start(bf16[235,1024]{1,0:T(8,128)(2,1)} %param.26) | copy-start | bytes 1443844
  0.0 20.1 %copy-start.13 = (s32[8]{0:T(128)S(1)}, s32[8]{0:T(128)}, u32[]{:S(2)}) copy-start(s32[8]{0:T(128)} %constant.38) | copy-start | bytes 100
  0.0 20.2 %copy-start.12 = (f32[7,8]{1,0:T(8,128)S(1)}, f32[7,8]{1,0:T(8,128)}, u32[]{:S(2)}) copy-start(f32[7,8]{1,0:T(8,128)} %param.19) | copy-start | bytes 676
  0.0 20.2 %copy-start.2 = (bf16[7,128,8]{1,2,0:T(8,128)(2,1)S(1)}, bf16[7,128,8]{1,2,0:T(8,128)(2,1)}, u32[]{:S(2)}) copy-start(bf16[7,128,8]{1,2,0:T(8,128)(2,1)} %param.33) | copy-start | bytes 43012
  1.8 19.1 %copy-start.3 = (bf16[392,64]{0,1:T(8,128)(2,1)}, bf16[392,64]{0,1:T(8,128)(2,1)S(1)}, u32[]{:S(2)}) copy-start(bf16[392,64]{0,1:T(8,128)(2,1)S(1)} %copy.27) | copy-start | bytes 150532
  3.6 17.4 %copy-start.10 = (bf16[90,128]{1,0:T(8,128)(2,1)S(1)}, bf16[90,128]{1,0:T(8,128)(2,1)}, u32[]{:S(2)}) copy-start(bf16[90,128]{1,0:T(8,128)(2,1)} %param.28) | copy-start | bytes 69124
  3.6 18.1 %copy-start.9 = (bf16[512,128]{1,0:T(8,128)(2,1)S(1)}, bf16[512,128]{1,0:T(8,128)(2,1)}, u32[]{:S(2)}) copy-start(bf16[512,128]{1,0:T(8,128)(2,1)} %param.27) | copy-start | bytes 393220
  3.6 18.9 %copy-start.8 = (bf16[128,896]{1,0:T(8,128)(2,1)S(1)}, bf16[128,896]{1,0:T(8,128)(2,1)}, u32[]{:S(2)}) copy-start(bf16[128,896]{1,0:T(8,128)(2,1)} %param.29) | copy-start | bytes 688132
  3.6 34.0 %all-to-all-start = ((bf16[32,8,392]{2,1,0:T(8,128)(2,1)}), bf16[32,8,392]{2,1,0:T(8,128)(2,1)S(1)}, u32[]{:S(2)}, u32[]{:S(2)}) async-start(bf16[32,8,392]{2,1,0:T(8,128)(2,1)} %bitcast.3), calls=%async_computation | async-start | bytes 524288 | tf_op jit(solution)/shard_map/all_to_all | solution.py:424
  18.7 4.7 %copy-start.11 = (s32[1024]{0:T(1024)S(1)}, s32[1024]{0:T(1024)}, u32[]{:S(2)}) copy-start(s32[1024]{0:T(1024)} %param.22) | copy-start | bytes 12292
  20.2 4.2 %copy-start.5 = (bf16[896,896]{1,0:T(8,128)(2,1)S(1)}, bf16[896,896]{1,0:T(8,128)(2,1)}, u32[]{:S(2)}) copy-start(bf16[896,896]{1,0:T(8,128)(2,1)} %param.30) | copy-start | bytes 4816900
  26.7 3.7 %copy-start.4 = (bf16[2,768,768]{2,1,0:T(8,128)(2,1)S(1)}, bf16[2,768,768]{2,1,0:T(8,128)(2,1)}, u32[]{:S(2)}) copy-start(bf16[2,768,768]{2,1,0:T(8,128)(2,1)} %param.31) | copy-start | bytes 7077892
  30.4 2.5 %copy-start.1 = (s32[64]{0:T(128)S(1)}, s32[64]{0:T(128)}, u32[]{:S(2)}) copy-start(s32[64]{0:T(128)} %param.20) | copy-start | bytes 772
  37.7 0.7 copy-start.6
  78.8 19.5 %copy-start.7 = (bf16[49,8,64]{2,1,0:T(8,128)(2,1)S(1)}, bf16[49,8,64]{2,1,0:T(8,128)(2,1)}, u32[]{:S(2)}) copy-start(bf16[49,8,64]{2,1,0:T(8,128)(2,1)} %param.18) | copy-start | bytes 150532

commit v10 on v9

--- a/solution.py
+++ b/solution.py
@@ -160,8 +160,15 @@
 
 def conv_kernel(
     src_ref, wig_ref, length_ref, kind_ref, basis_in_ref, kind_table_ref, radial_out_ref,
-    zero_ref, one_ref, two_ref, onehot_ref, out_ref,
+    zero_hbm, one_hbm, two_hbm, onehot_ref, out_ref, zero_ref, one_ref, two_ref, copy_sems,
 ):
+    loads = [
+        pltpu.make_async_copy(zero_hbm, zero_ref, copy_sems.at[0]),
+        pltpu.make_async_copy(one_hbm, one_ref, copy_sems.at[1]),
+        pltpu.make_async_copy(two_hbm, two_ref, copy_sems.at[2]),
+    ]
+    for load in loads:
+        load.start()
     levels = MAX_DEGREE + 1
     channel_count = CHANNELS
     num_edges = onehot_ref.shape[0]
@@ -250,10 +257,12 @@
         ],
         axis=0,
     )
+    loads[0].wait()
     mixed0 = jnp.dot(zero_ref[...], lowest, preferred_element_type=jnp.float32)
     mixed = [mixed0[degree * channel_count : (degree + 1) * channel_count] for degree in range(levels)]
     first_row = levels
-    for harmonic, weight_ref in ((1, one_ref), (2, two_ref)):
+    for harmonic, weight_ref, load in ((1, one_ref, loads[1]), (2, two_ref, loads[2])):
+        load.wait()
         span_rows = levels - harmonic
         plus_rows = jnp.concatenate(rotated[first_row : first_row + span_rows], axis=0)
         minus_rows = jnp.concatenate(rotated[first_row + span_rows : first_row + 2 * span_rows], axis=0)
@@ -336,14 +345,22 @@
     owners = source.shape[0]
     out_rows = 16 * pl.cdiv(coeffs * (channel_count // owners) // 2, 16)
     operands = (source,) + tuple(side)
-    radial_in, radial_out = side[4], side[6]
-    order_zero, order_one, order_two = side[7], side[8], side[9]
+    radial_in, radial_out = side[3], side[5]
+    order_zero, order_one, order_two = side[6], side[7], side[8]
     flops = 2 * num_edges * (order_zero.size + 2 * order_one.size + 2 * order_two.size + radial_out.size + radial_in.size)
     return pl.pallas_call(
         conv_kernel,
         out_shape=jax.ShapeDtypeStruct((owners, out_rows, 2 * atom_count), jnp.bfloat16),
-        in_specs=[pl.BlockSpec(memory_space=pltpu.VMEM)] * len(operands),
+        in_specs=[pl.BlockSpec(memory_space=pltpu.VMEM)] * 7
+        + [pl.BlockSpec(memory_space=pl.ANY)] * 3
+        + [pl.BlockSpec(memory_space=pltpu.VMEM)],
         out_specs=pl.BlockSpec(memory_space=pltpu.VMEM),
+        scratch_shapes=[
+            pltpu.VMEM(order_zero.shape, order_zero.dtype),
+            pltpu.VMEM(order_one.shape, order_one.dtype),
+            pltpu.VMEM(order_two.shape, order_two.dtype),
+            pltpu.SemaphoreType.DMA((3,)),
+        ],
         cost_estimate=pl.CostEstimate(
             flops=flops,
             transcendentals=num_edges * (radial_in.shape[1] + 2 * channel_count),

time: 99.5 us -> 99.7 us (level)
  no operation moved by 1% of the time
where the time goes in v10:
time: 99.7 us; the launch traced here: 99.1 us
  blocking collectives  45.6 us (46%)
  local copies, waits for them, and re-layouts  19.1 us (19%)
  starting transfers between devices  15 us (15%)
  Pallas kernels  14.3 us (14%)
  other arithmetic  4.3 us (4%)
    all_to_all x1, blocking collectives, body(): source = lax.all_to_all(outgoing, 'irreps', 0, 0, tiled=True)  26.3 us
    all_to_all x1, blocking collectives, body(): returned = lax.all_to_all(projected, 'irreps', 0, 0, tiled=True)  19.3 us
    all_to_all x1, starting transfers between devices, body(): arrived = lax.all_to_all(node_rows[send_list], 'graph', 0, 0, tiled=True)  15 us
    unnamed x34, local copies, waits for them, and re-layouts  11.5 us
    pallas_call x1, Pallas kernels, convolve_edges(): pl.pallas_call(conv_kernel, out_shape=jax.ShapeDtypeStruct((owners, out_r...  11.4 us
    pallas_call x1, Pallas kernels, gather_rows(): pl.pallas_call(gather_kernel, out_shape=jax.ShapeDtypeStruct((owners, per...  2.87 us
  transfers between devices with their start and end apart: 1, of which 0 were waited for; matrix products, arithmetic and copies ran while one was open for 18% of the time, Pallas kernels for 0%

profile of v10, /device:TPU:64, one launch (start us, length us, event | category | flops | bytes accessed | tf_op | source)
XLA Modules:
  0.0 99.1 jit_solution(14051385790626463181)
XLA Ops:
  0.0 0.0 copy-start
  0.0 0.0 copy-start.13
  0.0 0.0 copy-start.12
  0.0 0.0 copy-start.2
  0.0 0.7 compare_select_fusion
  0.8 1.0 %copy.27 = bf16[392,64]{0,1:T(8,128)(2,1)S(1)} copy(bf16[392,64]{1,0:T(8,128)(2,1)} %bitcast.47) | data formatting | bytes 100352 | tf_op jit(solution)/shard_map/reshape | solution.py:440
  1.8 0.0 copy-start.3
  1.8 1.8 %gather_fusion = bf16[256,392]{1,0:T(8,128)(2,1)} fusion(bf16[64,392]{1,0:T(8,128)(2,1)S(1)} %bitcast.33, s32[1024]{0:T(1024)S(1)} %pad_clamp_fusion.2), kind=kCustom, calls=%fused_computation | custom fusion | bytes 402432 | tf_op jit(solution)/shard_map/gather | solution.py:441
  3.6 0.0 copy-start.10
  3.6 0.0 copy-start.9
  3.6 0.0 copy-start.8
  3.6 15.0 %all-to-all-start = ((bf16[32,8,392]{2,1,0:T(8,128)(2,1)}), bf16[32,8,392]{2,1,0:T(8,128)(2,1)S(1)}, u32[]{:S(2)}, u32[]{:S(2)}) async-start(bf16[32,8,392]{2,1,0:T(8,128)(2,1)} %bitcast.3), calls=%async_computation | async-start | bytes 524288 | tf_op jit(solution)/shard_map/all_to_all | solution.py:441
  18.7 0.0 copy-start.11
  19.4 0.8 compare_select_fusion.1
  20.1 0.0 copy-done.13
  20.2 0.0 copy-done.12
  20.2 0.0 copy-done.2
  20.2 0.0 copy-start.5
  20.2 0.6 gather_fusion.1
  20.8 0.0 copy-done.3
  20.8 0.1 reshape.24
  20.9 0.1 copy.29
  21.0 0.0 copy-done.10
  21.0 0.7 copy.31
  21.8 0.0 copy-done.9
  21.8 0.8 copy.30
  22.5 0.0 copy-done.8
  22.5 0.8 copy.32
  23.4 0.0 copy-done.11
  23.4 1.0 %copy.36.index_ref = s32[1024,1]{1,0:T(8,128)} copy(s32[1024,1]{0,1:T(1,128)S(1)} %bitcast.51) | data formatting | bytes 8192 | tf_op jit(solution)/shard_map/broadcast_in_dim | solution.py:389
  24.4 0.0 copy-done.5
  24.4 2.3 %copy.33 = bf16[896,896]{0,1:T(8,128)(2,1)} copy(bf16[896,896]{1,0:T(8,128)(2,1)S(1)} %copy-done.5) | data formatting | bytes 3211264 | tf_op args[12]
  26.7 0.0 copy-start.4
  26.7 3.7 %copy.35 = bf16[2,640,640]{1,2,0:T(8,128)(2,1)} copy(bf16[2,640,640]{2,1,0:T(8,128)(2,1)} %param.32) | data formatting | bytes 3276800 | tf_op args[14]
  30.4 0.0 copy-done.4
  30.4 0.0 copy-start.1
  30.4 2.5 %copy.34 = bf16[2,768,768]{1,2,0:T(8,128)(2,1)} copy(bf16[2,768,768]{2,1,0:T(8,128)(2,1)S(1)} %copy-done.4) | data formatting | bytes 4718592 | tf_op args[13]
  32.8 0.0 copy-done.1
  32.8 0.8 gather_fusion.2
  33.6 1.3 %dynamic-slice_bitcast_fusion.refs_1_.length_ref = f32[1,64]{1,0:T(1,128)} fusion(f32[1024]{0:T(1024)} %param.25, s32[]{:T(128)S(6)} %select_n.28), kind=kLoop, calls=%fused_computation.29 | loop fusion | bytes 516 | tf_op jit(solution)/shard_map/broadcast_in_dim | solution.py:329
  35.0 0.7 fusion.3.extra_ref
  35.6 0.0 copy-done
  35.6 0.7 constant_dynamic-slice_fusion.refs_0_.wig_ref
  36.4 0.7 select_convert_fusion.refs_9_.onehot_ref
  37.0 0.6 fusion.refs_2_.kind_ref
  37.7 0.0 all-to-all-done
  37.7 0.0 copy-start.6
  37.7 0.7 copy-done.6
  38.3 2.9 %shard_map.172 = bf16[16,64,512]{2,1,0:T(8,128)(2,1)} custom-call(s32[1024,1]{1,0:T(8,128)} %copy.36.index_ref, bf16[64,392]{1,0:T(8,128)(2,1)} %bitcast.34, bf16[256,392]{1,0:T(8,128)(2,1)} %bitcast.46, bf16[64,120]{1,0:T(8,128)(2,1)} %fusion.3.extra_ref, bf16[235,64]{1,0:T(8,128)(2,1)} %constant_dynamic-slice_fusion.refs_0_.wig_ref, ...), custom_call_target="tpu_custom_call" | custom-call | flops 256901120 | bytes 1318912 | tf_op jit(solution)/shard_map/pallas_call | solution.py:390
  41.2 26.3 %all_to_all.21.src_ref = bf16[16,64,512]{2,1,0:T(8,128)(2,1)} all-to-all(bf16[16,64,512]{2,1,0:T(8,128)(2,1)} %shard_map.172), channel_id=1, replica_groups=mesh['graph'=32,'irreps'=16] {'irreps'}, dimensions={0} | all-to-all | bytes 2097152 | tf_op jit(solution)/shard_map/all_to_all | solution.py:476
  67.6 11.4 %shard_map.173 = bf16[16,208,128]{2,1,0:T(8,128)(2,1)} custom-call(bf16[16,64,512]{2,1,0:T(8,128)(2,1)} %all_to_all.21.src_ref, bf16[235,64]{1,0:T(8,128)(2,1)} %constant_dynamic-slice_fusion.refs_0_.wig_ref, f32[1,64]{1,0:T(1,128)} %dynamic-slice_bitcast_fusion.refs_1_.length_ref, bf16[90,64]{1,0:T(8,128)(2,1)} %fusion.refs_2_.kind_ref, ...), custom_call_target="tpu_custom_call" | custom-call | flops 637534208 | bytes 7937408 | tf_op jit(solution)/shard_map/pallas_call | solution.py:351
  79.0 0.0 copy-start.7
  79.0 19.3 %all_to_all.22 = bf16[16,208,128]{2,1,0:T(8,128)(2,1)S(1)} all-to-all(bf16[16,208,128]{2,1,0:T(8,128)(2,1)} %shard_map.173), channel_id=1, replica_groups=mesh['graph'=32,'irreps'=16] {'irreps'}, dimensions={0} | all-to-all | bytes 1703936 | tf_op jit(solution)/shard_map/all_to_all | solution.py:478
  98.2 0.1 convert_reduce_fusion
  98.4 0.1 reshape_reshape.3
  98.5 0.0 copy-done.7
  98.5 0.7 add_convert_fusion
  (9 shorter events, 0.1 us)
Async XLA Ops:
  0.0 35.6 %copy-start = (bf16[235,1024]{1,0:T(8,128)(2,1)S(1)}, bf16[235,1024]{1,0:T(8,128)(2,1)}, u32[]{:S(2)}) copy-start(bf16[235,1024]{1,0:T(8,128)(2,1)} %param.26) | copy-start | bytes 1443844
  0.0 20.1 %copy-start.13 = (s32[8]{0:T(128)S(1)}, s32[8]{0:T(128)}, u32[]{:S(2)}) copy-start(s32[8]{0:T(128)} %constant.38) | copy-start | bytes 100
  0.0 20.2 %copy-start.12 = (f32[7,8]{1,0:T(8,128)S(1)}, f32[7,8]{1,0:T(8,128)}, u32[]{:S(2)}) copy-start(f32[7,8]{1,0:T(8,128)} %param.19) | copy-start | bytes 676
  0.0 20.2 %copy-start.2 = (bf16[7,128,8]{1,2,0:T(8,128)(2,1)S(1)}, bf16[7,128,8]{1,2,0:T(8,128)(2,1)}, u32[]{:S(2)}) copy-start(bf16[7,128,8]{1,2,0:T(8,128)(2,1)} %param.33) | copy-start | bytes 43012
  1.8 19.1 %copy-start.3 = (bf16[392,64]{0,1:T(8,128)(2,1)}, bf16[392,64]{0,1:T(8,128)(2,1)S(1)}, u32[]{:S(2)}) copy-start(bf16[392,64]{0,1:T(8,128)(2,1)S(1)} %copy.27) | copy-start | bytes 150532
  3.6 17.4 %copy-start.10 = (bf16[90,128]{1,0:T(8,128)(2,1)S(1)}, bf16[90,128]{1,0:T(8,128)(2,1)}, u32[]{:S(2)}) copy-start(bf16[90,128]{1,0:T(8,128)(2,1)} %param.28) | copy-start | bytes 69124
  3.6 18.1 %copy-start.9 = (bf16[512,128]{1,0:T(8,128)(2,1)S(1)}, bf16[512,128]{1,0:T(8,128)(2,1)}, u32[]{:S(2)}) copy-start(bf16[512,128]{1,0:T(8,128)(2,1)} %param.27) | copy-start | bytes 393220
  3.6 18.9 %copy-start.8 = (bf16[128,896]{1,0:T(8,128)(2,1)S(1)}, bf16[128,896]{1,0:T(8,128)(2,1)}, u32[]{:S(2)}) copy-start(bf16[128,896]{1,0:T(8,128)(2,1)} %param.29) | copy-start | bytes 688132
  3.6 34.0 %all-to-all-start = ((bf16[32,8,392]{2,1,0:T(8,128)(2,1)}), bf16[32,8,392]{2,1,0:T(8,128)(2,1)S(1)}, u32[]{:S(2)}, u32[]{:S(2)}) async-start(bf16[32,8,392]{2,1,0:T(8,128)(2,1)} %bitcast.3), calls=%async_computation | async-start | bytes 524288 | tf_op jit(solution)/shard_map/all_to_all | solution.py:441
  18.7 4.7 %copy-start.11 = (s32[1024]{0:T(1024)S(1)}, s32[1024]{0:T(1024)}, u32[]{:S(2)}) copy-start(s32[1024]{0:T(1024)} %param.22) | copy-start | bytes 12292
  20.2 4.2 %copy-start.5 = (bf16[896,896]{1,0:T(8,128)(2,1)S(1)}, bf16[896,896]{1,0:T(8,128)(2,1)}, u32[]{:S(2)}) copy-start(bf16[896,896]{1,0:T(8,128)(2,1)} %param.30) | copy-start | bytes 4816900
  26.7 3.7 %copy-start.4 = (bf16[2,768,768]{2,1,0:T(8,128)(2,1)S(1)}, bf16[2,768,768]{2,1,0:T(8,128)(2,1)}, u32[]{:S(2)}) copy-start(bf16[2,768,768]{2,1,0:T(8,128)(2,1)} %param.31) | copy-start | bytes 7077892
  30.4 2.5 %copy-start.1 = (s32[64]{0:T(128)S(1)}, s32[64]{0:T(128)}, u32[]{:S(2)}) copy-start(s32[64]{0:T(128)} %param.20) | copy-start | bytes 772
  37.7 0.7 copy-start.6
  79.0 19.5 %copy-start.7 = (bf16[49,8,64]{2,1,0:T(8,128)(2,1)S(1)}, bf16[49,8,64]{2,1,0:T(8,128)(2,1)}, u32[]{:S(2)}) copy-start(bf16[49,8,64]{2,1,0:T(8,128)(2,1)} %param.18) | copy-start | bytes 150532

commit v11 on v10

--- a/solution.py
+++ b/solution.py
@@ -266,12 +266,11 @@
         span_rows = levels - harmonic
         plus_rows = jnp.concatenate(rotated[first_row : first_row + span_rows], axis=0)
         minus_rows = jnp.concatenate(rotated[first_row + span_rows : first_row + 2 * span_rows], axis=0)
-        real_plus = jnp.dot(weight_ref[0], plus_rows, preferred_element_type=jnp.float32)
-        real_minus = jnp.dot(weight_ref[0], minus_rows, preferred_element_type=jnp.float32)
-        cross_plus = jnp.dot(weight_ref[1], plus_rows, preferred_element_type=jnp.float32)
-        cross_minus = jnp.dot(weight_ref[1], minus_rows, preferred_element_type=jnp.float32)
-        new_plus = real_plus - cross_minus
-        new_minus = cross_plus + real_minus
+        joined = jnp.concatenate([plus_rows, minus_rows], axis=1)
+        real_part = jnp.dot(weight_ref[0], joined, preferred_element_type=jnp.float32)
+        cross_part = jnp.dot(weight_ref[1], joined, preferred_element_type=jnp.float32)
+        new_plus = real_part[:, :num_edges] - cross_part[:, num_edges:]
+        new_minus = cross_part[:, :num_edges] + real_part[:, num_edges:]
         mixed += [new_plus[k * channel_count : (k + 1) * channel_count] for k in range(span_rows)]
         mixed += [new_minus[k * channel_count : (k + 1) * channel_count] for k in range(span_rows)]
         first_row = first_row + 2 * span_rows
@@ -309,9 +308,8 @@
             piece = summed[j * channel_count : (j + 1) * channel_count]
             high = piece.astype(jnp.bfloat16)
             low = (piece - high.astype(jnp.float32)).astype(jnp.bfloat16)
-            result = jnp.dot(weight, high, preferred_element_type=jnp.float32) + jnp.dot(
-                weight, low, preferred_element_type=jnp.float32
-            )
+            both = jnp.dot(weight, jnp.concatenate([high, low], axis=1), preferred_element_type=jnp.float32)
+            result = both[:, :num_edges] + both[:, num_edges:]
             for r in range(owners):
                 block = result[r * span_chan : (r + 1) * span_chan]
                 pieces[r].append(jnp.concatenate([block[:half], block[half:]], axis=1))

time: 99.7 us -> 99.2 us (level)
  no operation moved by 1% of the time
where the time goes in v11:
time: 99.2 us; the launch traced here: 98.6 us
  blocking collectives  45.6 us (46%)
  local copies, waits for them, and re-layouts  19.1 us (19%)
  starting transfers between devices  15 us (15%)
  Pallas kernels  13.8 us (14%)
  other arithmetic  4.3 us (4%)
    all_to_all x1, blocking collectives, body(): source = lax.all_to_all(outgoing, 'irreps', 0, 0, tiled=True)  26.3 us
    all_to_all x1, blocking collectives, body(): returned = lax.all_to_all(projected, 'irreps', 0, 0, tiled=True)  19.3 us
    all_to_all x1, starting transfers between devices, body(): arrived = lax.all_to_all(node_rows[send_list], 'graph', 0, 0, tiled=True)  15 us
    unnamed x34, local copies, waits for them, and re-layouts  11.5 us
    pallas_call x1, Pallas kernels, convolve_edges(): pl.pallas_call(conv_kernel, out_shape=jax.ShapeDtypeStruct((owners, out_r...  10.9 us
    pallas_call x1, Pallas kernels, gather_rows(): pl.pallas_call(gather_kernel, out_shape=jax.ShapeDtypeStruct((owners, per...  2.87 us
  transfers between devices with their start and end apart: 1, of which 0 were waited for; matrix products, arithmetic and copies ran while one was open for 18% of the time, Pallas kernels for 0%

profile of v11, /device:TPU:64, one launch (start us, length us, event | category | flops | bytes accessed | tf_op | source)
XLA Modules:
  0.0 98.6 jit_solution(11304019925000670994)
XLA Ops:
  0.0 0.0 copy-start
  0.0 0.0 copy-start.13
  0.0 0.0 copy-start.12
  0.0 0.0 copy-start.2
  0.0 0.7 compare_select_fusion
  0.8 1.0 %copy.27 = bf16[392,64]{0,1:T(8,128)(2,1)S(1)} copy(bf16[392,64]{1,0:T(8,128)(2,1)} %bitcast.47) | data formatting | bytes 100352 | tf_op jit(solution)/shard_map/reshape | solution.py:438
  1.8 0.0 copy-start.3
  1.8 1.8 %gather_fusion = bf16[256,392]{1,0:T(8,128)(2,1)} fusion(bf16[64,392]{1,0:T(8,128)(2,1)S(1)} %bitcast.33, s32[1024]{0:T(1024)S(1)} %pad_clamp_fusion.2), kind=kCustom, calls=%fused_computation | custom fusion | bytes 402432 | tf_op jit(solution)/shard_map/gather | solution.py:439
  3.6 0.0 copy-start.10
  3.6 0.0 copy-start.9
  3.6 0.0 copy-start.8
  3.6 15.0 %all-to-all-start = ((bf16[32,8,392]{2,1,0:T(8,128)(2,1)}), bf16[32,8,392]{2,1,0:T(8,128)(2,1)S(1)}, u32[]{:S(2)}, u32[]{:S(2)}) async-start(bf16[32,8,392]{2,1,0:T(8,128)(2,1)} %bitcast.3), calls=%async_computation | async-start | bytes 524288 | tf_op jit(solution)/shard_map/all_to_all | solution.py:439
  18.7 0.0 copy-start.11
  19.4 0.8 compare_select_fusion.1
  20.1 0.0 copy-done.13
  20.2 0.0 copy-done.12
  20.2 0.0 copy-done.2
  20.2 0.0 copy-start.5
  20.2 0.6 gather_fusion.1
  20.8 0.0 copy-done.3
  20.8 0.1 reshape.24
  20.9 0.1 copy.29
  21.0 0.0 copy-done.10
  21.0 0.7 copy.31
  21.8 0.0 copy-done.9
  21.8 0.8 copy.30
  22.5 0.0 copy-done.8
  22.5 0.8 copy.32
  23.4 0.0 copy-done.11
  23.4 1.0 %copy.36.index_ref = s32[1024,1]{1,0:T(8,128)} copy(s32[1024,1]{0,1:T(1,128)S(1)} %bitcast.51) | data formatting | bytes 8192 | tf_op jit(solution)/shard_map/broadcast_in_dim | solution.py:387
  24.4 0.0 copy-done.5
  24.4 2.3 %copy.33 = bf16[896,896]{0,1:T(8,128)(2,1)} copy(bf16[896,896]{1,0:T(8,128)(2,1)S(1)} %copy-done.5) | data formatting | bytes 3211264 | tf_op args[12]
  26.7 0.0 copy-start.4
  26.7 3.7 %copy.35 = bf16[2,640,640]{1,2,0:T(8,128)(2,1)} copy(bf16[2,640,640]{2,1,0:T(8,128)(2,1)} %param.32) | data formatting | bytes 3276800 | tf_op args[14]
  30.4 0.0 copy-done.4
  30.4 0.0 copy-start.1
  30.4 2.5 %copy.34 = bf16[2,768,768]{1,2,0:T(8,128)(2,1)} copy(bf16[2,768,768]{2,1,0:T(8,128)(2,1)S(1)} %copy-done.4) | data formatting | bytes 4718592 | tf_op args[13]
  32.8 0.0 copy-done.1
  32.8 0.8 gather_fusion.2
  33.6 1.3 %dynamic-slice_bitcast_fusion.refs_1_.length_ref = f32[1,64]{1,0:T(1,128)} fusion(f32[1024]{0:T(1024)} %param.25, s32[]{:T(128)S(6)} %select_n.28), kind=kLoop, calls=%fused_computation.29 | loop fusion | bytes 516 | tf_op jit(solution)/shard_map/broadcast_in_dim | solution.py:327
  35.0 0.7 fusion.3.extra_ref
  35.6 0.0 copy-done
  35.6 0.7 constant_dynamic-slice_fusion.refs_0_.wig_ref
  36.4 0.7 select_convert_fusion.refs_9_.onehot_ref
  37.0 0.6 fusion.refs_2_.kind_ref
  37.7 0.0 all-to-all-done
  37.7 0.0 copy-start.6
  37.7 0.7 copy-done.6
  38.3 2.9 %shard_map.172 = bf16[16,64,512]{2,1,0:T(8,128)(2,1)} custom-call(s32[1024,1]{1,0:T(8,128)} %copy.36.index_ref, bf16[64,392]{1,0:T(8,128)(2,1)} %bitcast.34, bf16[256,392]{1,0:T(8,128)(2,1)} %bitcast.46, bf16[64,120]{1,0:T(8,128)(2,1)} %fusion.3.extra_ref, bf16[235,64]{1,0:T(8,128)(2,1)} %constant_dynamic-slice_fusion.refs_0_.wig_ref, ...), custom_call_target="tpu_custom_call" | custom-call | flops 256901120 | bytes 1318912 | tf_op jit(solution)/shard_map/pallas_call | solution.py:388
  41.2 26.3 %all_to_all.21.src_ref = bf16[16,64,512]{2,1,0:T(8,128)(2,1)} all-to-all(bf16[16,64,512]{2,1,0:T(8,128)(2,1)} %shard_map.172), channel_id=1, replica_groups=mesh['graph'=32,'irreps'=16] {'irreps'}, dimensions={0} | all-to-all | bytes 2097152 | tf_op jit(solution)/shard_map/all_to_all | solution.py:474
  67.6 10.9 %shard_map.173 = bf16[16,208,128]{2,1,0:T(8,128)(2,1)} custom-call(bf16[16,64,512]{2,1,0:T(8,128)(2,1)} %all_to_all.21.src_ref, bf16[235,64]{1,0:T(8,128)(2,1)} %constant_dynamic-slice_fusion.refs_0_.wig_ref, f32[1,64]{1,0:T(1,128)} %dynamic-slice_bitcast_fusion.refs_1_.length_ref, bf16[90,64]{1,0:T(8,128)(2,1)} %fusion.refs_2_.kind_ref, ...), custom_call_target="tpu_custom_call" | custom-call | flops 637534208 | bytes 7937408 | tf_op jit(solution)/shard_map/pallas_call | solution.py:349
  78.5 0.0 copy-start.7
  78.5 19.3 %all_to_all.22 = bf16[16,208,128]{2,1,0:T(8,128)(2,1)S(1)} all-to-all(bf16[16,208,128]{2,1,0:T(8,128)(2,1)} %shard_map.173), channel_id=1, replica_groups=mesh['graph'=32,'irreps'=16] {'irreps'}, dimensions={0} | all-to-all | bytes 1703936 | tf_op jit(solution)/shard_map/all_to_all | solution.py:476
  97.7 0.1 convert_reduce_fusion
  97.9 0.1 reshape_reshape.3
  98.0 0.0 copy-done.7
  98.0 0.7 add_convert_fusion
  (9 shorter events, 0.1 us)
Async XLA Ops:
  0.0 35.6 %copy-start = (bf16[235,1024]{1,0:T(8,128)(2,1)S(1)}, bf16[235,1024]{1,0:T(8,128)(2,1)}, u32[]{:S(2)}) copy-start(bf16[235,1024]{1,0:T(8,128)(2,1)} %param.26) | copy-start | bytes 1443844
  0.0 20.1 %copy-start.13 = (s32[8]{0:T(128)S(1)}, s32[8]{0:T(128)}, u32[]{:S(2)}) copy-start(s32[8]{0:T(128)} %constant.38) | copy-start | bytes 100
  0.0 20.2 %copy-start.12 = (f32[7,8]{1,0:T(8,128)S(1)}, f32[7,8]{1,0:T(8,128)}, u32[]{:S(2)}) copy-start(f32[7,8]{1,0:T(8,128)} %param.19) | copy-start | bytes 676
  0.0 20.2 %copy-start.2 = (bf16[7,128,8]{1,2,0:T(8,128)(2,1)S(1)}, bf16[7,128,8]{1,2,0:T(8,128)(2,1)}, u32[]{:S(2)}) copy-start(bf16[7,128,8]{1,2,0:T(8,128)(2,1)} %param.33) | copy-start | bytes 43012
  1.8 19.1 %copy-start.3 = (bf16[392,64]{0,1:T(8,128)(2,1)}, bf16[392,64]{0,1:T(8,128)(2,1)S(1)}, u32[]{:S(2)}) copy-start(bf16[392,64]{0,1:T(8,128)(2,1)S(1)} %copy.27) | copy-start | bytes 150532
  3.6 17.4 %copy-start.10 = (bf16[90,128]{1,0:T(8,128)(2,1)S(1)}, bf16[90,128]{1,0:T(8,128)(2,1)}, u32[]{:S(2)}) copy-start(bf16[90,128]{1,0:T(8,128)(2,1)} %param.28) | copy-start | bytes 69124
  3.6 18.1 %copy-start.9 = (bf16[512,128]{1,0:T(8,128)(2,1)S(1)}, bf16[512,128]{1,0:T(8,128)(2,1)}, u32[]{:S(2)}) copy-start(bf16[512,128]{1,0:T(8,128)(2,1)} %param.27) | copy-start | bytes 393220
  3.6 18.9 %copy-start.8 = (bf16[128,896]{1,0:T(8,128)(2,1)S(1)}, bf16[128,896]{1,0:T(8,128)(2,1)}, u32[]{:S(2)}) copy-start(bf16[128,896]{1,0:T(8,128)(2,1)} %param.29) | copy-start | bytes 688132
  3.6 34.0 %all-to-all-start = ((bf16[32,8,392]{2,1,0:T(8,128)(2,1)}), bf16[32,8,392]{2,1,0:T(8,128)(2,1)S(1)}, u32[]{:S(2)}, u32[]{:S(2)}) async-start(bf16[32,8,392]{2,1,0:T(8,128)(2,1)} %bitcast.3), calls=%async_computation | async-start | bytes 524288 | tf_op jit(solution)/shard_map/all_to_all | solution.py:439
  18.7 4.7 %copy-start.11 = (s32[1024]{0:T(1024)S(1)}, s32[1024]{0:T(1024)}, u32[]{:S(2)}) copy-start(s32[1024]{0:T(1024)} %param.22) | copy-start | bytes 12292
  20.2 4.2 %copy-start.5 = (bf16[896,896]{1,0:T(8,128)(2,1)S(1)}, bf16[896,896]{1,0:T(8,128)(2,1)}, u32[]{:S(2)}) copy-start(bf16[896,896]{1,0:T(8,128)(2,1)} %param.30) | copy-start | bytes 4816900
  26.7 3.7 %copy-start.4 = (bf16[2,768,768]{2,1,0:T(8,128)(2,1)S(1)}, bf16[2,768,768]{2,1,0:T(8,128)(2,1)}, u32[]{:S(2)}) copy-start(bf16[2,768,768]{2,1,0:T(8,128)(2,1)} %param.31) | copy-start | bytes 7077892
  30.4 2.5 %copy-start.1 = (s32[64]{0:T(128)S(1)}, s32[64]{0:T(128)}, u32[]{:S(2)}) copy-start(s32[64]{0:T(128)} %param.20) | copy-start | bytes 772
  37.7 0.7 copy-start.6
  78.5 19.5 %copy-start.7 = (bf16[49,8,64]{2,1,0:T(8,128)(2,1)S(1)}, bf16[49,8,64]{2,1,0:T(8,128)(2,1)}, u32[]{:S(2)}) copy-start(bf16[49,8,64]{2,1,0:T(8,128)(2,1)} %param.18) | copy-start | bytes 150532

commit v12 on v11

--- a/solution.py
+++ b/solution.py
@@ -297,8 +297,10 @@
     upper_part = stacked.astype(jnp.bfloat16)
     lower_part = (stacked - upper_part.astype(jnp.float32)).astype(jnp.bfloat16)
     onehot = onehot_ref[...]
-    summed = jnp.dot(upper_part, onehot, preferred_element_type=jnp.float32) + jnp.dot(
-        lower_part, onehot, preferred_element_type=jnp.float32
+    summed = jnp.dot(
+        jnp.concatenate([upper_part, lower_part], axis=1),
+        jnp.concatenate([onehot, onehot], axis=0),
+        preferred_element_type=jnp.float32,
     )
     half = span_chan // 2
     pieces = [[] for _ in range(owners)]

time: 99.2 us -> 101 us (1.018)
  Pallas kernels: 13.8 us -> 15.2 us
    pallas_call x1, Pallas kernels: 10.9 us -> 12.3 us  [convolve_edges(): pl.pallas_call(conv_kernel, out_shape=jax.ShapeDtypeStruct((owners, out_r...]
where the time goes in v12:
time: 101 us; the launch traced here: 100 us
  blocking collectives  45.6 us (45%)
  local copies, waits for them, and re-layouts  19.1 us (19%)
  Pallas kernels  15.2 us (15%)
  starting transfers between devices  15 us (15%)
  other arithmetic  4.3 us (4%)
    all_to_all x1, blocking collectives, body(): source = lax.all_to_all(outgoing, 'irreps', 0, 0, tiled=True)  26.3 us
    all_to_all x1, blocking collectives, body(): returned = lax.all_to_all(projected, 'irreps', 0, 0, tiled=True)  19.2 us
    all_to_all x1, starting transfers between devices, body(): arrived = lax.all_to_all(node_rows[send_list], 'graph', 0, 0, tiled=True)  15 us
    pallas_call x1, Pallas kernels, convolve_edges(): pl.pallas_call(conv_kernel, out_shape=jax.ShapeDtypeStruct((owners, out_r...  12.3 us
    unnamed x34, local copies, waits for them, and re-layouts  11.5 us
    pallas_call x1, Pallas kernels, gather_rows(): pl.pallas_call(gather_kernel, out_shape=jax.ShapeDtypeStruct((owners, per...  2.88 us
  transfers between devices with their start and end apart: 1, of which 0 were waited for; matrix products, arithmetic and copies ran while one was open for 18% of the time, Pallas kernels for 0%

profile of v12, /device:TPU:64, one launch (start us, length us, event | category | flops | bytes accessed | tf_op | source)
XLA Modules:
  0.0 100.0 jit_solution(15319298954662068304)
XLA Ops:
  0.0 0.0 copy-start
  0.0 0.0 copy-start.13
  0.0 0.0 copy-start.12
  0.0 0.0 copy-start.2
  0.0 0.7 compare_select_fusion
  0.8 1.0 %copy.27 = bf16[392,64]{0,1:T(8,128)(2,1)S(1)} copy(bf16[392,64]{1,0:T(8,128)(2,1)} %bitcast.47) | data formatting | bytes 100352 | tf_op jit(solution)/shard_map/reshape | solution.py:440
  1.8 0.0 copy-start.3
  1.8 1.8 %gather_fusion = bf16[256,392]{1,0:T(8,128)(2,1)} fusion(bf16[64,392]{1,0:T(8,128)(2,1)S(1)} %bitcast.33, s32[1024]{0:T(1024)S(1)} %pad_clamp_fusion.2), kind=kCustom, calls=%fused_computation | custom fusion | bytes 402432 | tf_op jit(solution)/shard_map/gather | solution.py:441
  3.6 0.0 copy-start.10
  3.6 0.0 copy-start.9
  3.6 0.0 copy-start.8
  3.6 15.0 %all-to-all-start = ((bf16[32,8,392]{2,1,0:T(8,128)(2,1)}), bf16[32,8,392]{2,1,0:T(8,128)(2,1)S(1)}, u32[]{:S(2)}, u32[]{:S(2)}) async-start(bf16[32,8,392]{2,1,0:T(8,128)(2,1)} %bitcast.3), calls=%async_computation | async-start | bytes 524288 | tf_op jit(solution)/shard_map/all_to_all | solution.py:441
  18.7 0.0 copy-start.11
  19.4 0.8 compare_select_fusion.1
  20.1 0.0 copy-done.13
  20.2 0.0 copy-done.12
  20.2 0.0 copy-done.2
  20.2 0.0 copy-start.5
  20.2 0.6 gather_fusion.1
  20.8 0.0 copy-done.3
  20.8 0.1 reshape.24
  20.9 0.1 copy.29
  21.0 0.0 copy-done.10
  21.0 0.7 copy.31
  21.8 0.0 copy-done.9
  21.8 0.8 copy.30
  22.5 0.0 copy-done.8
  22.5 0.8 copy.32
  23.4 0.0 copy-done.11
  23.4 1.0 %copy.36.index_ref = s32[1024,1]{1,0:T(8,128)} copy(s32[1024,1]{0,1:T(1,128)S(1)} %bitcast.51) | data formatting | bytes 8192 | tf_op jit(solution)/shard_map/broadcast_in_dim | solution.py:389
  24.4 0.0 copy-done.5
  24.4 2.3 %copy.33 = bf16[896,896]{0,1:T(8,128)(2,1)} copy(bf16[896,896]{1,0:T(8,128)(2,1)S(1)} %copy-done.5) | data formatting | bytes 3211264 | tf_op args[12]
  26.7 0.0 copy-start.4
  26.7 3.7 %copy.35 = bf16[2,640,640]{1,2,0:T(8,128)(2,1)} copy(bf16[2,640,640]{2,1,0:T(8,128)(2,1)} %param.32) | data formatting | bytes 3276800 | tf_op args[14]
  30.4 0.0 copy-done.4
  30.4 0.0 copy-start.1
  30.4 2.5 %copy.34 = bf16[2,768,768]{1,2,0:T(8,128)(2,1)} copy(bf16[2,768,768]{2,1,0:T(8,128)(2,1)S(1)} %copy-done.4) | data formatting | bytes 4718592 | tf_op args[13]
  32.8 0.0 copy-done.1
  32.8 0.8 gather_fusion.2
  33.6 1.3 %dynamic-slice_bitcast_fusion.refs_1_.length_ref = f32[1,64]{1,0:T(1,128)} fusion(f32[1024]{0:T(1024)} %param.25, s32[]{:T(128)S(6)} %select_n.28), kind=kLoop, calls=%fused_computation.29 | loop fusion | bytes 516 | tf_op jit(solution)/shard_map/broadcast_in_dim | solution.py:329
  35.0 0.7 fusion.3.extra_ref
  35.6 0.0 copy-done
  35.6 0.7 constant_dynamic-slice_fusion.refs_0_.wig_ref
  36.4 0.7 select_convert_fusion.refs_9_.onehot_ref
  37.0 0.6 fusion.refs_2_.kind_ref
  37.7 0.0 all-to-all-done
  37.7 0.0 copy-start.6
  37.7 0.7 copy-done.6
  38.3 2.9 %shard_map.172 = bf16[16,64,512]{2,1,0:T(8,128)(2,1)} custom-call(s32[1024,1]{1,0:T(8,128)} %copy.36.index_ref, bf16[64,392]{1,0:T(8,128)(2,1)} %bitcast.34, bf16[256,392]{1,0:T(8,128)(2,1)} %bitcast.46, bf16[64,120]{1,0:T(8,128)(2,1)} %fusion.3.extra_ref, bf16[235,64]{1,0:T(8,128)(2,1)} %constant_dynamic-slice_fusion.refs_0_.wig_ref, ...), custom_call_target="tpu_custom_call" | custom-call | flops 256901120 | bytes 1318912 | tf_op jit(solution)/shard_map/pallas_call | solution.py:390
  41.2 26.3 %all_to_all.21.src_ref = bf16[16,64,512]{2,1,0:T(8,128)(2,1)} all-to-all(bf16[16,64,512]{2,1,0:T(8,128)(2,1)} %shard_map.172), channel_id=1, replica_groups=mesh['graph'=32,'irreps'=16] {'irreps'}, dimensions={0} | all-to-all | bytes 2097152 | tf_op jit(solution)/shard_map/all_to_all | solution.py:476
  67.5 12.3 %shard_map.173 = bf16[16,208,128]{2,1,0:T(8,128)(2,1)} custom-call(bf16[16,64,512]{2,1,0:T(8,128)(2,1)} %all_to_all.21.src_ref, bf16[235,64]{1,0:T(8,128)(2,1)} %constant_dynamic-slice_fusion.refs_0_.wig_ref, f32[1,64]{1,0:T(1,128)} %dynamic-slice_bitcast_fusion.refs_1_.length_ref, bf16[90,64]{1,0:T(8,128)(2,1)} %fusion.refs_2_.kind_ref, ...), custom_call_target="tpu_custom_call" | custom-call | flops 637534208 | bytes 7937408 | tf_op jit(solution)/shard_map/pallas_call | solution.py:351
  79.9 0.0 copy-start.7
  79.9 19.2 %all_to_all.22 = bf16[16,208,128]{2,1,0:T(8,128)(2,1)S(1)} all-to-all(bf16[16,208,128]{2,1,0:T(8,128)(2,1)} %shard_map.173), channel_id=1, replica_groups=mesh['graph'=32,'irreps'=16] {'irreps'}, dimensions={0} | all-to-all | bytes 1703936 | tf_op jit(solution)/shard_map/all_to_all | solution.py:478
  99.1 0.1 convert_reduce_fusion
  99.3 0.1 reshape_reshape.3
  99.4 0.0 copy-done.7
  99.4 0.7 add_convert_fusion
  (9 shorter events, 0.1 us)
Async XLA Ops:
  0.0 35.6 %copy-start = (bf16[235,1024]{1,0:T(8,128)(2,1)S(1)}, bf16[235,1024]{1,0:T(8,128)(2,1)}, u32[]{:S(2)}) copy-start(bf16[235,1024]{1,0:T(8,128)(2,1)} %param.26) | copy-start | bytes 1443844
  0.0 20.1 %copy-start.13 = (s32[8]{0:T(128)S(1)}, s32[8]{0:T(128)}, u32[]{:S(2)}) copy-start(s32[8]{0:T(128)} %constant.38) | copy-start | bytes 100
  0.0 20.2 %copy-start.12 = (f32[7,8]{1,0:T(8,128)S(1)}, f32[7,8]{1,0:T(8,128)}, u32[]{:S(2)}) copy-start(f32[7,8]{1,0:T(8,128)} %param.19) | copy-start | bytes 676
  0.0 20.2 %copy-start.2 = (bf16[7,128,8]{1,2,0:T(8,128)(2,1)S(1)}, bf16[7,128,8]{1,2,0:T(8,128)(2,1)}, u32[]{:S(2)}) copy-start(bf16[7,128,8]{1,2,0:T(8,128)(2,1)} %param.33) | copy-start | bytes 43012
  1.8 19.1 %copy-start.3 = (bf16[392,64]{0,1:T(8,128)(2,1)}, bf16[392,64]{0,1:T(8,128)(2,1)S(1)}, u32[]{:S(2)}) copy-start(bf16[392,64]{0,1:T(8,128)(2,1)S(1)} %copy.27) | copy-start | bytes 150532
  3.6 17.4 %copy-start.10 = (bf16[90,128]{1,0:T(8,128)(2,1)S(1)}, bf16[90,128]{1,0:T(8,128)(2,1)}, u32[]{:S(2)}) copy-start(bf16[90,128]{1,0:T(8,128)(2,1)} %param.28) | copy-start | bytes 69124
  3.6 18.1 %copy-start.9 = (bf16[512,128]{1,0:T(8,128)(2,1)S(1)}, bf16[512,128]{1,0:T(8,128)(2,1)}, u32[]{:S(2)}) copy-start(bf16[512,128]{1,0:T(8,128)(2,1)} %param.27) | copy-start | bytes 393220
  3.6 18.9 %copy-start.8 = (bf16[128,896]{1,0:T(8,128)(2,1)S(1)}, bf16[128,896]{1,0:T(8,128)(2,1)}, u32[]{:S(2)}) copy-start(bf16[128,896]{1,0:T(8,128)(2,1)} %param.29) | copy-start | bytes 688132
  3.6 34.0 %all-to-all-start = ((bf16[32,8,392]{2,1,0:T(8,128)(2,1)}), bf16[32,8,392]{2,1,0:T(8,128)(2,1)S(1)}, u32[]{:S(2)}, u32[]{:S(2)}) async-start(bf16[32,8,392]{2,1,0:T(8,128)(2,1)} %bitcast.3), calls=%async_computation | async-start | bytes 524288 | tf_op jit(solution)/shard_map/all_to_all | solution.py:441
  18.7 4.7 %copy-start.11 = (s32[1024]{0:T(1024)S(1)}, s32[1024]{0:T(1024)}, u32[]{:S(2)}) copy-start(s32[1024]{0:T(1024)} %param.22) | copy-start | bytes 12292
  20.2 4.2 %copy-start.5 = (bf16[896,896]{1,0:T(8,128)(2,1)S(1)}, bf16[896,896]{1,0:T(8,128)(2,1)}, u32[]{:S(2)}) copy-start(bf16[896,896]{1,0:T(8,128)(2,1)} %param.30) | copy-start | bytes 4816900
  26.7 3.7 %copy-start.4 = (bf16[2,768,768]{2,1,0:T(8,128)(2,1)S(1)}, bf16[2,768,768]{2,1,0:T(8,128)(2,1)}, u32[]{:S(2)}) copy-start(bf16[2,768,768]{2,1,0:T(8,128)(2,1)} %param.31) | copy-start | bytes 7077892
  30.4 2.5 %copy-start.1 = (s32[64]{0:T(128)S(1)}, s32[64]{0:T(128)}, u32[]{:S(2)}) copy-start(s32[64]{0:T(128)} %param.20) | copy-start | bytes 772
  37.7 0.7 copy-start.6
  79.9 19.5 %copy-start.7 = (bf16[49,8,64]{2,1,0:T(8,128)(2,1)S(1)}, bf16[49,8,64]{2,1,0:T(8,128)(2,1)}, u32[]{:S(2)}) copy-start(bf16[49,8,64]{2,1,0:T(8,128)(2,1)} %param.18) | copy-start | bytes 150532

commit v13 on v11

--- a/solution.py
+++ b/solution.py
@@ -436,7 +436,12 @@
     row_used = coeffs * span_chan
     row_width = 128 * pl.cdiv(row_used, 128)
     node_rows = node_feats.reshape(row_used, atom_count).T
-    arrived = lax.all_to_all(node_rows[send_list], "graph", 0, 0, tiled=True)
+    send_hot = (send_list[:, None] == jnp.arange(atom_count, dtype=jnp.int32)[None, :]).astype(jnp.bfloat16)
+    outgoing_rows = lax.dot_general(
+        send_hot, node_feats.reshape(row_used, atom_count), (((1,), (1,)), ((), ())),
+        preferred_element_type=jnp.float32,
+    ).astype(jnp.bfloat16)
+    arrived = lax.all_to_all(outgoing_rows, "graph", 0, 0, tiled=True)
 
     gain_high = lax.reduce_precision(norm_gain, exponent_bits=8, mantissa_bits=7)
     gain_rest = norm_gain - gain_high

time: 99.2 us -> 97.3 us (0.981)
  the two profiles are of different devices: /device:TPU:64 before, /device:TPU:32 now
where the time goes in v13:
time: 97.3 us; the launch traced here: 96.7 us
  blocking collectives  42.5 us (44%)
  local copies, waits for them, and re-layouts  17.9 us (18%)
  starting transfers between devices  15.5 us (16%)
  Pallas kernels  13.8 us (14%)
  other arithmetic  4.91 us (5%)
  matrix products  1.29 us (1%)
    all_to_all x1, blocking collectives, body(): source = lax.all_to_all(outgoing, 'irreps', 0, 0, tiled=True)  24.6 us
    all_to_all x1, blocking collectives, body(): returned = lax.all_to_all(projected, 'irreps', 0, 0, tiled=True)  17.9 us
    all_to_all x1, starting transfers between devices, body(): arrived = lax.all_to_all(outgoing_rows, 'graph', 0, 0, tiled=True)  15.5 us
    unnamed x28, local copies, waits for them, and re-layouts  11.6 us
    pallas_call x1, Pallas kernels, convolve_edges(): pl.pallas_call(conv_kernel, out_shape=jax.ShapeDtypeStruct((owners, out_r...  10.9 us
    pallas_call x1, Pallas kernels, gather_rows(): pl.pallas_call(gather_kernel, out_shape=jax.ShapeDtypeStruct((owners, per...  2.87 us
  transfers between devices with their start and end apart: 1, of which 0 were waited for; matrix products, arithmetic and copies ran while one was open for 21% of the time, Pallas kernels for 0%

profile of v13, /device:TPU:32, one launch (start us, length us, event | category | flops | bytes accessed | tf_op | source)
XLA Modules:
  0.0 96.7 jit_solution(14592016008565645812)
XLA Ops:
  0.0 0.0 copy-start
  0.0 0.0 copy-start.2
  0.0 1.3 %convolution_convert_fusion = bf16[256,392]{0,1:T(8,128)(2,1)S(1)} fusion(s32[256]{0:T(256)} %param.21, bf16[49,8,64]{2,1,0:T(8,128)(2,1)} %param.18), kind=kOutput, calls=%fused_computation.3 | convolution fusion | flops 12961792 | bytes 251904 | tf_op jit(solution)/shard_map/dot_general | solution.py:440
  1.3 0.0 copy-start.9
  1.3 0.0 copy-start.6
  1.3 0.0 copy-start.8
  1.3 0.9 copy.29
  2.2 0.0 copy-start.7
  2.2 15.5 %all-to-all-start = ((bf16[32,8,392]{2,1,0:T(8,128)(2,1)}), bf16[32,8,392]{2,1,0:T(8,128)(2,1)S(1)}, u32[]{:S(2)}, u32[]{:S(2)}) async-start(bf16[32,8,392]{2,1,0:T(8,128)(2,1)} %bitcast.3), calls=%async_computation | async-start | bytes 524288 | tf_op jit(solution)/shard_map/all_to_all | solution.py:444
  17.7 0.0 copy-start.10
  18.4 0.8 compare_select_fusion
  19.2 0.7 pad_clamp_fusion.1
  19.8 0.7 fusion.7
  20.5 0.0 copy-done.2
  20.5 0.0 copy-start.4
  20.5 0.6 gather_fusion
  21.2 0.1 reshape.26
  21.2 0.1 copy.31
  21.3 0.0 copy-done.9
  21.4 0.7 copy.33
  22.1 0.0 copy-done.6
  22.1 0.8 copy.28
  22.8 0.0 copy-done.8
  22.8 0.8 copy.32
  23.6 0.0 copy-done.7
  23.6 0.8 copy.34
  24.5 0.0 copy-done.10
  24.5 1.0 %copy.38.index_ref = s32[1024,1]{1,0:T(8,128)} copy(s32[1024,1]{0,1:T(1,128)S(1)} %bitcast.52) | data formatting | bytes 8192 | tf_op jit(solution)/shard_map/broadcast_in_dim | solution.py:387
  25.5 0.0 copy-done.4
  25.5 2.3 %copy.35 = bf16[896,896]{0,1:T(8,128)(2,1)} copy(bf16[896,896]{1,0:T(8,128)(2,1)S(1)} %copy-done.4) | data formatting | bytes 3211264 | tf_op args[12]
  27.8 0.0 copy-start.3
  27.8 3.7 %copy.37 = bf16[2,640,640]{1,2,0:T(8,128)(2,1)} copy(bf16[2,640,640]{2,1,0:T(8,128)(2,1)} %param.32) | data formatting | bytes 3276800 | tf_op args[14]
  31.5 0.0 copy-done.3
  31.5 0.0 copy-start.1
  31.5 2.5 %copy.36 = bf16[2,768,768]{1,2,0:T(8,128)(2,1)} copy(bf16[2,768,768]{2,1,0:T(8,128)(2,1)S(1)} %copy-done.3) | data formatting | bytes 4718592 | tf_op args[13]
  34.0 0.0 copy-done.1
  34.0 0.8 gather_fusion.1
  34.8 1.3 %dynamic-slice_bitcast_fusion.refs_1_.length_ref = f32[1,64]{1,0:T(1,128)} fusion(f32[1024]{0:T(1024)} %param.25, s32[]{:T(128)S(6)} %select_n.24), kind=kLoop, calls=%fused_computation.29 | loop fusion | bytes 516 | tf_op jit(solution)/shard_map/broadcast_in_dim | solution.py:327
  36.1 0.7 fusion.4.extra_ref
  36.7 0.0 copy-done
  36.7 0.7 constant_dynamic-slice_fusion.refs_0_.wig_ref
  37.5 0.7 select_convert_fusion.refs_9_.onehot_ref
  38.2 0.6 fusion.1.refs_2_.kind_ref
  38.8 0.0 all-to-all-done
  38.8 0.0 copy-start.5
  38.8 0.7 copy-done.5
  39.5 2.9 %shard_map.172 = bf16[16,64,512]{2,1,0:T(8,128)(2,1)} custom-call(s32[1024,1]{1,0:T(8,128)} %copy.38.index_ref, bf16[64,392]{1,0:T(8,128)(2,1)} %bitcast.50, bf16[256,392]{1,0:T(8,128)(2,1)} %bitcast.46, bf16[64,120]{1,0:T(8,128)(2,1)} %fusion.4.extra_ref, bf16[235,64]{1,0:T(8,128)(2,1)} %constant_dynamic-slice_fusion.refs_0_.wig_ref, ...), custom_call_target="tpu_custom_call" | custom-call | flops 256901120 | bytes 1318912 | tf_op jit(solution)/shard_map/pallas_call | solution.py:388
  42.4 24.6 %all_to_all.21.src_ref = bf16[16,64,512]{2,1,0:T(8,128)(2,1)} all-to-all(bf16[16,64,512]{2,1,0:T(8,128)(2,1)} %shard_map.172), channel_id=1, replica_groups=mesh['graph'=32,'irreps'=16] {'irreps'}, dimensions={0} | all-to-all | bytes 2097152 | tf_op jit(solution)/shard_map/all_to_all | solution.py:479
  67.0 10.9 %shard_map.173 = bf16[16,208,128]{2,1,0:T(8,128)(2,1)} custom-call(bf16[16,64,512]{2,1,0:T(8,128)(2,1)} %all_to_all.21.src_ref, bf16[235,64]{1,0:T(8,128)(2,1)} %constant_dynamic-slice_fusion.refs_0_.wig_ref, f32[1,64]{1,0:T(1,128)} %dynamic-slice_bitcast_fusion.refs_1_.length_ref, bf16[90,64]{1,0:T(8,128)(2,1)} %fusion.1.refs_2_.kind_ref, ...), custom_call_target="tpu_custom_call" | custom-call | flops 637534208 | bytes 7937408 | tf_op jit(solution)/shard_map/pallas_call | solution.py:349
  77.9 17.9 %all_to_all.22 = bf16[16,208,128]{2,1,0:T(8,128)(2,1)S(1)} all-to-all(bf16[16,208,128]{2,1,0:T(8,128)(2,1)} %shard_map.173), channel_id=1, replica_groups=mesh['graph'=32,'irreps'=16] {'irreps'}, dimensions={0} | all-to-all | bytes 1703936 | tf_op jit(solution)/shard_map/all_to_all | solution.py:481
  95.8 0.1 convert_reduce_fusion
  95.9 0.1 reshape_reshape.3
  96.0 0.7 add_convert_fusion
  (6 shorter events, 0.0 us)
Async XLA Ops:
  0.0 36.7 %copy-start = (bf16[235,1024]{1,0:T(8,128)(2,1)S(1)}, bf16[235,1024]{1,0:T(8,128)(2,1)}, u32[]{:S(2)}) copy-start(bf16[235,1024]{1,0:T(8,128)(2,1)} %param.26) | copy-start | bytes 1443844
  0.0 20.5 %copy-start.2 = (bf16[7,128,8]{1,2,0:T(8,128)(2,1)S(1)}, bf16[7,128,8]{1,2,0:T(8,128)(2,1)}, u32[]{:S(2)}) copy-start(bf16[7,128,8]{1,2,0:T(8,128)(2,1)} %param.33) | copy-start | bytes 43012
  1.3 20.0 %copy-start.9 = (bf16[90,128]{1,0:T(8,128)(2,1)S(1)}, bf16[90,128]{1,0:T(8,128)(2,1)}, u32[]{:S(2)}) copy-start(bf16[90,128]{1,0:T(8,128)(2,1)} %param.28) | copy-start | bytes 69124
  1.3 20.8 %copy-start.6 = (bf16[49,8,64]{2,1,0:T(8,128)(2,1)S(1)}, bf16[49,8,64]{2,1,0:T(8,128)(2,1)}, u32[]{:S(2)}) copy-start(bf16[49,8,64]{2,1,0:T(8,128)(2,1)} %param.18) | copy-start | bytes 150532
  1.3 21.5 %copy-start.8 = (bf16[512,128]{1,0:T(8,128)(2,1)S(1)}, bf16[512,128]{1,0:T(8,128)(2,1)}, u32[]{:S(2)}) copy-start(bf16[512,128]{1,0:T(8,128)(2,1)} %param.27) | copy-start | bytes 393220
  2.2 21.4 %copy-start.7 = (bf16[128,896]{1,0:T(8,128)(2,1)S(1)}, bf16[128,896]{1,0:T(8,128)(2,1)}, u32[]{:S(2)}) copy-start(bf16[128,896]{1,0:T(8,128)(2,1)} %param.29) | copy-start | bytes 688132
  2.2 36.6 %all-to-all-start = ((bf16[32,8,392]{2,1,0:T(8,128)(2,1)}), bf16[32,8,392]{2,1,0:T(8,128)(2,1)S(1)}, u32[]{:S(2)}, u32[]{:S(2)}) async-start(bf16[32,8,392]{2,1,0:T(8,128)(2,1)} %bitcast.3), calls=%async_computation | async-start | bytes 524288 | tf_op jit(solution)/shard_map/all_to_all | solution.py:444
  17.7 6.8 %copy-start.10 = (s32[1024]{0:T(1024)S(1)}, s32[1024]{0:T(1024)}, u32[]{:S(2)}) copy-start(s32[1024]{0:T(1024)} %param.22) | copy-start | bytes 12292
  20.5 5.0 %copy-start.4 = (bf16[896,896]{1,0:T(8,128)(2,1)S(1)}, bf16[896,896]{1,0:T(8,128)(2,1)}, u32[]{:S(2)}) copy-start(bf16[896,896]{1,0:T(8,128)(2,1)} %param.30) | copy-start | bytes 4816900
  27.8 3.7 %copy-start.3 = (bf16[2,768,768]{2,1,0:T(8,128)(2,1)S(1)}, bf16[2,768,768]{2,1,0:T(8,128)(2,1)}, u32[]{:S(2)}) copy-start(bf16[2,768,768]{2,1,0:T(8,128)(2,1)} %param.31) | copy-start | bytes 7077892
  31.5 2.5 %copy-start.1 = (s32[64]{0:T(128)S(1)}, s32[64]{0:T(128)}, u32[]{:S(2)}) copy-start(s32[64]{0:T(128)} %param.20) | copy-start | bytes 772
  38.8 0.7 copy-start.5

commit v14 on v11

--- a/solution.py
+++ b/solution.py
@@ -367,6 +367,24 @@
     )(*operands)
 
 
+def send_kernel(index_ref, feats_ref, out_ref):
+    hot = (
+        index_ref[...] == lax.broadcasted_iota(jnp.int32, (index_ref.shape[0], feats_ref.shape[1]), 1)
+    ).astype(feats_ref.dtype)
+    out_ref[...] = lax.dot_general(
+        hot, feats_ref[...], (((1,), (1,)), ((), ())), preferred_element_type=jnp.float32
+    ).astype(out_ref.dtype)
+
+
+def send_rows(send_list, feats):
+    return pl.pallas_call(
+        send_kernel,
+        out_shape=jax.ShapeDtypeStruct((send_list.shape[0], feats.shape[0]), feats.dtype),
+        in_specs=[pl.BlockSpec(memory_space=pltpu.VMEM)] * 2,
+        out_specs=pl.BlockSpec(memory_space=pltpu.VMEM),
+    )(send_list[:, None], feats)
+
+
 def gather_kernel(index_ref, local_ref, arrived_ref, extra_ref, *refs):
     out_ref = refs[-1]
     owners, per_owner, row_width = out_ref.shape
@@ -436,7 +454,8 @@
     row_used = coeffs * span_chan
     row_width = 128 * pl.cdiv(row_used, 128)
     node_rows = node_feats.reshape(row_used, atom_count).T
-    arrived = lax.all_to_all(node_rows[send_list], "graph", 0, 0, tiled=True)
+    outgoing_rows = send_rows(send_list, node_feats.reshape(row_used, atom_count))
+    arrived = lax.all_to_all(outgoing_rows, "graph", 0, 0, tiled=True)
 
     gain_high = lax.reduce_precision(norm_gain, exponent_bits=8, mantissa_bits=7)
     gain_rest = norm_gain - gain_high

time: 99.2 us -> 99.6 us (level)
  the two profiles are of different devices: /device:TPU:64 before, /device:TPU:32 now
where the time goes in v14:
time: 99.6 us; the launch traced here: 99 us
  blocking collectives  42.7 us (43%)
  local copies, waits for them, and re-layouts  19.5 us (20%)
  Pallas kernels  15.7 us (16%)
  starting transfers between devices  15.5 us (16%)
  other arithmetic  4.9 us (5%)
    all_to_all x1, blocking collectives, body(): source = lax.all_to_all(outgoing, 'irreps', 0, 0, tiled=True)  24.6 us
    all_to_all x1, blocking collectives, body(): returned = lax.all_to_all(projected, 'irreps', 0, 0, tiled=True)  18 us
    all_to_all x1, starting transfers between devices, body(): arrived = lax.all_to_all(outgoing_rows, 'graph', 0, 0, tiled=True)  15.5 us
    unnamed x28, local copies, waits for them, and re-layouts  11.6 us
    pallas_call x1, Pallas kernels, convolve_edges(): pl.pallas_call(conv_kernel, out_shape=jax.ShapeDtypeStruct((owners, out_r...  10.9 us
    pallas_call x1, Pallas kernels, gather_rows(): pl.pallas_call(gather_kernel, out_shape=jax.ShapeDtypeStruct((owners, per...  2.87 us
  transfers between devices with their start and end apart: 1, of which 0 were waited for; matrix products, arithmetic and copies ran while one was open for 21% of the time, Pallas kernels for 0%

profile of v14, /device:TPU:32, one launch (start us, length us, event | category | flops | bytes accessed | tf_op | source)
XLA Modules:
  0.0 99.0 jit_solution(9492535110843455238)
XLA Ops:
  0.0 0.0 copy-start
  0.0 0.0 copy-start.2
  0.0 1.5 %copy.29.index_ref = s32[256,1]{1,0:T(8,128)} copy(s32[256,1]{0,1:T(1,128)} %bitcast.54) | data formatting | bytes 2048 | tf_op jit(solution)/shard_map/broadcast_in_dim | solution.py:385
  1.5 0.0 copy-start.9
  1.5 2.0 %shard_map.172 = bf16[256,392]{1,0:T(8,128)(2,1)} custom-call(s32[256,1]{1,0:T(8,128)} %copy.29.index_ref, bf16[392,64]{1,0:T(8,128)(2,1)} %bitcast.47), custom_call_target="tpu_custom_call" | custom-call | tf_op jit(solution)/shard_map/pallas_call | solution.py:380
  3.5 0.0 copy-start.8
  3.5 0.0 copy-start.7
  3.5 15.5 %all-to-all-start = ((bf16[32,8,392]{2,1,0:T(8,128)(2,1)}), bf16[32,8,392]{2,1,0:T(8,128)(2,1)S(1)}, u32[]{:S(2)}, u32[]{:S(2)}) async-start(bf16[32,8,392]{2,1,0:T(8,128)(2,1)} %bitcast.46), calls=%async_computation | async-start | bytes 524288 | tf_op jit(solution)/shard_map/all_to_all | solution.py:458
  19.0 0.0 copy-start.10
  19.0 1.6 %copy.28 = bf16[392,64]{0,1:T(8,128)(2,1)} copy(bf16[392,64]{1,0:T(8,128)(2,1)} %bitcast.48) | data formatting | bytes 100352 | tf_op jit(solution)/shard_map/reshape | solution.py:456
  21.3 0.8 compare_select_fusion
  22.1 0.7 pad_clamp_fusion.1
  22.8 0.7 fusion.6
  23.5 0.0 copy-done.2
  23.5 0.0 copy-start.4
  23.5 0.6 gather_fusion
  24.1 0.1 reshape.25
  24.2 0.1 copy.31
  24.3 0.0 copy-done.9
  24.3 0.7 copy.33
  25.0 0.0 copy-done.8
  25.0 0.8 copy.32
  25.8 0.0 copy-done.7
  25.8 0.8 copy.34
  26.6 0.0 copy-done.10
  26.6 1.0 %copy.38.index_ref = s32[1024,1]{1,0:T(8,128)} copy(s32[1024,1]{0,1:T(1,128)S(1)} %bitcast.53) | data formatting | bytes 8192 | tf_op jit(solution)/shard_map/broadcast_in_dim | solution.py:405
  27.7 0.0 copy-done.4
  27.7 2.3 %copy.35 = bf16[896,896]{0,1:T(8,128)(2,1)} copy(bf16[896,896]{1,0:T(8,128)(2,1)S(1)} %copy-done.4) | data formatting | bytes 3211264 | tf_op args[12]
  30.0 0.0 copy-start.3
  30.0 3.7 %copy.37 = bf16[2,640,640]{1,2,0:T(8,128)(2,1)} copy(bf16[2,640,640]{2,1,0:T(8,128)(2,1)} %param.32) | data formatting | bytes 3276800 | tf_op args[14]
  33.7 0.0 copy-done.3
  33.7 0.0 copy-start.1
  33.7 2.5 %copy.36 = bf16[2,768,768]{1,2,0:T(8,128)(2,1)} copy(bf16[2,768,768]{2,1,0:T(8,128)(2,1)S(1)} %copy-done.3) | data formatting | bytes 4718592 | tf_op args[13]
  36.2 0.0 copy-done.1
  36.2 0.8 gather_fusion.1
  37.0 1.3 %dynamic-slice_bitcast_fusion.refs_1_.length_ref = f32[1,64]{1,0:T(1,128)} fusion(f32[1024]{0:T(1024)} %param.25, s32[]{:T(128)S(6)} %select_n.24), kind=kLoop, calls=%fused_computation.26 | loop fusion | bytes 516 | tf_op jit(solution)/shard_map/broadcast_in_dim | solution.py:327
  38.2 0.7 fusion.3.extra_ref
  38.9 0.0 copy-done
  38.9 0.7 constant_dynamic-slice_fusion.refs_0_.wig_ref
  39.7 0.7 select_convert_fusion.refs_9_.onehot_ref
  40.3 0.6 fusion.refs_2_.kind_ref
  41.0 0.0 all-to-all-done
  41.0 0.0 copy-start.5
  41.0 0.7 copy-done.5
  41.7 2.9 %shard_map.173 = bf16[16,64,512]{2,1,0:T(8,128)(2,1)} custom-call(s32[1024,1]{1,0:T(8,128)} %copy.38.index_ref, bf16[64,392]{1,0:T(8,128)(2,1)} %bitcast.51, bf16[256,392]{1,0:T(8,128)(2,1)} %bitcast.45, bf16[64,120]{1,0:T(8,128)(2,1)} %fusion.3.extra_ref, bf16[235,64]{1,0:T(8,128)(2,1)} %constant_dynamic-slice_fusion.refs_0_.wig_ref, ...), custom_call_target="tpu_custom_call" | custom-call | flops 256901120 | bytes 1318912 | tf_op jit(solution)/shard_map/pallas_call | solution.py:406
  44.6 24.6 %all_to_all.21.src_ref = bf16[16,64,512]{2,1,0:T(8,128)(2,1)} all-to-all(bf16[16,64,512]{2,1,0:T(8,128)(2,1)} %shard_map.173), channel_id=1, replica_groups=mesh['graph'=32,'irreps'=16] {'irreps'}, dimensions={0} | all-to-all | bytes 2097152 | tf_op jit(solution)/shard_map/all_to_all | solution.py:493
  69.2 10.9 %shard_map.174 = bf16[16,208,128]{2,1,0:T(8,128)(2,1)} custom-call(bf16[16,64,512]{2,1,0:T(8,128)(2,1)} %all_to_all.21.src_ref, bf16[235,64]{1,0:T(8,128)(2,1)} %constant_dynamic-slice_fusion.refs_0_.wig_ref, f32[1,64]{1,0:T(1,128)} %dynamic-slice_bitcast_fusion.refs_1_.length_ref, bf16[90,64]{1,0:T(8,128)(2,1)} %fusion.refs_2_.kind_ref, ...), custom_call_target="tpu_custom_call" | custom-call | flops 637534208 | bytes 7937408 | tf_op jit(solution)/shard_map/pallas_call | solution.py:349
  80.1 0.0 copy-start.6
  80.1 18.0 %all_to_all.22 = bf16[16,208,128]{2,1,0:T(8,128)(2,1)S(1)} all-to-all(bf16[16,208,128]{2,1,0:T(8,128)(2,1)} %shard_map.174), channel_id=1, replica_groups=mesh['graph'=32,'irreps'=16] {'irreps'}, dimensions={0} | all-to-all | bytes 1703936 | tf_op jit(solution)/shard_map/all_to_all | solution.py:495
  98.1 0.1 convert_reduce_fusion
  98.3 0.1 reshape_reshape.3
  98.4 0.0 copy-done.6
  98.4 0.7 add_convert_fusion
  (6 shorter events, 0.0 us)
Async XLA Ops:
  0.0 38.9 %copy-start = (bf16[235,1024]{1,0:T(8,128)(2,1)S(1)}, bf16[235,1024]{1,0:T(8,128)(2,1)}, u32[]{:S(2)}) copy-start(bf16[235,1024]{1,0:T(8,128)(2,1)} %param.26) | copy-start | bytes 1443844
  0.0 23.5 %copy-start.2 = (bf16[7,128,8]{1,2,0:T(8,128)(2,1)S(1)}, bf16[7,128,8]{1,2,0:T(8,128)(2,1)}, u32[]{:S(2)}) copy-start(bf16[7,128,8]{1,2,0:T(8,128)(2,1)} %param.33) | copy-start | bytes 43012
  1.5 22.7 %copy-start.9 = (bf16[90,128]{1,0:T(8,128)(2,1)S(1)}, bf16[90,128]{1,0:T(8,128)(2,1)}, u32[]{:S(2)}) copy-start(bf16[90,128]{1,0:T(8,128)(2,1)} %param.28) | copy-start | bytes 69124
  3.5 21.5 %copy-start.8 = (bf16[512,128]{1,0:T(8,128)(2,1)S(1)}, bf16[512,128]{1,0:T(8,128)(2,1)}, u32[]{:S(2)}) copy-start(bf16[512,128]{1,0:T(8,128)(2,1)} %param.27) | copy-start | bytes 393220
  3.5 22.3 %copy-start.7 = (bf16[128,896]{1,0:T(8,128)(2,1)S(1)}, bf16[128,896]{1,0:T(8,128)(2,1)}, u32[]{:S(2)}) copy-start(bf16[128,896]{1,0:T(8,128)(2,1)} %param.29) | copy-start | bytes 688132
  3.5 37.5 %all-to-all-start = ((bf16[32,8,392]{2,1,0:T(8,128)(2,1)}), bf16[32,8,392]{2,1,0:T(8,128)(2,1)S(1)}, u32[]{:S(2)}, u32[]{:S(2)}) async-start(bf16[32,8,392]{2,1,0:T(8,128)(2,1)} %bitcast.46), calls=%async_computation | async-start | bytes 524288 | tf_op jit(solution)/shard_map/all_to_all | solution.py:458
  19.0 7.6 %copy-start.10 = (s32[1024]{0:T(1024)S(1)}, s32[1024]{0:T(1024)}, u32[]{:S(2)}) copy-start(s32[1024]{0:T(1024)} %param.22) | copy-start | bytes 12292
  23.5 4.2 %copy-start.4 = (bf16[896,896]{1,0:T(8,128)(2,1)S(1)}, bf16[896,896]{1,0:T(8,128)(2,1)}, u32[]{:S(2)}) copy-start(bf16[896,896]{1,0:T(8,128)(2,1)} %param.30) | copy-start | bytes 4816900
  30.0 3.7 %copy-start.3 = (bf16[2,768,768]{2,1,0:T(8,128)(2,1)S(1)}, bf16[2,768,768]{2,1,0:T(8,128)(2,1)}, u32[]{:S(2)}) copy-start(bf16[2,768,768]{2,1,0:T(8,128)(2,1)} %param.31) | copy-start | bytes 7077892
  33.7 2.5 %copy-start.1 = (s32[64]{0:T(128)S(1)}, s32[64]{0:T(128)}, u32[]{:S(2)}) copy-start(s32[64]{0:T(128)} %param.20) | copy-start | bytes 772
  41.0 0.7 copy-start.5
  80.1 18.3 %copy-start.6 = (bf16[49,8,64]{2,1,0:T(8,128)(2,1)S(1)}, bf16[49,8,64]{2,1,0:T(8,128)(2,1)}, u32[]{:S(2)}) copy-start(bf16[49,8,64]{2,1,0:T(8,128)(2,1)} %param.18) | copy-start | bytes 150532

commit v15 on v13

--- a/solution.py
+++ b/solution.py
@@ -341,7 +341,7 @@
     onehot = side[-1]
     num_edges, atom_count = onehot.shape
     owners = source.shape[0]
-    out_rows = 16 * pl.cdiv(coeffs * (channel_count // owners) // 2, 16)
+    out_rows = 8 * pl.cdiv(coeffs * (channel_count // owners) // 2, 8)
     operands = (source,) + tuple(side)
     radial_in, radial_out = side[3], side[5]
     order_zero, order_one, order_two = side[6], side[7], side[8]

time: 97.3 us -> 96.8 us (level)
  no operation moved by 1% of the time
where the time goes in v15:
time: 96.8 us; the launch traced here: 96.2 us
  blocking collectives  42.1 us (43%)
  local copies, waits for them, and re-layouts  17.9 us (18%)
  starting transfers between devices  15.5 us (16%)
  Pallas kernels  13.7 us (14%)
  other arithmetic  4.9 us (5%)
  matrix products  1.29 us (1%)
    all_to_all x1, blocking collectives, body(): source = lax.all_to_all(outgoing, 'irreps', 0, 0, tiled=True)  24.6 us
    all_to_all x1, blocking collectives, body(): returned = lax.all_to_all(projected, 'irreps', 0, 0, tiled=True)  17.5 us
    all_to_all x1, starting transfers between devices, body(): arrived = lax.all_to_all(outgoing_rows, 'graph', 0, 0, tiled=True)  15.5 us
    unnamed x28, local copies, waits for them, and re-layouts  11.6 us
    pallas_call x1, Pallas kernels, convolve_edges(): pl.pallas_call(conv_kernel, out_shape=jax.ShapeDtypeStruct((owners, out_r...  10.9 us
    pallas_call x1, Pallas kernels, gather_rows(): pl.pallas_call(gather_kernel, out_shape=jax.ShapeDtypeStruct((owners, per...  2.87 us
  transfers between devices with their start and end apart: 1, of which 0 were waited for; matrix products, arithmetic and copies ran while one was open for 21% of the time, Pallas kernels for 0%

profile of v15, /device:TPU:32, one launch (start us, length us, event | category | flops | bytes accessed | tf_op | source)
XLA Modules:
  0.0 96.2 jit_solution(15288922908477836493)
XLA Ops:
  0.0 0.0 copy-start
  0.0 0.0 copy-start.2
  0.0 1.3 %convolution_convert_fusion = bf16[256,392]{0,1:T(8,128)(2,1)S(1)} fusion(s32[256]{0:T(256)} %param.21, bf16[49,8,64]{2,1,0:T(8,128)(2,1)} %param.18), kind=kOutput, calls=%fused_computation.3 | convolution fusion | flops 12961792 | bytes 251904 | tf_op jit(solution)/shard_map/dot_general | solution.py:440
  1.3 0.0 copy-start.9
  1.3 0.0 copy-start.6
  1.3 0.0 copy-start.8
  1.3 0.9 copy.29
  2.2 0.0 copy-start.7
  2.2 15.5 %all-to-all-start = ((bf16[32,8,392]{2,1,0:T(8,128)(2,1)}), bf16[32,8,392]{2,1,0:T(8,128)(2,1)S(1)}, u32[]{:S(2)}, u32[]{:S(2)}) async-start(bf16[32,8,392]{2,1,0:T(8,128)(2,1)} %bitcast.3), calls=%async_computation | async-start | bytes 524288 | tf_op jit(solution)/shard_map/all_to_all | solution.py:444
  17.7 0.0 copy-start.10
  18.4 0.8 compare_select_fusion
  19.2 0.7 pad_clamp_fusion.1
  19.8 0.7 fusion.7
  20.5 0.0 copy-done.2
  20.5 0.0 copy-start.4
  20.5 0.6 gather_fusion
  21.2 0.1 reshape.26
  21.2 0.1 copy.31
  21.3 0.0 copy-done.9
  21.4 0.7 copy.33
  22.1 0.0 copy-done.6
  22.1 0.8 copy.28
  22.8 0.0 copy-done.8
  22.8 0.8 copy.32
  23.6 0.0 copy-done.7
  23.6 0.8 copy.34
  24.5 0.0 copy-done.10
  24.5 1.0 %copy.38.index_ref = s32[1024,1]{1,0:T(8,128)} copy(s32[1024,1]{0,1:T(1,128)S(1)} %bitcast.54) | data formatting | bytes 8192 | tf_op jit(solution)/shard_map/broadcast_in_dim | solution.py:387
  25.5 0.0 copy-done.4
  25.5 2.3 %copy.35 = bf16[896,896]{0,1:T(8,128)(2,1)} copy(bf16[896,896]{1,0:T(8,128)(2,1)S(1)} %copy-done.4) | data formatting | bytes 3211264 | tf_op args[12]
  27.8 0.0 copy-start.3
  27.8 3.7 %copy.37 = bf16[2,640,640]{1,2,0:T(8,128)(2,1)} copy(bf16[2,640,640]{2,1,0:T(8,128)(2,1)} %param.32) | data formatting | bytes 3276800 | tf_op args[14]
  31.5 0.0 copy-done.3
  31.5 0.0 copy-start.1
  31.5 2.5 %copy.36 = bf16[2,768,768]{1,2,0:T(8,128)(2,1)} copy(bf16[2,768,768]{2,1,0:T(8,128)(2,1)S(1)} %copy-done.3) | data formatting | bytes 4718592 | tf_op args[13]
  34.0 0.0 copy-done.1
  34.0 0.8 gather_fusion.1
  34.8 1.3 %dynamic-slice_bitcast_fusion.refs_1_.length_ref = f32[1,64]{1,0:T(1,128)} fusion(f32[1024]{0:T(1024)} %param.25, s32[]{:T(128)S(6)} %select_n.24), kind=kLoop, calls=%fused_computation.29 | loop fusion | bytes 516 | tf_op jit(solution)/shard_map/broadcast_in_dim | solution.py:327
  36.1 0.7 fusion.4.extra_ref
  36.7 0.0 copy-done
  36.7 0.7 constant_dynamic-slice_fusion.refs_0_.wig_ref
  37.5 0.7 select_convert_fusion.refs_9_.onehot_ref
  38.2 0.6 fusion.1.refs_2_.kind_ref
  38.8 0.0 all-to-all-done
  38.8 0.0 copy-start.5
  38.8 0.7 copy-done.5
  39.5 2.9 %shard_map.172 = bf16[16,64,512]{2,1,0:T(8,128)(2,1)} custom-call(s32[1024,1]{1,0:T(8,128)} %copy.38.index_ref, bf16[64,392]{1,0:T(8,128)(2,1)} %bitcast.52, bf16[256,392]{1,0:T(8,128)(2,1)} %bitcast.47, bf16[64,120]{1,0:T(8,128)(2,1)} %fusion.4.extra_ref, bf16[235,64]{1,0:T(8,128)(2,1)} %constant_dynamic-slice_fusion.refs_0_.wig_ref, ...), custom_call_target="tpu_custom_call" | custom-call | flops 256901120 | bytes 1318912 | tf_op jit(solution)/shard_map/pallas_call | solution.py:388
  42.4 24.6 %all_to_all.21.src_ref = bf16[16,64,512]{2,1,0:T(8,128)(2,1)} all-to-all(bf16[16,64,512]{2,1,0:T(8,128)(2,1)} %shard_map.172), channel_id=1, replica_groups=mesh['graph'=32,'irreps'=16] {'irreps'}, dimensions={0} | all-to-all | bytes 2097152 | tf_op jit(solution)/shard_map/all_to_all | solution.py:479
  67.0 10.9 %shard_map.173 = bf16[16,200,128]{2,1,0:T(8,128)(2,1)} custom-call(bf16[16,64,512]{2,1,0:T(8,128)(2,1)} %all_to_all.21.src_ref, bf16[235,64]{1,0:T(8,128)(2,1)} %constant_dynamic-slice_fusion.refs_0_.wig_ref, f32[1,64]{1,0:T(1,128)} %dynamic-slice_bitcast_fusion.refs_1_.length_ref, bf16[90,64]{1,0:T(8,128)(2,1)} %fusion.1.refs_2_.kind_ref, ...), custom_call_target="tpu_custom_call" | custom-call | flops 637534208 | bytes 7904640 | tf_op jit(solution)/shard_map/pallas_call | solution.py:349
  77.8 17.5 %all_to_all.22 = bf16[16,200,128]{2,1,0:T(8,128)(2,1)S(1)} all-to-all(bf16[16,200,128]{2,1,0:T(8,128)(2,1)} %shard_map.173), channel_id=1, replica_groups=mesh['graph'=32,'irreps'=16] {'irreps'}, dimensions={0} | all-to-all | bytes 1638400 | tf_op jit(solution)/shard_map/all_to_all | solution.py:481
  95.4 0.1 convert_reduce_fusion
  95.5 0.1 reshape_reshape.3
  95.6 0.7 add_convert_fusion
  (5 shorter events, 0.0 us)
Async XLA Ops:
  0.0 36.7 %copy-start = (bf16[235,1024]{1,0:T(8,128)(2,1)S(1)}, bf16[235,1024]{1,0:T(8,128)(2,1)}, u32[]{:S(2)}) copy-start(bf16[235,1024]{1,0:T(8,128)(2,1)} %param.26) | copy-start | bytes 1443844
  0.0 20.5 %copy-start.2 = (bf16[7,128,8]{1,2,0:T(8,128)(2,1)S(1)}, bf16[7,128,8]{1,2,0:T(8,128)(2,1)}, u32[]{:S(2)}) copy-start(bf16[7,128,8]{1,2,0:T(8,128)(2,1)} %param.33) | copy-start | bytes 43012
  1.3 20.0 %copy-start.9 = (bf16[90,128]{1,0:T(8,128)(2,1)S(1)}, bf16[90,128]{1,0:T(8,128)(2,1)}, u32[]{:S(2)}) copy-start(bf16[90,128]{1,0:T(8,128)(2,1)} %param.28) | copy-start | bytes 69124
  1.3 20.8 %copy-start.6 = (bf16[49,8,64]{2,1,0:T(8,128)(2,1)S(1)}, bf16[49,8,64]{2,1,0:T(8,128)(2,1)}, u32[]{:S(2)}) copy-start(bf16[49,8,64]{2,1,0:T(8,128)(2,1)} %param.18) | copy-start | bytes 150532
  1.3 21.5 %copy-start.8 = (bf16[512,128]{1,0:T(8,128)(2,1)S(1)}, bf16[512,128]{1,0:T(8,128)(2,1)}, u32[]{:S(2)}) copy-start(bf16[512,128]{1,0:T(8,128)(2,1)} %param.27) | copy-start | bytes 393220
  2.2 21.4 %copy-start.7 = (bf16[128,896]{1,0:T(8,128)(2,1)S(1)}, bf16[128,896]{1,0:T(8,128)(2,1)}, u32[]{:S(2)}) copy-start(bf16[128,896]{1,0:T(8,128)(2,1)} %param.29) | copy-start | bytes 688132
  2.2 36.6 %all-to-all-start = ((bf16[32,8,392]{2,1,0:T(8,128)(2,1)}), bf16[32,8,392]{2,1,0:T(8,128)(2,1)S(1)}, u32[]{:S(2)}, u32[]{:S(2)}) async-start(bf16[32,8,392]{2,1,0:T(8,128)(2,1)} %bitcast.3), calls=%async_computation | async-start | bytes 524288 | tf_op jit(solution)/shard_map/all_to_all | solution.py:444
  17.7 6.8 %copy-start.10 = (s32[1024]{0:T(1024)S(1)}, s32[1024]{0:T(1024)}, u32[]{:S(2)}) copy-start(s32[1024]{0:T(1024)} %param.22) | copy-start | bytes 12292
  20.5 5.0 %copy-start.4 = (bf16[896,896]{1,0:T(8,128)(2,1)S(1)}, bf16[896,896]{1,0:T(8,128)(2,1)}, u32[]{:S(2)}) copy-start(bf16[896,896]{1,0:T(8,128)(2,1)} %param.30) | copy-start | bytes 4816900
  27.8 3.7 %copy-start.3 = (bf16[2,768,768]{2,1,0:T(8,128)(2,1)S(1)}, bf16[2,768,768]{2,1,0:T(8,128)(2,1)}, u32[]{:S(2)}) copy-start(bf16[2,768,768]{2,1,0:T(8,128)(2,1)} %param.31) | copy-start | bytes 7077892
  31.5 2.5 %copy-start.1 = (s32[64]{0:T(128)S(1)}, s32[64]{0:T(128)}, u32[]{:S(2)}) copy-start(s32[64]{0:T(128)} %param.20) | copy-start | bytes 772
  38.8 0.7 copy-start.5

commit v16 on v15

--- a/solution.py
+++ b/solution.py
@@ -315,9 +315,8 @@
                 pieces[r].append(jnp.concatenate([block[:half], block[half:]], axis=1))
     fill = out_ref.shape[1] - COEFFS * half
     for r in range(owners):
-        out_ref[r] = jnp.concatenate(
-            pieces[r] + [jnp.zeros((fill, out_ref.shape[2]), jnp.float32)], axis=0
-        ).astype(out_ref.dtype)
+        tail = [jnp.zeros((fill, out_ref.shape[2]), jnp.float32)] if fill else []
+        out_ref[r] = jnp.concatenate(pieces[r] + tail, axis=0).astype(out_ref.dtype)
 
 
 def edge_operands(wig_mine, lengths, kind_onehot, radial_in, species_table, radial_out,
@@ -341,7 +340,7 @@
     onehot = side[-1]
     num_edges, atom_count = onehot.shape
     owners = source.shape[0]
-    out_rows = 8 * pl.cdiv(coeffs * (channel_count // owners) // 2, 8)
+    out_rows = coeffs * (channel_count // owners) // 2
     operands = (source,) + tuple(side)
     radial_in, radial_out = side[3], side[5]
     order_zero, order_one, order_two = side[6], side[7], side[8]

time: 96.8 us -> 96.8 us (level)
  no operation moved by 1% of the time
where the time goes in v16:
time: 96.8 us; the launch traced here: 96.2 us
  blocking collectives  42.1 us (43%)
  local copies, waits for them, and re-layouts  17.9 us (18%)
  starting transfers between devices  15.5 us (16%)
  Pallas kernels  13.7 us (14%)
  other arithmetic  4.9 us (5%)
  matrix products  1.29 us (1%)
    all_to_all x1, blocking collectives, body(): source = lax.all_to_all(outgoing, 'irreps', 0, 0, tiled=True)  24.6 us
    all_to_all x1, blocking collectives, body(): returned = lax.all_to_all(projected, 'irreps', 0, 0, tiled=True)  17.5 us
    all_to_all x1, starting transfers between devices, body(): arrived = lax.all_to_all(outgoing_rows, 'graph', 0, 0, tiled=True)  15.5 us
    unnamed x28, local copies, waits for them, and re-layouts  11.6 us
    pallas_call x1, Pallas kernels, convolve_edges(): pl.pallas_call(conv_kernel, out_shape=jax.ShapeDtypeStruct((owners, out_r...  10.9 us
    pallas_call x1, Pallas kernels, gather_rows(): pl.pallas_call(gather_kernel, out_shape=jax.ShapeDtypeStruct((owners, per...  2.87 us
  transfers between devices with their start and end apart: 1, of which 0 were waited for; matrix products, arithmetic and copies ran while one was open for 21% of the time, Pallas kernels for 0%

profile of v16, /device:TPU:32, one launch (start us, length us, event | category | flops | bytes accessed | tf_op | source)
XLA Modules:
  0.0 96.2 jit_solution(6740227714170803819)
XLA Ops:
  0.0 0.0 copy-start
  0.0 0.0 copy-start.2
  0.0 1.3 %convolution_convert_fusion = bf16[256,392]{0,1:T(8,128)(2,1)S(1)} fusion(s32[256]{0:T(256)} %param.21, bf16[49,8,64]{2,1,0:T(8,128)(2,1)} %param.18), kind=kOutput, calls=%fused_computation.3 | convolution fusion | flops 12961792 | bytes 251904 | tf_op jit(solution)/shard_map/dot_general | solution.py:439
  1.3 0.0 copy-start.9
  1.3 0.0 copy-start.6
  1.3 0.0 copy-start.8
  1.3 0.9 copy.29
  2.2 0.0 copy-start.7
  2.2 15.5 %all-to-all-start = ((bf16[32,8,392]{2,1,0:T(8,128)(2,1)}), bf16[32,8,392]{2,1,0:T(8,128)(2,1)S(1)}, u32[]{:S(2)}, u32[]{:S(2)}) async-start(bf16[32,8,392]{2,1,0:T(8,128)(2,1)} %bitcast.3), calls=%async_computation | async-start | bytes 524288 | tf_op jit(solution)/shard_map/all_to_all | solution.py:443
  17.7 0.0 copy-start.10
  18.4 0.8 compare_select_fusion
  19.2 0.7 pad_clamp_fusion.1
  19.8 0.7 fusion.7
  20.5 0.0 copy-done.2
  20.5 0.0 copy-start.4
  20.5 0.6 gather_fusion
  21.2 0.1 reshape.26
  21.2 0.1 copy.31
  21.3 0.0 copy-done.9
  21.4 0.7 copy.33
  22.1 0.0 copy-done.6
  22.1 0.8 copy.28
  22.8 0.0 copy-done.8
  22.8 0.8 copy.32
  23.6 0.0 copy-done.7
  23.6 0.8 copy.34
  24.5 0.0 copy-done.10
  24.5 1.0 %copy.38.index_ref = s32[1024,1]{1,0:T(8,128)} copy(s32[1024,1]{0,1:T(1,128)S(1)} %bitcast.52) | data formatting | bytes 8192 | tf_op jit(solution)/shard_map/broadcast_in_dim | solution.py:386
  25.5 0.0 copy-done.4
  25.5 2.3 %copy.35 = bf16[896,896]{0,1:T(8,128)(2,1)} copy(bf16[896,896]{1,0:T(8,128)(2,1)S(1)} %copy-done.4) | data formatting | bytes 3211264 | tf_op args[12]
  27.8 0.0 copy-start.3
  27.8 3.7 %copy.37 = bf16[2,640,640]{1,2,0:T(8,128)(2,1)} copy(bf16[2,640,640]{2,1,0:T(8,128)(2,1)} %param.32) | data formatting | bytes 3276800 | tf_op args[14]
  31.5 0.0 copy-done.3
  31.5 0.0 copy-start.1
  31.5 2.5 %copy.36 = bf16[2,768,768]{1,2,0:T(8,128)(2,1)} copy(bf16[2,768,768]{2,1,0:T(8,128)(2,1)S(1)} %copy-done.3) | data formatting | bytes 4718592 | tf_op args[13]
  34.0 0.0 copy-done.1
  34.0 0.8 gather_fusion.1
  34.8 1.3 %dynamic-slice_bitcast_fusion.refs_1_.length_ref = f32[1,64]{1,0:T(1,128)} fusion(f32[1024]{0:T(1024)} %param.25, s32[]{:T(128)S(6)} %select_n.24), kind=kLoop, calls=%fused_computation.29 | loop fusion | bytes 516 | tf_op jit(solution)/shard_map/broadcast_in_dim | solution.py:326
  36.1 0.7 fusion.4.extra_ref
  36.7 0.0 copy-done
  36.7 0.7 constant_dynamic-slice_fusion.refs_0_.wig_ref
  37.5 0.7 select_convert_fusion.refs_9_.onehot_ref
  38.2 0.6 fusion.1.refs_2_.kind_ref
  38.8 0.0 all-to-all-done
  38.8 0.0 copy-start.5
  38.8 0.7 copy-done.5
  39.5 2.9 %shard_map.172 = bf16[16,64,512]{2,1,0:T(8,128)(2,1)} custom-call(s32[1024,1]{1,0:T(8,128)} %copy.38.index_ref, bf16[64,392]{1,0:T(8,128)(2,1)} %bitcast.50, bf16[256,392]{1,0:T(8,128)(2,1)} %bitcast.46, bf16[64,120]{1,0:T(8,128)(2,1)} %fusion.4.extra_ref, bf16[235,64]{1,0:T(8,128)(2,1)} %constant_dynamic-slice_fusion.refs_0_.wig_ref, ...), custom_call_target="tpu_custom_call" | custom-call | flops 256901120 | bytes 1318912 | tf_op jit(solution)/shard_map/pallas_call | solution.py:387
  42.4 24.6 %all_to_all.21.src_ref = bf16[16,64,512]{2,1,0:T(8,128)(2,1)} all-to-all(bf16[16,64,512]{2,1,0:T(8,128)(2,1)} %shard_map.172), channel_id=1, replica_groups=mesh['graph'=32,'irreps'=16] {'irreps'}, dimensions={0} | all-to-all | bytes 2097152 | tf_op jit(solution)/shard_map/all_to_all | solution.py:478
  67.0 10.9 %shard_map.173 = bf16[16,196,128]{2,1,0:T(8,128)(2,1)} custom-call(bf16[16,64,512]{2,1,0:T(8,128)(2,1)} %all_to_all.21.src_ref, bf16[235,64]{1,0:T(8,128)(2,1)} %constant_dynamic-slice_fusion.refs_0_.wig_ref, f32[1,64]{1,0:T(1,128)} %dynamic-slice_bitcast_fusion.refs_1_.length_ref, bf16[90,64]{1,0:T(8,128)(2,1)} %fusion.1.refs_2_.kind_ref, ...), custom_call_target="tpu_custom_call" | custom-call | flops 637534208 | bytes 7888256 | tf_op jit(solution)/shard_map/pallas_call | solution.py:348
  77.8 17.5 %all_to_all.22 = bf16[16,196,128]{2,1,0:T(8,128)(2,1)S(1)} all-to-all(bf16[16,196,128]{2,1,0:T(8,128)(2,1)} %shard_map.173), channel_id=1, replica_groups=mesh['graph'=32,'irreps'=16] {'irreps'}, dimensions={0} | all-to-all | bytes 1605632 | tf_op jit(solution)/shard_map/all_to_all | solution.py:480
  95.4 0.1 convert_reduce_fusion
  95.5 0.1 reshape_reshape.3
  95.6 0.7 add_convert_fusion
  (5 shorter events, 0.0 us)
Async XLA Ops:
  0.0 36.7 %copy-start = (bf16[235,1024]{1,0:T(8,128)(2,1)S(1)}, bf16[235,1024]{1,0:T(8,128)(2,1)}, u32[]{:S(2)}) copy-start(bf16[235,1024]{1,0:T(8,128)(2,1)} %param.26) | copy-start | bytes 1443844
  0.0 20.5 %copy-start.2 = (bf16[7,128,8]{1,2,0:T(8,128)(2,1)S(1)}, bf16[7,128,8]{1,2,0:T(8,128)(2,1)}, u32[]{:S(2)}) copy-start(bf16[7,128,8]{1,2,0:T(8,128)(2,1)} %param.33) | copy-start | bytes 43012
  1.3 20.0 %copy-start.9 = (bf16[90,128]{1,0:T(8,128)(2,1)S(1)}, bf16[90,128]{1,0:T(8,128)(2,1)}, u32[]{:S(2)}) copy-start(bf16[90,128]{1,0:T(8,128)(2,1)} %param.28) | copy-start | bytes 69124
  1.3 20.8 %copy-start.6 = (bf16[49,8,64]{2,1,0:T(8,128)(2,1)S(1)}, bf16[49,8,64]{2,1,0:T(8,128)(2,1)}, u32[]{:S(2)}) copy-start(bf16[49,8,64]{2,1,0:T(8,128)(2,1)} %param.18) | copy-start | bytes 150532
  1.3 21.5 %copy-start.8 = (bf16[512,128]{1,0:T(8,128)(2,1)S(1)}, bf16[512,128]{1,0:T(8,128)(2,1)}, u32[]{:S(2)}) copy-start(bf16[512,128]{1,0:T(8,128)(2,1)} %param.27) | copy-start | bytes 393220
  2.2 21.4 %copy-start.7 = (bf16[128,896]{1,0:T(8,128)(2,1)S(1)}, bf16[128,896]{1,0:T(8,128)(2,1)}, u32[]{:S(2)}) copy-start(bf16[128,896]{1,0:T(8,128)(2,1)} %param.29) | copy-start | bytes 688132
  2.2 36.6 %all-to-all-start = ((bf16[32,8,392]{2,1,0:T(8,128)(2,1)}), bf16[32,8,392]{2,1,0:T(8,128)(2,1)S(1)}, u32[]{:S(2)}, u32[]{:S(2)}) async-start(bf16[32,8,392]{2,1,0:T(8,128)(2,1)} %bitcast.3), calls=%async_computation | async-start | bytes 524288 | tf_op jit(solution)/shard_map/all_to_all | solution.py:443
  17.7 6.8 %copy-start.10 = (s32[1024]{0:T(1024)S(1)}, s32[1024]{0:T(1024)}, u32[]{:S(2)}) copy-start(s32[1024]{0:T(1024)} %param.22) | copy-start | bytes 12292
  20.5 5.0 %copy-start.4 = (bf16[896,896]{1,0:T(8,128)(2,1)S(1)}, bf16[896,896]{1,0:T(8,128)(2,1)}, u32[]{:S(2)}) copy-start(bf16[896,896]{1,0:T(8,128)(2,1)} %param.30) | copy-start | bytes 4816900
  27.8 3.7 %copy-start.3 = (bf16[2,768,768]{2,1,0:T(8,128)(2,1)S(1)}, bf16[2,768,768]{2,1,0:T(8,128)(2,1)}, u32[]{:S(2)}) copy-start(bf16[2,768,768]{2,1,0:T(8,128)(2,1)} %param.31) | copy-start | bytes 7077892
  31.5 2.5 %copy-start.1 = (s32[64]{0:T(128)S(1)}, s32[64]{0:T(128)}, u32[]{:S(2)}) copy-start(s32[64]{0:T(128)} %param.20) | copy-start | bytes 772
  38.8 0.7 copy-start.5
